TPU v7x, 768 devices: a whole 4x8x12 slice. The times are simulated.
768 devices in a mesh: tiles: 96 (over x, z, core), cams: 8 (over y).
Axes of the slice: x: 4, y: 8, z: 12, core: 2. Of those that a mesh axis runs over, the one named last changes fastest.
Arguments:
- offsets: float32 [2, 196608], P(None, ('tiles', 'cams')), may hold values from -6 to 6
- factor_diag: float32 [2, 196608], P(None, ('tiles', 'cams')), may hold values from 0.8 to 4
- factor_off: float32 [196608], P(('tiles', 'cams')), may hold values from -4 to 4
- logit: float32 [196608], P(('tiles', 'cams')), may hold values from -6 to 6
- appearance: float32 [19, 196608], P(None, ('tiles', 'cams')), may hold values from -6 to 6
- cam_linear: float32 [8, 4], P('cams'), may hold values from -0.3 to 0.3
- cam_shift: float32 [8, 2], P('cams'), may hold values from -2 to 2
- block_lists: int32 [8, 1536, 2, 3], P('cams', 'tiles'), may hold values from 0 to 24575, as said below
- pix_grad: bfloat16 [19, 8, 393216], P(None, 'cams', 'tiles'), may hold values from -6 to 6
Outputs:
- rendered: float32 [19, 8, 393216], P(None, 'cams', 'tiles')
- grad_geometry: float32 [6, 196608], P(None, ('tiles', 'cams'))
- grad_appearance: float32 [19, 196608], P(None, ('tiles', 'cams'))
Inputs may be any that keep to these rules, and one draw needn't show every extreme that they name: `block_lists`: call blocks k * 256 to (k+1) * 256 - 1 column k. For each camera and each aligned run of 16 tiles (the tiles of one device), at most 2 list entries of both slabs together name blocks of one column, and exactly 2 name blocks of some column.
All inputs are finite; a program needn't handle non-finite values.
Results may differ from a plain program's by a relative error of at most 0.012.
The roundings to bfloat16 on the way count: a program that leaves them out, or rounds other values in their place, can miss the bound.
Values may be sent and summed in bfloat16 or wider, within the bound.
No kernel may reach another device: no remote copies, remote signals or barrier semaphores. Data moves between devices by JAX's collectives and lax.ppermute only.
A program may use at most 32 MiB of HBM per device.

v0:
```python
import jax
import jax.numpy as jnp
from jax import lax
from jax.sharding import PartitionSpec as P

SIDE = 16
TPD = 16
LIST = 3
BLK = 8


def project(geometry, linear, camera_shift):
    lin_xx = 1.0 + linear[0]
    lin_xy = linear[1]
    lin_yx = linear[2]
    lin_yy = 1.0 + linear[3]
    diag_x = geometry[2]
    diag_y = geometry[3]
    lower = geometry[4]
    cov_xx = diag_x * diag_x
    cov_xy = diag_x * lower
    cov_yy = lower * lower + diag_y * diag_y
    half_xx = lin_xx * cov_xx + lin_xy * cov_xy
    half_xy = lin_xx * cov_xy + lin_xy * cov_yy
    half_yx = lin_yx * cov_xx + lin_yy * cov_xy
    half_yy = lin_yx * cov_xy + lin_yy * cov_yy
    img_xx = half_xx * lin_xx + half_xy * lin_xy + 0.3
    img_xy = half_xx * lin_yx + half_xy * lin_yy
    img_yy = half_yx * lin_yx + half_yy * lin_yy + 0.3
    determ = img_xx * img_yy - img_xy * img_xy
    centre_x = lin_xx * geometry[0] + lin_xy * geometry[1] + camera_shift[0]
    centre_y = lin_yx * geometry[0] + lin_yy * geometry[1] + camera_shift[1]
    opacity = 0.95 * jax.nn.sigmoid(geometry[5])
    return jnp.stack(
        [centre_x, centre_y, img_yy / determ, -img_xy / determ, img_xx / determ, opacity]
    )


def render_tile(projected, colours):
    pixels = jnp.arange(SIDE * SIDE)
    across = (pixels % SIDE).astype(jnp.float32) + 0.5 - SIDE / 2
    downward = (pixels // SIDE).astype(jnp.float32) + 0.5 - SIDE / 2
    delta_x = across[None, :] - projected[0][:, None]
    delta_y = downward[None, :] - projected[1][:, None]
    quadric = (
        projected[2][:, None] * delta_x * delta_x
        + 2.0 * projected[3][:, None] * delta_x * delta_y
        + projected[4][:, None] * delta_y * delta_y
    )
    coverage = projected[5][:, None] * jnp.exp(-0.5 * quadric)
    log_keep = jnp.log1p(-coverage)
    weight = jnp.exp(jnp.cumsum(log_keep, axis=0) - log_keep) * coverage
    return jnp.dot(
        colours, weight, precision=lax.Precision.HIGHEST, preferred_element_type=jnp.float32
    )


def tile_grads(projected, colours, cotangent):
    per_tile = projected.shape[1] // TPD
    channels = colours.shape[0]
    proj_tiles = projected.reshape(6, TPD, per_tile)
    colour_tiles = colours.reshape(channels, TPD, per_tile)

    def forward(proj_arg, colour_arg):
        return jax.vmap(render_tile, in_axes=(1, 1), out_axes=1)(proj_arg, colour_arg)

    picture, pullback = jax.vjp(forward, proj_tiles, colour_tiles)
    grad_proj, grad_colour = pullback(cotangent)
    return (picture, grad_proj.reshape(6, -1), grad_colour.reshape(channels, -1))


def slot_ranks(entries, blocks_per_column, columns):
    column = entries // blocks_per_column
    in_column = entries % blocks_per_column
    matches = (column[..., None] == jnp.arange(columns, dtype=jnp.int32)).astype(jnp.int32)
    before = jnp.cumsum(matches, axis=-2) - matches
    ranking = jnp.sum(before * matches, axis=-1)
    return (column, ranking, in_column)


def local(
    offsets,
    factor_diag,
    factor_off,
    logit,
    appearance,
    cam_linear,
    cam_shift,
    block_lists,
    pix_grad,
):
    columns = lax.axis_size("tiles")
    capacity = 4 * TPD * LIST // columns
    slot_count = columns * capacity
    channels = appearance.shape[0]
    geometry = jnp.concatenate([offsets, factor_diag, factor_off[None, :], logit[None, :]], axis=0)
    geometry_col, appearance_col = (
        lax.all_gather(geometry, "cams", axis=1, tiled=True),
        lax.all_gather(appearance, "cams", axis=1, tiled=True),
    )
    per_column = geometry_col.shape[1] // BLK
    linear = cam_linear[0]
    camera_shift = cam_shift[0]
    entries = block_lists.reshape(-1)
    entry_count = entries.shape[0]
    column, ranking, in_column = slot_ranks(entries, per_column, columns)
    entry_slot = column * capacity + ranking
    request = jnp.zeros((slot_count,), jnp.int32).at[entry_slot].set(in_column)
    wanted = lax.all_to_all(request, "tiles", split_axis=0, concat_axis=0, tiled=True)
    raw_params = geometry_col.reshape(6, per_column, BLK)[:, wanted].reshape(6, slot_count * BLK)
    raw_colours = appearance_col.reshape(channels, per_column, BLK)[:, wanted].reshape(
        channels, slot_count * BLK
    )
    send_proj = project(raw_params, linear, camera_shift).astype(jnp.bfloat16)
    got_proj, got_colour = (
        lax.all_to_all(send_proj, "tiles", split_axis=1, concat_axis=1, tiled=True),
        lax.all_to_all(
            raw_colours.astype(jnp.bfloat16), "tiles", split_axis=1, concat_axis=1, tiled=True
        ),
    )
    projected = (
        got_proj.reshape(6, slot_count, BLK)[:, entry_slot]
        .reshape(6, entry_count * BLK)
        .astype(jnp.float32)
    )
    colours = (
        got_colour.reshape(channels, slot_count, BLK)[:, entry_slot]
        .reshape(channels, entry_count * BLK)
        .astype(jnp.float32)
    )
    cotangent = pix_grad.reshape(channels, TPD, -1).astype(jnp.float32)
    picture, grad_proj, grad_colour = tile_grads(projected, colours, cotangent)
    back_proj = (
        jnp.zeros((6, slot_count, BLK), jnp.bfloat16)
        .at[:, entry_slot]
        .set(grad_proj.reshape(6, entry_count, BLK).astype(jnp.bfloat16))
    )
    back_colour = (
        jnp.zeros((channels, slot_count, BLK), jnp.bfloat16)
        .at[:, entry_slot]
        .set(grad_colour.reshape(channels, entry_count, BLK).astype(jnp.bfloat16))
    )
    ret_proj, ret_colour = (
        lax.all_to_all(back_proj.reshape(6, -1), "tiles", split_axis=1, concat_axis=1, tiled=True),
        lax.all_to_all(
            back_colour.reshape(channels, -1), "tiles", split_axis=1, concat_axis=1, tiled=True
        ),
    )
    unused, pull_params = jax.vjp(lambda params: project(params, linear, camera_shift), raw_params)
    grad_raw = pull_params(ret_proj.astype(jnp.float32))[0]
    owner_hot = (wanted[:, None] == jnp.arange(per_column, dtype=jnp.int32)[None, :]).astype(
        jnp.float32
    )

    def collect(values, row_count):
        summed = jnp.einsum(
            "rsb,sk->rkb",
            values.reshape(row_count, slot_count, BLK),
            owner_hot,
            precision=lax.Precision.HIGHEST,
        )
        return summed.reshape(row_count, per_column * BLK)

    column_geometry = collect(grad_raw, 6)
    column_colour = collect(ret_colour.astype(jnp.float32), channels)
    grad_geometry, grad_appearance = (
        lax.psum_scatter(column_geometry, "cams", scatter_dimension=1, tiled=True),
        lax.psum_scatter(column_colour, "cams", scatter_dimension=1, tiled=True),
    )
    return (picture.reshape(channels, 1, -1), grad_geometry, grad_appearance)


def solution(mesh):
    return jax.shard_map(
        local,
        mesh=mesh,
        in_specs=(
            P(None, ("tiles", "cams")),
            P(None, ("tiles", "cams")),
            P(("tiles", "cams")),
            P(("tiles", "cams")),
            P(None, ("tiles", "cams")),
            P("cams", None),
            P("cams", None),
            P("cams", "tiles", None, None),
            P(None, "cams", "tiles"),
        ),
        out_specs=(
            P(None, "cams", "tiles"),
            P(None, ("tiles", "cams")),
            P(None, ("tiles", "cams")),
        ),
        check_vma=False,
    )
```

profile of v0, /device:TPU:6, one launch (start us, length us, event | category | flops | bytes accessed | tf_op | source)
XLA Modules:
  0.0 278.3 jit_solution(3127060774234298678)
XLA Ops:
  10.3 19.4 %all-to-all-start = ((s32[96,2,1]{1,2,0:T(1,128)}), s32[96,2,1]{1,2,0:T(1,128)S(1)}, u32[]{:S(2)}, u32[]{:S(2)}) async-start(s32[96,2,1]{1,2,0:T(1,128)} %bitcast.3), calls=%async_computation | async-start | bytes 98304 | tf_op jit(solution)/shard_map/all_to_all | solution.py:109
  29.7 1.5 fusion.60
  31.1 1.3 fusion.61
  33.2 26.2 %all_gather.6 = bf16[19,2048]{1,0:T(8,128)(2,1)S(1)} all-gather(bf16[19,256]{1,0:T(8,128)(2,1)S(1)} %convert.43), channel_id=1, replica_groups=mesh['tiles'=96,'cams'=8] {'cams'}, dimensions={1}, use_global_device_ids=true | all-gather | bytes 87552 | tf_op jit(solution)/shard_map/all_gather | solution.py:99
  60.1 24.6 %all_gather.7 = f32[6,2048]{1,0:T(8,128)S(1)} all-gather(f32[6,256]{1,0:T(8,128)S(1)} %pad_maximum_fusion), channel_id=1, replica_groups=mesh['tiles'=96,'cams'=8] {'cams'}, dimensions={1}, use_global_device_ids=true | all-gather | bytes 55296 | tf_op jit(solution)/shard_map/all_gather | solution.py:98
  91.3 2.4 add_convert_fusion.1
  96.1 13.2 %all-to-all-start.2 = ((bf16[6,96,16]{2,0,1:T(8,128)(2,1)}), bf16[6,96,16]{2,0,1:T(8,128)(2,1)S(1)}, u32[]{:S(2)}, u32[]{:S(2)}) async-start(bf16[6,96,16]{2,0,1:T(8,128)(2,1)} %copy.112), calls=%async_computation.2 | async-start | bytes 393216 | tf_op jit(solution)/shard_map/all_to_all | solution.py:116
  113.1 11.4 %all-to-all-done.2 = bf16[6,96,16]{2,0,1:T(8,128)(2,1)S(1)} async-done(((bf16[6,96,16]{2,0,1:T(8,128)(2,1)}), bf16[6,96,16]{2,0,1:T(8,128)(2,1)S(1)}, u32[]{:S(2)}, u32[]{:S(2)}) %all-to-all-start.2) | async-done | bytes 18464 | tf_op jit(solution)/shard_map/all_to_all | solution.py:116
  124.5 7.9 %all-to-all-start.1 = ((bf16[96,2,152]{2,1,0:T(2,128)(2,1)}), bf16[96,2,152]{2,1,0:T(2,128)(2,1)S(1)}, u32[]{:S(2)}, u32[]{:S(2)}) async-start(bf16[96,2,152]{2,1,0:T(2,128)(2,1)} %reshape.1074), calls=%async_computation.1 | async-start | bytes 196608 | tf_op jit(solution)/shard_map/all_to_all | solution.py:117
  136.1 1.8 fusion
  138.2 3.4 %scatter_fusion.1 = bf16[19,192,8]{0,2,1:T(8,128)(2,1)S(1)} fusion(bf16[19,192,8]{0,2,1:T(8,128)(2,1)S(1)} %broadcast_in_dim.20, s32[96]{0:T(128)S(1)} %fusion.51, bf16[96,19,8]{1,2,0:T(8,128)(2,1)S(1)} %bitcast.88), kind=kCustom, calls=%fused_computation.6 | custom fusion | bytes 87936 | tf_op jit(solution)/shard_map/scatter | solution.py:141
  142.6 1.7 all-to-all-done.1
  144.3 11.5 %all-to-all-start.4 = ((bf16[96,2,152]{2,1,0:T(2,128)(2,1)}), bf16[96,2,152]{2,1,0:T(2,128)(2,1)S(1)}, u32[]{:S(2)}, u32[]{:S(2)}) async-start(bf16[96,2,152]{2,1,0:T(2,128)(2,1)} %reshape.1076), calls=%async_computation.5 | async-start | bytes 196608 | tf_op jit(solution)/shard_map/all_to_all | solution.py:145
  158.9 2.9 %fusion.14 = (f32[16,48]{1,0:T(8,128)S(1)}, f32[16,48]{1,0:T(8,128)S(1)}, f32[16,48]{1,0:T(8,128)S(1)}, f32[16,48]{1,0:T(8,128)S(1)}, f32[16,48]{1,0:T(8,128)S(1)}, /*index=5*/f32[16,48]{1,0:T(8,128)S(1)}) fusion(f32[16,48]{1,0:T(8,128)S(1)} %sub.116, f32[256]{0:T(256)S(1)} %get-tuple-element.73, f32[16,48]{1,0:T(8,128)S(1)} %mul.1397, ...), kind=kLoop, calls=%fused_computation.36 | loop fusion | flops 9432576 | bytes 2398208 | tf_op jit(solution)/shard_map/transpose(jvp(vmap()))/reduce_sum | solution.py:48
  162.2 3.4 %scatter_fusion = bf16[6,192,8]{2,0,1:T(8,128)(2,1)S(1)} fusion(bf16[6,192,8]{2,0,1:T(8,128)(2,1)S(1)} %broadcast_in_dim.16, s32[96]{0:T(128)S(1)} %fusion.51, bf16[96,6,8]{2,1,0:T(8,128)(2,1)S(1)} %copy.123), kind=kCustom, calls=%fused_computation.5 | custom fusion | bytes 28032 | tf_op jit(solution)/shard_map/scatter | solution.py:136
  166.5 1.3 all-to-all-done.4
  167.9 11.9 %all-to-all-start.3 = ((bf16[6,96,16]{2,0,1:T(8,128)(2,1)}), bf16[6,96,16]{2,0,1:T(8,128)(2,1)S(1)}, u32[]{:S(2)}, u32[]{:S(2)}) async-start(bf16[6,96,16]{2,0,1:T(8,128)(2,1)} %copy.125), calls=%async_computation.3 | async-start | bytes 393216 | tf_op jit(solution)/shard_map/all_to_all | solution.py:144
  180.7 1.4 copy.135
  182.2 12.8 %all-to-all-done.3 = bf16[6,96,16]{2,0,1:T(8,128)(2,1)S(1)} async-done(((bf16[6,96,16]{2,0,1:T(8,128)(2,1)}), bf16[6,96,16]{2,0,1:T(8,128)(2,1)S(1)}, u32[]{:S(2)}, u32[]{:S(2)}) %all-to-all-start.3) | async-done | bytes 18464 | tf_op jit(solution)/shard_map/all_to_all | solution.py:144
  194.9 2.4 fusion.35
  203.6 1.5 convolution_bitcast_fusion
  206.3 20.6 %reduce-scatter.5.cloned.1.call-done = f32[19,256]{0,1:T(8,128)} async-done(((f32[19,2048]{0,1:T(8,128)}), f32[19,256]{0,1:T(8,128)}) %reduce-scatter.5.cloned.1.call-update) | async-done | bytes 19472 | tf_op jit(solution)/shard_map/reduce_scatter | solution.py:168
  226.9 1.6 copy.137
  228.5 43.0 %reduce-scatter.3.cloned.1.call-done = f32[6,256]{1,0:T(8,128)} async-done(((f32[6,2048]{1,0:T(8,128)}), f32[6,256]{1,0:T(8,128)}) %reduce-scatter.3.cloned.1.call-update) | async-done | bytes 6160 | tf_op jit(solution)/shard_map/reduce_scatter | solution.py:167
  (126 shorter events, 33.1 us)
Async XLA Ops:
  10.3 77.1 %all-to-all-start = ((s32[96,2,1]{1,2,0:T(1,128)}), s32[96,2,1]{1,2,0:T(1,128)S(1)}, u32[]{:S(2)}, u32[]{:S(2)}) async-start(s32[96,2,1]{1,2,0:T(1,128)} %bitcast.3), calls=%async_computation | async-start | bytes 98304 | tf_op jit(solution)/shard_map/all_to_all | solution.py:109
  85.1 1.8 copy-start
  96.1 28.4 %all-to-all-start.2 = ((bf16[6,96,16]{2,0,1:T(8,128)(2,1)}), bf16[6,96,16]{2,0,1:T(8,128)(2,1)S(1)}, u32[]{:S(2)}, u32[]{:S(2)}) async-start(bf16[6,96,16]{2,0,1:T(8,128)(2,1)} %copy.112), calls=%async_computation.2 | async-start | bytes 393216 | tf_op jit(solution)/shard_map/all_to_all | solution.py:116
  124.5 19.9 %all-to-all-start.1 = ((bf16[96,2,152]{2,1,0:T(2,128)(2,1)}), bf16[96,2,152]{2,1,0:T(2,128)(2,1)S(1)}, u32[]{:S(2)}, u32[]{:S(2)}) async-start(bf16[96,2,152]{2,1,0:T(2,128)(2,1)} %reshape.1074), calls=%async_computation.1 | async-start | bytes 196608 | tf_op jit(solution)/shard_map/all_to_all | solution.py:117
  144.3 23.5 %all-to-all-start.4 = ((bf16[96,2,152]{2,1,0:T(2,128)(2,1)}), bf16[96,2,152]{2,1,0:T(2,128)(2,1)S(1)}, u32[]{:S(2)}, u32[]{:S(2)}) async-start(bf16[96,2,152]{2,1,0:T(2,128)(2,1)} %reshape.1076), calls=%async_computation.5 | async-start | bytes 196608 | tf_op jit(solution)/shard_map/all_to_all | solution.py:145
  167.9 27.1 %all-to-all-start.3 = ((bf16[6,96,16]{2,0,1:T(8,128)(2,1)}), bf16[6,96,16]{2,0,1:T(8,128)(2,1)S(1)}, u32[]{:S(2)}, u32[]{:S(2)}) async-start(bf16[6,96,16]{2,0,1:T(8,128)(2,1)} %copy.125), calls=%async_computation.3 | async-start | bytes 393216 | tf_op jit(solution)/shard_map/all_to_all | solution.py:144
  179.8 47.1 %reduce-scatter.5.cloned.1.call-start = ((), (), s32[]{:S(2)}) async-start(), calls=%async_computation.8 | async-start | bytes 1179648 | tf_op jit(solution)/shard_map/reduce_scatter | solution.py:168
  182.1 89.4 %reduce-scatter.3.cloned.1.call-start = ((), (), s32[]{:S(2)}) async-start(), calls=%async_computation.7 | async-start | bytes 73728 | tf_op jit(solution)/shard_map/reduce_scatter | solution.py:167
Sparse Core Ops, SparseCore 0:
  183.7 43.0 reduce-scatter.4
  230.5 40.9 reduce-scatter.2
where the time goes:
time: 279 us; the launch traced here: 278 us
  waiting for transfers between devices  90.9 us (33%)
  starting transfers between devices  64.3 us (23%)
  blocking collectives  50.8 us (18%)
  local copies, waits for them, and re-layouts  32.5 us (12%)
  other arithmetic  18.9 us (7%)
  between operations  16.1 us (6%)
  matrix products  5.02 us (2%)
    reduce_scatter x1, waiting for transfers between devices, local(): lax.psum_scatter(column_geometry, 'cams', scatter_dimension=1, tiled=True)  43 us
    all_gather x1, blocking collectives, local(): lax.all_gather(appearance, 'cams', axis=1, tiled=True)  26.2 us
    all_gather x1, blocking collectives, local(): lax.all_gather(geometry, 'cams', axis=1, tiled=True)  24.6 us
    reduce_scatter x1, waiting for transfers between devices, local(): lax.psum_scatter(column_colour, 'cams', scatter_dimension=1, tiled=True)  20.6 us
    all_to_all x1, starting transfers between devices, local(): lax.all_to_all(request, 'tiles', split_axis=0, concat_axis=0, tiled=True)  19.4 us
    all_to_all x1, starting transfers between devices, local(): lax.all_to_all(send_proj, 'tiles', split_axis=1, concat_axis=1, tiled=True)  13.2 us
    all_to_all x1, waiting for transfers between devices, local(): lax.all_to_all(back_proj.reshape(6, -1), 'tiles', split_axis=1, concat_ax...  12.8 us
    all_to_all x1, starting transfers between devices, local(): lax.all_to_all(back_proj.reshape(6, -1), 'tiles', split_axis=1, concat_ax...  11.9 us
  transfers between devices with their start and end apart: 7, of which 6 were waited for; matrix products, arithmetic and copies ran while one was open for 16% of the time, Pallas kernels for 0%

commit v1 on v0

--- a/solution.py
+++ b/solution.py
@@ -94,10 +94,10 @@
     slot_count = columns * capacity
     channels = appearance.shape[0]
     geometry = jnp.concatenate([offsets, factor_diag, factor_off[None, :], logit[None, :]], axis=0)
-    geometry_col, appearance_col = (
-        lax.all_gather(geometry, "cams", axis=1, tiled=True),
-        lax.all_gather(appearance, "cams", axis=1, tiled=True),
-    )
+    params = jnp.concatenate([geometry, appearance], axis=0)
+    params_col = lax.all_gather(params, "cams", axis=1, tiled=True)
+    geometry_col = params_col[:6]
+    appearance_col = params_col[6:]
     per_column = geometry_col.shape[1] // BLK
     linear = cam_linear[0]
     camera_shift = cam_shift[0]
@@ -112,12 +112,15 @@
         channels, slot_count * BLK
     )
     send_proj = project(raw_params, linear, camera_shift).astype(jnp.bfloat16)
-    got_proj, got_colour = (
-        lax.all_to_all(send_proj, "tiles", split_axis=1, concat_axis=1, tiled=True),
-        lax.all_to_all(
-            raw_colours.astype(jnp.bfloat16), "tiles", split_axis=1, concat_axis=1, tiled=True
-        ),
-    )
+    sent = lax.all_to_all(
+        jnp.concatenate([send_proj, raw_colours.astype(jnp.bfloat16)], axis=0),
+        "tiles",
+        split_axis=1,
+        concat_axis=1,
+        tiled=True,
+    )
+    got_proj = sent[:6]
+    got_colour = sent[6:]
     projected = (
         got_proj.reshape(6, slot_count, BLK)[:, entry_slot]
         .reshape(6, entry_count * BLK)
@@ -140,12 +143,15 @@
         .at[:, entry_slot]
         .set(grad_colour.reshape(channels, entry_count, BLK).astype(jnp.bfloat16))
     )
-    ret_proj, ret_colour = (
-        lax.all_to_all(back_proj.reshape(6, -1), "tiles", split_axis=1, concat_axis=1, tiled=True),
-        lax.all_to_all(
-            back_colour.reshape(channels, -1), "tiles", split_axis=1, concat_axis=1, tiled=True
-        ),
-    )
+    returned = lax.all_to_all(
+        jnp.concatenate([back_proj.reshape(6, -1), back_colour.reshape(channels, -1)], axis=0),
+        "tiles",
+        split_axis=1,
+        concat_axis=1,
+        tiled=True,
+    )
+    ret_proj = returned[:6]
+    ret_colour = returned[6:]
     unused, pull_params = jax.vjp(lambda params: project(params, linear, camera_shift), raw_params)
     grad_raw = pull_params(ret_proj.astype(jnp.float32))[0]
     owner_hot = (wanted[:, None] == jnp.arange(per_column, dtype=jnp.int32)[None, :]).astype(
@@ -163,10 +169,14 @@
 
     column_geometry = collect(grad_raw, 6)
     column_colour = collect(ret_colour.astype(jnp.float32), channels)
-    grad_geometry, grad_appearance = (
-        lax.psum_scatter(column_geometry, "cams", scatter_dimension=1, tiled=True),
-        lax.psum_scatter(column_colour, "cams", scatter_dimension=1, tiled=True),
-    )
+    grads = lax.psum_scatter(
+        jnp.concatenate([column_geometry, column_colour], axis=0),
+        "cams",
+        scatter_dimension=1,
+        tiled=True,
+    )
+    grad_geometry = grads[:6]
+    grad_appearance = grads[6:]
     return (picture.reshape(channels, 1, -1), grad_geometry, grad_appearance)
 
 

time: 279 us -> 202 us (0.72)
  waiting for transfers between devices: 90.9 us -> 53.9 us
  blocking collectives: 50.8 us -> 26.4 us
  starting transfers between devices: 64.3 us -> 40.9 us
  local copies, waits for them, and re-layouts: 32.5 us -> 37.8 us
    reduce_scatter x2 -> x1, waiting for transfers between devices: 63.6 us -> 32.2 us  [local(): lax.psum_scatter(jnp.concatenate([column_geometry, column_colour], axis=0...]
    all_gather x2 -> x1, blocking collectives: 50.8 us -> 26.4 us  [local(): params_col = lax.all_gather(params, 'cams', axis=1, tiled=True)]
    all_to_all x4 -> x2, starting transfers between devices: 44.6 us -> 21.3 us  [the longest x1 13.4 us: local(): lax.all_to_all(jnp.concatenate([send_proj, raw_colours.astype(jnp.bfloat1...]
    all_to_all x4 -> x2, waiting for transfers between devices: 27.2 us -> 21.6 us  [the longest x1 11 us: local(): lax.all_to_all(jnp.concatenate([back_proj.reshape(6, -1), back_colour.res...]
    concatenate x0 -> x3, local copies, waits for them, and re-layouts: none -> 3.98 us  [the longest x1 1.55 us: local(): params = jnp.concatenate([geometry, appearance], axis=0)]
    slice x0 -> x7, local copies, waits for them, and re-layouts: none -> 3.33 us  [the longest x1 1.37 us: local(): grad_appearance = grads[6:]]
  transfers between devices with their start and end apart: 7 -> 4, of which waited for: 6 -> 3; matrix products, arithmetic and copies ran while one was open for 16% -> 5% of each run, Pallas kernels for 0% -> 0%
where the time goes in v1:
time: 202 us; the launch traced here: 201 us
  waiting for transfers between devices  53.9 us (27%)
  starting transfers between devices  40.9 us (20%)
  local copies, waits for them, and re-layouts  37.8 us (19%)
  blocking collectives  26.4 us (13%)
  other arithmetic  21 us (10%)
  between operations  16 us (8%)
  matrix products  4.97 us (2%)
    reduce_scatter x1, waiting for transfers between devices, local(): lax.psum_scatter(jnp.concatenate([column_geometry, column_colour], axis=0...  32.2 us
    all_gather x1, blocking collectives, local(): params_col = lax.all_gather(params, 'cams', axis=1, tiled=True)  26.4 us
    all_to_all x1, starting transfers between devices, local(): lax.all_to_all(request, 'tiles', split_axis=0, concat_axis=0, tiled=True)  19.4 us
    all_to_all x1, starting transfers between devices, local(): lax.all_to_all(jnp.concatenate([send_proj, raw_colours.astype(jnp.bfloat1...  13.4 us
    all_to_all x1, waiting for transfers between devices, local(): lax.all_to_all(jnp.concatenate([back_proj.reshape(6, -1), back_colour.res...  11 us
    all_to_all x1, waiting for transfers between devices, local(): lax.all_to_all(jnp.concatenate([send_proj, raw_colours.astype(jnp.bfloat1...  10.6 us
    all_to_all x1, starting transfers between devices, local(): lax.all_to_all(jnp.concatenate([back_proj.reshape(6, -1), back_colour.res...  7.87 us
    dot_general x3, matrix products, render_tile(): jnp.dot(colours, weight, precision=lax.Precision.HIGHEST, preferred_eleme...  4.38 us
  transfers between devices with their start and end apart: 4, of which 3 were waited for; matrix products, arithmetic and copies ran while one was open for 5% of the time, Pallas kernels for 0%

profile of v1, /device:TPU:6, one launch (start us, length us, event | category | flops | bytes accessed | tf_op | source)
XLA Modules:
  0.0 200.9 jit_solution(8236717117568908258)
XLA Ops:
  10.3 19.4 %all-to-all-start = ((s32[96,2,1]{1,2,0:T(1,128)}), s32[96,2,1]{1,2,0:T(1,128)S(1)}, u32[]{:S(2)}, u32[]{:S(2)}) async-start(s32[96,2,1]{1,2,0:T(1,128)} %bitcast.5), calls=%async_computation | async-start | bytes 98304 | tf_op jit(solution)/shard_map/all_to_all | solution.py:109
  29.6 1.5 fusion.57
  31.1 1.3 fusion.58
  32.4 1.6 concatenate.21
  34.0 26.4 %all_gather.3 = f32[25,2048]{1,0:T(8,128)S(1)} all-gather(f32[25,256]{1,0:T(8,128)S(1)} %concatenate.21), channel_id=1, replica_groups=mesh['tiles'=96,'cams'=8] {'cams'}, dimensions={1}, use_global_device_ids=true | all-gather | bytes 230400 | tf_op jit(solution)/shard_map/all_gather | solution.py:98
  65.5 2.0 slice_add_fusion
  70.2 2.5 %add_convert_fusion.1 = (bf16[1,192,8]{1,2,0:T(8,128)(2,1)S(1)}, bf16[1,192,8]{1,2,0:T(8,128)(2,1)S(1)}) fusion(f32[6,192,8]{1,2,0:T(8,128)S(1)} %bitcast.104, f32[]{:T(128)} %bitcast.12, f32[]{:T(128)} %bitcast.11, f32[]{:T(128)} %bitcast.10, f32[]{:T(128)} %bitcast.9, f32[]{:T(128)} %bitcast.8, f32[]{:T(128)} %bitcast), kind=kLoop, calls=%fused_computation.111 | loop fusion | flops 15360 | bytes 18456 | tf_op jit(solution)/shard_map/convert.6
  74.3 1.2 concatenate.22
  76.6 13.4 %all-to-all-start.1 = ((bf16[96,2,200]{2,1,0:T(2,128)(2,1)}), bf16[96,2,200]{2,1,0:T(2,128)(2,1)S(1)}, u32[]{:S(2)}, u32[]{:S(2)}) async-start(bf16[96,2,200]{2,1,0:T(2,128)(2,1)} %reshape.1047), calls=%async_computation.1 | async-start | bytes 196608 | tf_op jit(solution)/shard_map/all_to_all | solution.py:115
  91.5 10.6 %all-to-all-done.1 = bf16[96,2,200]{2,1,0:T(2,128)(2,1)S(1)} async-done(((bf16[96,2,200]{2,1,0:T(2,128)(2,1)}), bf16[96,2,200]{2,1,0:T(2,128)(2,1)S(1)}, u32[]{:S(2)}, u32[]{:S(2)}) %all-to-all-start.1) | async-done | bytes 76832 | tf_op jit(solution)/shard_map/all_to_all | solution.py:115
  107.7 1.8 fusion
  111.6 2.9 %fusion.14 = (f32[16,48]{1,0:T(8,128)S(1)}, f32[16,48]{1,0:T(8,128)S(1)}, f32[16,48]{1,0:T(8,128)S(1)}, f32[16,48]{1,0:T(8,128)S(1)}, f32[16,48]{1,0:T(8,128)S(1)}, /*index=5*/f32[16,48]{1,0:T(8,128)S(1)}) fusion(f32[16,48]{1,0:T(8,128)S(1)} %sub.116, f32[256]{0:T(256)S(1)} %get-tuple-element.82, f32[16,48]{1,0:T(8,128)S(1)} %mul.1397, ...), kind=kLoop, calls=%fused_computation.36 | loop fusion | flops 9432576 | bytes 2398208 | tf_op jit(solution)/shard_map/transpose(jvp(vmap()))/reduce_sum | solution.py:48
  114.8 3.4 %scatter_fusion = bf16[6,192,8]{2,0,1:T(8,128)(2,1)S(1)} fusion(bf16[6,192,8]{2,0,1:T(8,128)(2,1)S(1)} %broadcast_in_dim.16, s32[96]{0:T(128)S(1)} %copy-done.3, bf16[96,6,8]{2,1,0:T(8,128)(2,1)S(1)} %copy.232), kind=kCustom, calls=%fused_computation.5 | custom fusion | bytes 28032 | tf_op jit(solution)/shard_map/scatter | solution.py:139
  118.2 1.2 copy.251
  119.7 3.4 %scatter_fusion.1 = bf16[19,192,8]{0,2,1:T(8,128)(2,1)S(1)} fusion(bf16[19,192,8]{0,2,1:T(8,128)(2,1)S(1)} %broadcast_in_dim.20, s32[96]{0:T(128)S(1)} %copy-done.3, bf16[96,19,8]{1,2,0:T(8,128)(2,1)S(1)} %bitcast.93), kind=kCustom, calls=%fused_computation.6 | custom fusion | bytes 87936 | tf_op jit(solution)/shard_map/scatter | solution.py:144
  124.4 7.9 %all-to-all-start.2 = ((bf16[96,2,200]{2,1,0:T(2,128)(2,1)}), bf16[96,2,200]{2,1,0:T(2,128)(2,1)S(1)}, u32[]{:S(2)}, u32[]{:S(2)}) async-start(bf16[96,2,200]{2,1,0:T(2,128)(2,1)} %reshape.1049), calls=%async_computation.2 | async-start | bytes 196608 | tf_op jit(solution)/shard_map/all_to_all | solution.py:146
  133.2 11.0 %all-to-all-done.2 = bf16[96,2,200]{2,1,0:T(2,128)(2,1)S(1)} async-done(((bf16[96,2,200]{2,1,0:T(2,128)(2,1)}), bf16[96,2,200]{2,1,0:T(2,128)(2,1)S(1)}, u32[]{:S(2)}, u32[]{:S(2)}) %all-to-all-start.2) | async-done | bytes 76832 | tf_op jit(solution)/shard_map/all_to_all | solution.py:146
  144.8 4.0 %fusion.17 = (f32[96,16]{1,0:T(8,128)S(1)}, f32[96,16]{1,0:T(8,128)S(1)}, f32[96,16]{1,0:T(8,128)S(1)}, f32[96,16]{1,0:T(8,128)S(1)}, f32[96,16]{1,0:T(8,128)S(1...) fusion(f32[6,96,16]{0,2,1:T(8,128)S(1)} %slice_convert_fusion, f32[]{:T(128)} %bitcast.10, ...), kind=kLoop, calls=%fused_computation.43 | loop fusion | flops 7680 | bytes 86032 | tf_op jit(solution)/shard_map/transpose(jvp())/mul | solution.py:33
  149.6 1.4 negate_add_fusion
  151.0 1.4 multiply_add_fusion.4
  156.6 1.5 convolution_bitcast_fusion
  159.2 32.2 %reduce-scatter.2.cloned.1.call-done = f32[25,256]{1,0:T(8,128)} async-done(((f32[25,2048]{1,0:T(8,128)}), f32[25,256]{1,0:T(8,128)}) %reduce-scatter.2.cloned.1.call-update) | async-done | bytes 25616 | tf_op jit(solution)/shard_map/reduce_scatter | solution.py:172
  191.4 1.4 slice.175
  192.8 1.3 slice.174
  (128 shorter events, 30.3 us)
Async XLA Ops:
  8.6 23.8 %copy-start.2 = (s32[96]{0:T(128)}, s32[96]{0:T(128)S(1)}, u32[]{:S(2)}) copy-start(s32[96]{0:T(128)S(1)} %fusion.48) | copy-start | bytes 1156
  10.3 52.6 %all-to-all-start = ((s32[96,2,1]{1,2,0:T(1,128)}), s32[96,2,1]{1,2,0:T(1,128)S(1)}, u32[]{:S(2)}, u32[]{:S(2)}) async-start(s32[96,2,1]{1,2,0:T(1,128)} %bitcast.5), calls=%async_computation | async-start | bytes 98304 | tf_op jit(solution)/shard_map/all_to_all | solution.py:109
  74.3 15.7 %copy-start = (bf16[19,1,4096]{2,0,1:T(8,128)(2,1)S(1)}, bf16[19,1,4096]{2,0,1:T(8,128)(2,1)}, u32[]{:S(2)}) copy-start(bf16[19,1,4096]{2,0,1:T(8,128)(2,1)} %param.17) | copy-start | bytes 466948
  75.5 14.6 %copy-start.3 = (s32[96]{0:T(128)S(1)}, s32[96]{0:T(128)}, u32[]{:S(2)}) copy-start(s32[96]{0:T(128)} %copy-done.2) | copy-start | bytes 1156
  75.6 14.6 %copy-start.1 = (f32[1,192,8]{1,2,0:T(8,128)S(1)}, f32[1,192,8]{1,2,0:T(8,128)}, u32[]{:S(2)}) copy-start(f32[1,192,8]{1,2,0:T(8,128)} %get-tuple-element.64) | copy-start | bytes 18436
  76.6 25.4 %all-to-all-start.1 = ((bf16[96,2,200]{2,1,0:T(2,128)(2,1)}), bf16[96,2,200]{2,1,0:T(2,128)(2,1)S(1)}, u32[]{:S(2)}, u32[]{:S(2)}) async-start(bf16[96,2,200]{2,1,0:T(2,128)(2,1)} %reshape.1047), calls=%async_computation.1 | async-start | bytes 196608 | tf_op jit(solution)/shard_map/all_to_all | solution.py:115
  124.4 19.9 %all-to-all-start.2 = ((bf16[96,2,200]{2,1,0:T(2,128)(2,1)}), bf16[96,2,200]{2,1,0:T(2,128)(2,1)S(1)}, u32[]{:S(2)}, u32[]{:S(2)}) async-start(bf16[96,2,200]{2,1,0:T(2,128)(2,1)} %reshape.1049), calls=%async_computation.2 | async-start | bytes 196608 | tf_op jit(solution)/shard_map/all_to_all | solution.py:146
  132.2 59.2 %reduce-scatter.2.cloned.1.call-start = ((), (), s32[]{:S(2)}) async-start(), calls=%async_computation.4 | async-start | bytes 294912 | tf_op jit(solution)/shard_map/reduce_scatter | solution.py:172
Sparse Core Ops, SparseCore 0:
  156.7 34.6 reduce-scatter.1

commit v2 on v1

--- a/solution.py
+++ b/solution.py
@@ -95,7 +95,11 @@
     channels = appearance.shape[0]
     geometry = jnp.concatenate([offsets, factor_diag, factor_off[None, :], logit[None, :]], axis=0)
     params = jnp.concatenate([geometry, appearance], axis=0)
-    params_col = lax.all_gather(params, "cams", axis=1, tiled=True)
+    cams = lax.axis_size("cams")
+    gathered = lax.all_to_all(
+        jnp.broadcast_to(params[None], (cams,) + params.shape), "cams", 0, 0, tiled=True
+    )
+    params_col = gathered.transpose(1, 0, 2).reshape(params.shape[0], cams * params.shape[1])
     geometry_col = params_col[:6]
     appearance_col = params_col[6:]
     per_column = geometry_col.shape[1] // BLK
@@ -169,12 +173,11 @@
 
     column_geometry = collect(grad_raw, 6)
     column_colour = collect(ret_colour.astype(jnp.float32), channels)
-    grads = lax.psum_scatter(
-        jnp.concatenate([column_geometry, column_colour], axis=0),
-        "cams",
-        scatter_dimension=1,
-        tiled=True,
-    )
+    column_all = jnp.concatenate([column_geometry, column_colour], axis=0)
+    rows = column_all.shape[0]
+    grads = lax.all_to_all(
+        column_all.reshape(rows, cams, -1), "cams", 1, 1, tiled=True
+    ).sum(axis=1)
     grad_geometry = grads[:6]
     grad_appearance = grads[6:]
     return (picture.reshape(channels, 1, -1), grad_geometry, grad_appearance)

time: 202 us -> 158 us (0.78)
  blocking collectives: 26.4 us -> 0 us
  between operations: 16 us -> 2.65 us
  waiting for transfers between devices: 53.9 us -> 46.7 us
  starting transfers between devices: 40.9 us -> 45.6 us
    reduce_scatter x1 -> x0, waiting for transfers between devices: 32.2 us -> none  [local(): lax.psum_scatter(jnp.concatenate([column_geometry, column_colour], axis=0...]
    all_gather x1 -> x0, blocking collectives: 26.4 us -> none  [local(): params_col = lax.all_gather(params, 'cams', axis=1, tiled=True)]
    all_to_all x0 -> x2, waiting for transfers between devices: none -> 17.4 us  [the longest x1 9 us: local(): lax.all_to_all(column_all.reshape(rows, cams, -1), 'cams', 1, 1, tiled=True)]
    all_to_all x0 -> x2, starting transfers between devices: none -> 10.5 us  [the longest x1 7.1 us: local(): lax.all_to_all(jnp.broadcast_to(params[None], (cams,) + params.shape), 'c...]
    all_to_all x1, waiting for transfers between devices: 0.01 us -> 7.43 us  [local(): lax.all_to_all(request, 'tiles', split_axis=0, concat_axis=0, tiled=True)]
    all_to_all x1, starting transfers between devices: 13.4 us -> 7.88 us  [local(): lax.all_to_all(jnp.concatenate([send_proj, raw_colours.astype(jnp.bfloat1...]
  transfers between devices with their start and end apart: 4 -> 5, of which waited for: 3 -> 5; matrix products, arithmetic and copies ran while one was open for 5% -> 6% of each run, Pallas kernels for 0% -> 0%
where the time goes in v2:
time: 158 us; the launch traced here: 157 us
  waiting for transfers between devices  46.7 us (30%)
  starting transfers between devices  45.6 us (29%)
  local copies, waits for them, and re-layouts  36.8 us (23%)
  other arithmetic  19.8 us (13%)
  matrix products  4.97 us (3%)
  between operations  2.65 us (2%)
    all_to_all x1, starting transfers between devices, local(): lax.all_to_all(request, 'tiles', split_axis=0, concat_axis=0, tiled=True)  19.4 us
    all_to_all x1, waiting for transfers between devices, local(): lax.all_to_all(jnp.concatenate([back_proj.reshape(6, -1), back_colour.res...  11.4 us
    all_to_all x1, waiting for transfers between devices, local(): lax.all_to_all(jnp.concatenate([send_proj, raw_colours.astype(jnp.bfloat1...  10.6 us
    all_to_all x1, waiting for transfers between devices, local(): lax.all_to_all(column_all.reshape(rows, cams, -1), 'cams', 1, 1, tiled=True)  9 us
    all_to_all x1, waiting for transfers between devices, local(): lax.all_to_all(jnp.broadcast_to(params[None], (cams,) + params.shape), 'c...  8.36 us
    all_to_all x1, starting transfers between devices, local(): lax.all_to_all(jnp.concatenate([send_proj, raw_colours.astype(jnp.bfloat1...  7.88 us
    all_to_all x1, starting transfers between devices, local(): lax.all_to_all(jnp.concatenate([back_proj.reshape(6, -1), back_colour.res...  7.88 us
    all_to_all x1, waiting for transfers between devices, local(): lax.all_to_all(request, 'tiles', split_axis=0, concat_axis=0, tiled=True)  7.43 us
  transfers between devices with their start and end apart: 5, of which 5 were waited for; matrix products, arithmetic and copies ran while one was open for 6% of the time, Pallas kernels for 0%

profile of v2, /device:TPU:6, one launch (start us, length us, event | category | flops | bytes accessed | tf_op | source)
XLA Modules:
  0.0 156.7 jit_solution(16366336310787599004)
XLA Ops:
  3.7 19.4 %all-to-all-start.1 = ((s32[96,2,1]{1,2,0:T(1,128)}), s32[96,2,1]{1,2,0:T(1,128)S(1)}, u32[]{:S(2)}, u32[]{:S(2)}) async-start(s32[96,2,1]{1,2,0:T(1,128)} %bitcast.6), calls=%async_computation.1 | async-start | bytes 98304 | tf_op jit(solution)/shard_map/all_to_all | solution.py:113
  23.1 1.5 fusion.57
  24.6 1.6 concatenate.26
  26.1 7.4 %all-to-all-done.1 = s32[96,2,1]{1,2,0:T(1,128)S(1)} async-done(((s32[96,2,1]{1,2,0:T(1,128)}), s32[96,2,1]{1,2,0:T(1,128)S(1)}, u32[]{:S(2)}, u32[]{:S(2)}) %all-to-all-start.1) | async-done | bytes 800 | tf_op jit(solution)/shard_map/all_to_all | solution.py:113
  34.3 7.1 %all-to-all-start = ((f32[8,25,256]{2,1,0:T(8,128)}), f32[8,25,256]{2,1,0:T(8,128)S(1)}, u32[]{:S(2)}, u32[]{:S(2)}) async-start(f32[8,25,256]{2,1,0:T(8,128)} %broadcast_in_dim.18), calls=%async_computation | async-start | bytes 524288 | tf_op jit(solution)/shard_map/all_to_all | solution.py:99
  44.6 8.4 %all-to-all-done = f32[8,25,256]{2,1,0:T(8,128)S(1)} async-done(((f32[8,25,256]{2,1,0:T(8,128)}), f32[8,25,256]{2,1,0:T(8,128)S(1)}, u32[]{:S(2)}, u32[]{:S(2)}) %all-to-all-start) | async-done | bytes 204832 | tf_op jit(solution)/shard_map/all_to_all | solution.py:99
  55.2 1.8 %slice_add_fusion = (f32[1,192,8]{1,2,0:T(8,128)S(1)}, f32[1,192,8]{1,2,0:T(8,128)S(1)}, f32[1,192,8]{1,2,0:T(8,128)S(1)}, f32[1,192,8]{1,2,0:T(8,128)S(1)}, f32...) fusion(f32[6,192,8]{1,2,0:T(8,128)S(1)} %bitcast.108, ...), kind=kLoop, calls=%fused_computation.113 | loop fusion | flops 53760 | bytes 82960 | tf_op jit(solution)/shard_map/transpose(jvp())/mul | solution.py:22
  59.7 2.5 %add_convert_fusion.1 = (bf16[1,192,8]{1,2,0:T(8,128)(2,1)S(1)}, bf16[1,192,8]{1,2,0:T(8,128)(2,1)S(1)}) fusion(f32[6,192,8]{1,2,0:T(8,128)S(1)} %bitcast.109, f32[]{:T(128)} %bitcast.13, f32[]{:T(128)} %bitcast.12, f32[]{:T(128)} %bitcast.11, f32[]{:T(128)} %bitcast.10, f32[]{:T(128)} %bitcast.9, f32[]{:T(128)} %bitcast), kind=kLoop, calls=%fused_computation.111 | loop fusion | flops 15360 | bytes 18456 | tf_op jit(solution)/shard_map/convert.6
  64.1 1.2 concatenate.27
  66.4 7.9 %all-to-all-start.2 = ((bf16[96,2,200]{2,1,0:T(2,128)(2,1)}), bf16[96,2,200]{2,1,0:T(2,128)(2,1)S(1)}, u32[]{:S(2)}, u32[]{:S(2)}) async-start(bf16[96,2,200]{2,1,0:T(2,128)(2,1)} %reshape.1052), calls=%async_computation.2 | async-start | bytes 196608 | tf_op jit(solution)/shard_map/all_to_all | solution.py:119
  75.7 10.6 %all-to-all-done.2 = bf16[96,2,200]{2,1,0:T(2,128)(2,1)S(1)} async-done(((bf16[96,2,200]{2,1,0:T(2,128)(2,1)}), bf16[96,2,200]{2,1,0:T(2,128)(2,1)S(1)}, u32[]{:S(2)}, u32[]{:S(2)}) %all-to-all-start.2) | async-done | bytes 76832 | tf_op jit(solution)/shard_map/all_to_all | solution.py:119
  91.9 1.8 %fusion = bf16[19,16,48]{2,0,1:T(8,128)(2,1)S(1)} fusion(f32[16,48]{1,0:T(8,128)S(1)} %mul.1397, f32[16,48]{1,0:T(8,128)S(1)} %sub.116, f32[256]{0:T(256)S(1)} %get-tuple-element.82, f32[16,48]{1,0:T(8,128)S(1)} %mul.1393, f32[16,48]{1,0:T(8,128)S(1)} %sub.110, f32[256]{0:T(256)S(1)} %get-tuple-element.83, f32[16,48]{1,0:T(8,128)S(1)} %mul.1388, ...), kind=kOutput, calls=%fused_computation.21 | convolution fusion | flops 47790336 | bytes 991744 | tf_op jit(solution)/shard_map/transpose(jvp(vmap()))/dot_general | solution.py:53
  95.8 2.9 %fusion.14 = (f32[16,48]{1,0:T(8,128)S(1)}, f32[16,48]{1,0:T(8,128)S(1)}, f32[16,48]{1,0:T(8,128)S(1)}, f32[16,48]{1,0:T(8,128)S(1)}, f32[16,48]{1,0:T(8,128)S(1)}, /*index=5*/f32[16,48]{1,0:T(8,128)S(1)}) fusion(f32[16,48]{1,0:T(8,128)S(1)} %sub.116, f32[256]{0:T(256)S(1)} %get-tuple-element.82, f32[16,48]{1,0:T(8,128)S(1)} %mul.1397, ...), kind=kLoop, calls=%fused_computation.37 | loop fusion | flops 9432576 | bytes 2398208 | tf_op jit(solution)/shard_map/transpose(jvp(vmap()))/reduce_sum | solution.py:48
  99.1 3.4 %scatter_fusion = bf16[6,192,8]{2,0,1:T(8,128)(2,1)S(1)} fusion(bf16[6,192,8]{2,0,1:T(8,128)(2,1)S(1)} %broadcast_in_dim.19, s32[96]{0:T(128)S(1)} %copy-done.5, bf16[96,6,8]{2,1,0:T(8,128)(2,1)S(1)} %copy.252), kind=kCustom, calls=%fused_computation.5 | custom fusion | bytes 28032 | tf_op jit(solution)/shard_map/scatter | solution.py:143
  102.5 1.2 copy.275
  103.9 3.4 %scatter_fusion.1 = bf16[19,192,8]{0,2,1:T(8,128)(2,1)S(1)} fusion(bf16[19,192,8]{0,2,1:T(8,128)(2,1)S(1)} %broadcast_in_dim.23, s32[96]{0:T(128)S(1)} %copy-done.5, bf16[96,19,8]{1,2,0:T(8,128)(2,1)S(1)} %bitcast.96), kind=kCustom, calls=%fused_computation.6 | custom fusion | bytes 87936 | tf_op jit(solution)/shard_map/scatter | solution.py:148
  108.6 7.9 %all-to-all-start.3 = ((bf16[96,2,200]{2,1,0:T(2,128)(2,1)}), bf16[96,2,200]{2,1,0:T(2,128)(2,1)S(1)}, u32[]{:S(2)}, u32[]{:S(2)}) async-start(bf16[96,2,200]{2,1,0:T(2,128)(2,1)} %reshape.1054), calls=%async_computation.3 | async-start | bytes 196608 | tf_op jit(solution)/shard_map/all_to_all | solution.py:150
  117.1 11.4 %all-to-all-done.3 = bf16[96,2,200]{2,1,0:T(2,128)(2,1)S(1)} async-done(((bf16[96,2,200]{2,1,0:T(2,128)(2,1)}), bf16[96,2,200]{2,1,0:T(2,128)(2,1)S(1)}, u32[]{:S(2)}, u32[]{:S(2)}) %all-to-all-start.3) | async-done | bytes 76832 | tf_op jit(solution)/shard_map/all_to_all | solution.py:150
  129.0 3.9 %fusion.17 = (f32[96,16]{1,0:T(8,128)S(1)}, f32[96,16]{1,0:T(8,128)S(1)}, f32[96,16]{1,0:T(8,128)S(1)}, f32[96,16]{1,0:T(8,128)S(1)}, f32[96,16]{1,0:T(8,128)S(1...) fusion(f32[6,96,16]{0,2,1:T(8,128)S(1)} %slice_convert_fusion, f32[]{:T(128)} %bitcast.11, ...), kind=kLoop, calls=%fused_computation.44 | loop fusion | flops 7680 | bytes 86032 | tf_op jit(solution)/shard_map/transpose(jvp())/mul | solution.py:33
  133.7 1.3 negate_add_fusion
  134.9 1.3 multiply_add_fusion.4
  140.4 3.4 %all-to-all-start.4 = ((f32[25,8,256]{2,0,1:T(8,128)}), f32[25,8,256]{2,0,1:T(8,128)S(1)}, u32[]{:S(2)}, u32[]{:S(2)}) async-start(f32[25,8,256]{2,0,1:T(8,128)} %copy.266), calls=%async_computation.4 | async-start | bytes 524288 | tf_op jit(solution)/shard_map/all_to_all | solution.py:178
  143.8 1.4 convolution_bitcast_fusion
  146.4 9.0 %all-to-all-done.4 = f32[25,8,256]{2,0,1:T(8,128)S(1)} async-done(((f32[25,8,256]{2,0,1:T(8,128)}), f32[25,8,256]{2,0,1:T(8,128)S(1)}, u32[]{:S(2)}, u32[]{:S(2)}) %all-to-all-start.4) | async-done | bytes 204832 | tf_op jit(solution)/shard_map/all_to_all | solution.py:178
  (136 shorter events, 32.6 us)
Async XLA Ops:
  0.6 40.8 %copy-start.6 = (f32[1,2]{1,0:T(1,128)S(1)}, f32[1,2]{1,0:T(1,128)}, u32[]{:S(2)}) copy-start(f32[1,2]{1,0:T(1,128)} %param.15) | copy-start | bytes 28
  2.1 22.5 %copy-start.4 = (s32[96]{0:T(128)}, s32[96]{0:T(128)S(1)}, u32[]{:S(2)}) copy-start(s32[96]{0:T(128)S(1)} %fusion.48) | copy-start | bytes 1156
  3.7 29.8 %all-to-all-start.1 = ((s32[96,2,1]{1,2,0:T(1,128)}), s32[96,2,1]{1,2,0:T(1,128)S(1)}, u32[]{:S(2)}, u32[]{:S(2)}) async-start(s32[96,2,1]{1,2,0:T(1,128)} %bitcast.6), calls=%async_computation.1 | async-start | bytes 98304 | tf_op jit(solution)/shard_map/all_to_all | solution.py:113
  34.3 18.7 %all-to-all-start = ((f32[8,25,256]{2,1,0:T(8,128)}), f32[8,25,256]{2,1,0:T(8,128)S(1)}, u32[]{:S(2)}, u32[]{:S(2)}) async-start(f32[8,25,256]{2,1,0:T(8,128)} %broadcast_in_dim.18), calls=%async_computation | async-start | bytes 524288 | tf_op jit(solution)/shard_map/all_to_all | solution.py:99
  64.1 10.2 %copy-start.2 = (bf16[19,1,4096]{2,0,1:T(8,128)(2,1)S(1)}, bf16[19,1,4096]{2,0,1:T(8,128)(2,1)}, u32[]{:S(2)}) copy-start(bf16[19,1,4096]{2,0,1:T(8,128)(2,1)} %param.17) | copy-start | bytes 466948
  65.3 9.0 %copy-start.5 = (s32[96]{0:T(128)S(1)}, s32[96]{0:T(128)}, u32[]{:S(2)}) copy-start(s32[96]{0:T(128)} %copy-done.4) | copy-start | bytes 1156
  65.3 9.2 %copy-start.3 = (f32[1,192,8]{1,2,0:T(8,128)S(1)}, f32[1,192,8]{1,2,0:T(8,128)}, u32[]{:S(2)}) copy-start(f32[1,192,8]{1,2,0:T(8,128)} %get-tuple-element.64) | copy-start | bytes 18436
  66.4 19.9 %all-to-all-start.2 = ((bf16[96,2,200]{2,1,0:T(2,128)(2,1)}), bf16[96,2,200]{2,1,0:T(2,128)(2,1)S(1)}, u32[]{:S(2)}, u32[]{:S(2)}) async-start(bf16[96,2,200]{2,1,0:T(2,128)(2,1)} %reshape.1052), calls=%async_computation.2 | async-start | bytes 196608 | tf_op jit(solution)/shard_map/all_to_all | solution.py:119
  91.2 4.6 %copy-start = (f32[16,48,256]{2,0,1:T(8,128)}, f32[16,48,256]{2,0,1:T(8,128)S(1)}, u32[]{:S(2)}) copy-start(f32[16,48,256]{2,0,1:T(8,128)S(1)} %fusion.24) | copy-start | bytes 2359300
  108.6 19.9 %all-to-all-start.3 = ((bf16[96,2,200]{2,1,0:T(2,128)(2,1)}), bf16[96,2,200]{2,1,0:T(2,128)(2,1)S(1)}, u32[]{:S(2)}, u32[]{:S(2)}) async-start(bf16[96,2,200]{2,1,0:T(2,128)(2,1)} %reshape.1054), calls=%async_computation.3 | async-start | bytes 196608 | tf_op jit(solution)/shard_map/all_to_all | solution.py:150
  139.3 4.5 %copy-start.1 = (f32[16,48,256]{2,0,1:T(8,128)S(1)}, f32[16,48,256]{2,0,1:T(8,128)}, u32[]{:S(2)}) copy-start(f32[16,48,256]{2,0,1:T(8,128)} %copy-done) | copy-start | bytes 2359300
  140.4 15.0 %all-to-all-start.4 = ((f32[25,8,256]{2,0,1:T(8,128)}), f32[25,8,256]{2,0,1:T(8,128)S(1)}, u32[]{:S(2)}, u32[]{:S(2)}) async-start(f32[25,8,256]{2,0,1:T(8,128)} %copy.266), calls=%async_computation.4 | async-start | bytes 524288 | tf_op jit(solution)/shard_map/all_to_all | solution.py:178

commit v3 on v2

--- a/solution.py
+++ b/solution.py
@@ -123,32 +123,29 @@
         concat_axis=1,
         tiled=True,
     )
-    got_proj = sent[:6]
-    got_colour = sent[6:]
-    projected = (
-        got_proj.reshape(6, slot_count, BLK)[:, entry_slot]
-        .reshape(6, entry_count * BLK)
-        .astype(jnp.float32)
-    )
-    colours = (
-        got_colour.reshape(channels, slot_count, BLK)[:, entry_slot]
-        .reshape(channels, entry_count * BLK)
-        .astype(jnp.float32)
-    )
+    rows = sent.shape[0]
+    slot_hot = (jnp.arange(slot_count, dtype=jnp.int32)[:, None] == entry_slot[None, :]).astype(
+        jnp.bfloat16
+    )
+    picked = jnp.einsum(
+        "rsb,se->reb",
+        sent.reshape(rows, slot_count, BLK),
+        slot_hot,
+        preferred_element_type=jnp.float32,
+    ).reshape(rows, entry_count * BLK)
+    projected = picked[:6]
+    colours = picked[6:]
     cotangent = pix_grad.reshape(channels, TPD, -1).astype(jnp.float32)
     picture, grad_proj, grad_colour = tile_grads(projected, colours, cotangent)
-    back_proj = (
-        jnp.zeros((6, slot_count, BLK), jnp.bfloat16)
-        .at[:, entry_slot]
-        .set(grad_proj.reshape(6, entry_count, BLK).astype(jnp.bfloat16))
-    )
-    back_colour = (
-        jnp.zeros((channels, slot_count, BLK), jnp.bfloat16)
-        .at[:, entry_slot]
-        .set(grad_colour.reshape(channels, entry_count, BLK).astype(jnp.bfloat16))
-    )
+    entry_grads = jnp.concatenate([grad_proj, grad_colour], axis=0).astype(jnp.bfloat16)
+    back = jnp.einsum(
+        "reb,se->rsb",
+        entry_grads.reshape(rows, entry_count, BLK),
+        slot_hot,
+        preferred_element_type=jnp.float32,
+    ).astype(jnp.bfloat16)
     returned = lax.all_to_all(
-        jnp.concatenate([back_proj.reshape(6, -1), back_colour.reshape(channels, -1)], axis=0),
+        back.reshape(rows, -1),
         "tiles",
         split_axis=1,
         concat_axis=1,

time: 158 us -> 148 us (0.937)
  local copies, waits for them, and re-layouts: 36.8 us -> 27.5 us
  other arithmetic: 19.8 us -> 18 us
    scatter x2 -> x0, local copies, waits for them, and re-layouts: 6.76 us -> none  [the longest x1 3.38 us: local(): back_proj = jnp.zeros((6, slot_count, BLK), jnp.bfloat16).at[:, entry_slo...]
    unnamed x20 -> x39, local copies, waits for them, and re-layouts: 3.57 us -> 3.63 us
  transfers between devices with their start and end apart: 5 -> 5, of which waited for: 5 -> 5; matrix products, arithmetic and copies ran while one was open for 6% -> 7% of each run, Pallas kernels for 0% -> 0%
where the time goes in v3:
time: 148 us; the launch traced here: 146 us
  waiting for transfers between devices  46.3 us (31%)
  starting transfers between devices  45.6 us (31%)
  local copies, waits for them, and re-layouts  27.5 us (19%)
  other arithmetic  18 us (12%)
  matrix products  5.92 us (4%)
  between operations  2.89 us (2%)
    all_to_all x1, starting transfers between devices, local(): lax.all_to_all(request, 'tiles', split_axis=0, concat_axis=0, tiled=True)  19.4 us
    all_to_all x1, waiting for transfers between devices, local(): lax.all_to_all(back.reshape(rows, -1), 'tiles', split_axis=1, concat_axis...  11.4 us
    all_to_all x1, waiting for transfers between devices, local(): lax.all_to_all(jnp.concatenate([send_proj, raw_colours.astype(jnp.bfloat1...  10.6 us
    all_to_all x1, waiting for transfers between devices, local(): lax.all_to_all(column_all.reshape(rows, cams, -1), 'cams', 1, 1, tiled=True)  8.66 us
    all_to_all x1, waiting for transfers between devices, local(): lax.all_to_all(jnp.broadcast_to(params[None], (cams,) + params.shape), 'c...  8.23 us
    all_to_all x1, starting transfers between devices, local(): lax.all_to_all(jnp.concatenate([send_proj, raw_colours.astype(jnp.bfloat1...  7.88 us
    all_to_all x1, starting transfers between devices, local(): lax.all_to_all(back.reshape(rows, -1), 'tiles', split_axis=1, concat_axis...  7.88 us
    all_to_all x1, waiting for transfers between devices, local(): lax.all_to_all(request, 'tiles', split_axis=0, concat_axis=0, tiled=True)  7.42 us
  transfers between devices with their start and end apart: 5, of which 5 were waited for; matrix products, arithmetic and copies ran while one was open for 7% of the time, Pallas kernels for 0%

profile of v3, /device:TPU:6, one launch (start us, length us, event | category | flops | bytes accessed | tf_op | source)
XLA Modules:
  0.0 146.3 jit_solution(17447560577640630077)
XLA Ops:
  3.7 19.4 %all-to-all-start.1 = ((s32[96,2,1]{1,2,0:T(1,128)}), s32[96,2,1]{1,2,0:T(1,128)S(1)}, u32[]{:S(2)}, u32[]{:S(2)}) async-start(s32[96,2,1]{1,2,0:T(1,128)} %bitcast.7), calls=%async_computation.1 | async-start | bytes 98304 | tf_op jit(solution)/shard_map/all_to_all | solution.py:113
  23.1 1.5 %fusion.69 = (f32[1,1]{1,0:T(1,128)}, f32[1,1]{1,0:T(1,128)}, f32[1,1]{1,0:T(1,128)}, f32[1,1]{1,0:T(1,128)}) fusion(f32[1,4]{1,0:T(1,128)} %param.14), kind=kLoop, calls=%fused_computation.163 | loop fusion | bytes 32 | tf_op jit(solution)/shard_map/slice | solution.py:15
  24.6 1.6 %concatenate.27 = f32[25,256]{1,0:T(8,128)S(1)} concatenate(f32[2,256]{1,0:T(2,128)} %param.9, f32[2,256]{1,0:T(2,128)} %param.10, f32[1,256]{1,0:T(1,128)} %bitcast.115, f32[1,256]{1,0:T(1,128)} %bitcast.116, f32[19,256]{1,0:T(8,128)} %param.13), dimensions={0} | concatenate | bytes 51200 | tf_op jit(solution)/shard_map/concatenate | solution.py:97
  26.1 7.4 %all-to-all-done.1 = s32[96,2,1]{1,2,0:T(1,128)S(1)} async-done(((s32[96,2,1]{1,2,0:T(1,128)}), s32[96,2,1]{1,2,0:T(1,128)S(1)}, u32[]{:S(2)}, u32[]{:S(2)}) %all-to-all-start.1) | async-done | bytes 800 | tf_op jit(solution)/shard_map/all_to_all | solution.py:113
  34.3 7.1 %all-to-all-start = ((f32[8,25,256]{2,1,0:T(8,128)}), f32[8,25,256]{2,1,0:T(8,128)S(1)}, u32[]{:S(2)}, u32[]{:S(2)}) async-start(f32[8,25,256]{2,1,0:T(8,128)} %broadcast_in_dim.14), calls=%async_computation | async-start | bytes 524288 | tf_op jit(solution)/shard_map/all_to_all | solution.py:99
  44.8 8.2 %all-to-all-done = f32[8,25,256]{2,1,0:T(8,128)S(1)} async-done(((f32[8,25,256]{2,1,0:T(8,128)}), f32[8,25,256]{2,1,0:T(8,128)S(1)}, u32[]{:S(2)}, u32[]{:S(2)}) %all-to-all-start) | async-done | bytes 204832 | tf_op jit(solution)/shard_map/all_to_all | solution.py:99
  56.2 1.2 slice_add_fusion
  57.4 2.4 %add_convert_fusion.1 = (bf16[1,192,8]{1,2,0:T(8,128)(2,1)S(1)}, bf16[1,192,8]{1,2,0:T(8,128)(2,1)S(1)}) fusion(f32[6,192,8]{1,2,0:T(8,128)S(1)} %bitcast.109, f32[]{:T(128)} %bitcast.14, f32[]{:T(128)} %bitcast.13, f32[]{:T(128)} %bitcast.12, f32[]{:T(128)} %bitcast.11, f32[]{:T(128)} %bitcast.10, f32[]{:T(128)} %bitcast.1), kind=kLoop, calls=%fused_computation.110 | loop fusion | flops 15360 | bytes 18456 | tf_op jit(solution)/shard_map/convert.11
  63.4 1.2 concatenate.28
  64.6 1.0 reshape.1004
  65.7 7.9 %all-to-all-start.2 = ((bf16[96,2,200]{2,1,0:T(2,128)(2,1)}), bf16[96,2,200]{2,1,0:T(2,128)(2,1)S(1)}, u32[]{:S(2)}, u32[]{:S(2)}) async-start(bf16[96,2,200]{2,1,0:T(2,128)(2,1)} %reshape.1004), calls=%async_computation.2 | async-start | bytes 196608 | tf_op jit(solution)/shard_map/all_to_all | solution.py:119
  75.0 10.6 %all-to-all-done.2 = bf16[96,2,200]{2,1,0:T(2,128)(2,1)S(1)} async-done(((bf16[96,2,200]{2,1,0:T(2,128)(2,1)}), bf16[96,2,200]{2,1,0:T(2,128)(2,1)S(1)}, u32[]{:S(2)}, u32[]{:S(2)}) %all-to-all-start.2) | async-done | bytes 76832 | tf_op jit(solution)/shard_map/all_to_all | solution.py:119
  88.7 1.8 %fusion.1 = bf16[19,16,48]{2,0,1:T(8,128)(2,1)S(1)} fusion(f32[16,48]{1,0:T(8,128)S(1)} %mul.1406, f32[16,48]{1,0:T(8,128)S(1)} %sub.116, f32[256]{0:T(256)S(1)} %get-tuple-element.82, f32[16,48]{1,0:T(8,128)S(1)} %mul.1402, f32[16,48]{1,0:T(8,128)S(1)} %sub.110, f32[256]{0:T(256)S(1)} %get-tuple-element.83, f32[16,48]{1,0:T(8,128)S(1)} %mul.1397, ...), kind=kOutput, calls=%fused_computation.19 | convolution fusion | flops 47790336 | bytes 991744 | tf_op jit(solution)/shard_map/transpose(jvp(vmap()))/dot_general | solution.py:53
  91.0 1.3 multiply_multiply_fusion.1
  93.3 2.9 %fusion.15 = (f32[16,48]{1,0:T(8,128)S(1)}, f32[16,48]{1,0:T(8,128)S(1)}, f32[16,48]{1,0:T(8,128)S(1)}, f32[16,48]{1,0:T(8,128)S(1)}, f32[16,48]{1,0:T(8,128)S(1)}, /*index=5*/f32[16,48]{1,0:T(8,128)S(1)}) fusion(f32[16,48]{1,0:T(8,128)S(1)} %sub.116, f32[256]{0:T(256)S(1)} %get-tuple-element.82, f32[16,48]{1,0:T(8,128)S(1)} %mul.1406, ...), kind=kLoop, calls=%fused_computation.35 | loop fusion | flops 9432576 | bytes 2398208 | tf_op jit(solution)/shard_map/transpose(jvp(vmap()))/reduce_sum | solution.py:48
  97.1 1.0 reshape.1006
  98.2 7.9 %all-to-all-start.3 = ((bf16[96,2,200]{2,1,0:T(2,128)(2,1)}), bf16[96,2,200]{2,1,0:T(2,128)(2,1)S(1)}, u32[]{:S(2)}, u32[]{:S(2)}) async-start(bf16[96,2,200]{2,1,0:T(2,128)(2,1)} %reshape.1006), calls=%async_computation.3 | async-start | bytes 196608 | tf_op jit(solution)/shard_map/all_to_all | solution.py:147
  106.6 11.4 %all-to-all-done.3 = bf16[96,2,200]{2,1,0:T(2,128)(2,1)S(1)} async-done(((bf16[96,2,200]{2,1,0:T(2,128)(2,1)}), bf16[96,2,200]{2,1,0:T(2,128)(2,1)S(1)}, u32[]{:S(2)}, u32[]{:S(2)}) %all-to-all-start.3) | async-done | bytes 76832 | tf_op jit(solution)/shard_map/all_to_all | solution.py:147
  118.6 3.9 %fusion.18 = (f32[96,16]{1,0:T(8,128)S(1)}, f32[96,16]{1,0:T(8,128)S(1)}, f32[96,16]{1,0:T(8,128)S(1)}, f32[96,16]{1,0:T(8,128)S(1)}, f32[96,16]{1,0:T(8,128)S(1...) fusion(f32[6,96,16]{0,2,1:T(8,128)S(1)} %slice_convert_fusion, f32[]{:T(128)} %bitcast.12, ...), kind=kLoop, calls=%fused_computation.42 | loop fusion | flops 7680 | bytes 86032 | tf_op jit(solution)/shard_map/transpose(jvp())/mul | solution.py:33
  123.2 1.3 negate_add_fusion
  124.5 1.3 multiply_add_fusion.4
  130.0 3.4 %all-to-all-start.4 = ((f32[25,8,256]{2,0,1:T(8,128)}), f32[25,8,256]{2,0,1:T(8,128)S(1)}, u32[]{:S(2)}, u32[]{:S(2)}) async-start(f32[25,8,256]{2,0,1:T(8,128)} %copy.288), calls=%async_computation.4 | async-start | bytes 524288 | tf_op jit(solution)/shard_map/all_to_all | solution.py:175
  133.5 1.7 %convolution_bitcast_fusion = f32[19,16,256]{2,0,1:T(8,128)S(1)} fusion(f32[19,16,48]{0,2,1:T(8,128)S(1)} %bitcast.107, f32[16,48]{1,0:T(8,128)S(1)} %mul.1406, f32[16,48]{1,0:T(8,128)S(1)} %copy-done.4, f32[256]{0:T(256)S(1)} %copy-done.12, f32[16,48]{1,0:T(8,128)S(1)} %copy-done.6, f32[16,48]{1,0:T(8,128)S(1)} %copy-done.8, f32[256]{0:T(256)S(1)} %copy-done.14, ...), kind=kOutput, calls=%fused_computation.14 | convolution fusion | flops 47775744 | bytes 1176576 | tf_op jit(solution)/shard_map/jvp(vmap())/dot_general | solution.py:53
  136.4 8.7 %all-to-all-done.4 = f32[25,8,256]{2,0,1:T(8,128)S(1)} async-done(((f32[25,8,256]{2,0,1:T(8,128)}), f32[25,8,256]{2,0,1:T(8,128)S(1)}, u32[]{:S(2)}, u32[]{:S(2)}) %all-to-all-start.4) | async-done | bytes 204832 | tf_op jit(solution)/shard_map/all_to_all | solution.py:175
  (157 shorter events, 27.4 us)
Async XLA Ops:
  0.6 40.8 %copy-start.15 = (f32[1,2]{1,0:T(1,128)S(1)}, f32[1,2]{1,0:T(1,128)}, u32[]{:S(2)}) copy-start(f32[1,2]{1,0:T(1,128)} %param.15) | copy-start | bytes 28
  3.7 29.8 %all-to-all-start.1 = ((s32[96,2,1]{1,2,0:T(1,128)}), s32[96,2,1]{1,2,0:T(1,128)S(1)}, u32[]{:S(2)}, u32[]{:S(2)}) async-start(s32[96,2,1]{1,2,0:T(1,128)} %bitcast.7), calls=%async_computation.1 | async-start | bytes 98304 | tf_op jit(solution)/shard_map/all_to_all | solution.py:113
  34.3 18.7 %all-to-all-start = ((f32[8,25,256]{2,1,0:T(8,128)}), f32[8,25,256]{2,1,0:T(8,128)S(1)}, u32[]{:S(2)}, u32[]{:S(2)}) async-start(f32[8,25,256]{2,1,0:T(8,128)} %broadcast_in_dim.14), calls=%async_computation | async-start | bytes 524288 | tf_op jit(solution)/shard_map/all_to_all | solution.py:99
  63.4 10.2 %copy-start.2 = (bf16[19,1,4096]{2,0,1:T(8,128)(2,1)S(1)}, bf16[19,1,4096]{2,0,1:T(8,128)(2,1)}, u32[]{:S(2)}) copy-start(bf16[19,1,4096]{2,0,1:T(8,128)(2,1)} %param.17) | copy-start | bytes 466948
  65.7 19.9 %all-to-all-start.2 = ((bf16[96,2,200]{2,1,0:T(2,128)(2,1)}), bf16[96,2,200]{2,1,0:T(2,128)(2,1)S(1)}, u32[]{:S(2)}, u32[]{:S(2)}) async-start(bf16[96,2,200]{2,1,0:T(2,128)(2,1)} %reshape.1004), calls=%async_computation.2 | async-start | bytes 196608 | tf_op jit(solution)/shard_map/all_to_all | solution.py:119
  73.6 19.7 %copy-start.11 = (f32[256]{0:T(256)}, f32[256]{0:T(256)S(1)}, u32[]{:S(2)}) copy-start(f32[256]{0:T(256)S(1)} %get-tuple-element.82) | copy-start | bytes 3076
  73.6 19.7 %copy-start.13 = (f32[256]{0:T(256)}, f32[256]{0:T(256)S(1)}, u32[]{:S(2)}) copy-start(f32[256]{0:T(256)S(1)} %get-tuple-element.83) | copy-start | bytes 3076
  86.7 6.5 %copy-start.3 = (f32[16,48]{1,0:T(8,128)}, f32[16,48]{1,0:T(8,128)S(1)}, u32[]{:S(2)}) copy-start(f32[16,48]{1,0:T(8,128)S(1)} %sub.116) | copy-start | bytes 9220
  86.9 6.4 %copy-start.5 = (f32[16,48]{1,0:T(8,128)}, f32[16,48]{1,0:T(8,128)S(1)}, u32[]{:S(2)}) copy-start(f32[16,48]{1,0:T(8,128)S(1)} %mul.1402) | copy-start | bytes 9220
  87.1 6.2 %copy-start.7 = (f32[16,48]{1,0:T(8,128)}, f32[16,48]{1,0:T(8,128)S(1)}, u32[]{:S(2)}) copy-start(f32[16,48]{1,0:T(8,128)S(1)} %sub.110) | copy-start | bytes 9220
  87.3 6.0 %copy-start.9 = (f32[16,48]{1,0:T(8,128)}, f32[16,48]{1,0:T(8,128)S(1)}, u32[]{:S(2)}) copy-start(f32[16,48]{1,0:T(8,128)S(1)} %mul.1397) | copy-start | bytes 9220
  88.7 4.6 %copy-start = (f32[16,48,256]{2,0,1:T(8,128)}, f32[16,48,256]{2,0,1:T(8,128)S(1)}, u32[]{:S(2)}) copy-start(f32[16,48,256]{2,0,1:T(8,128)S(1)} %fusion.25) | copy-start | bytes 2359300
  98.2 19.9 %all-to-all-start.3 = ((bf16[96,2,200]{2,1,0:T(2,128)(2,1)}), bf16[96,2,200]{2,1,0:T(2,128)(2,1)S(1)}, u32[]{:S(2)}, u32[]{:S(2)}) async-start(bf16[96,2,200]{2,1,0:T(2,128)(2,1)} %reshape.1006), calls=%async_computation.3 | async-start | bytes 196608 | tf_op jit(solution)/shard_map/all_to_all | solution.py:147
  128.9 4.5 %copy-start.1 = (f32[16,48,256]{2,0,1:T(8,128)S(1)}, f32[16,48,256]{2,0,1:T(8,128)}, u32[]{:S(2)}) copy-start(f32[16,48,256]{2,0,1:T(8,128)} %copy-done) | copy-start | bytes 2359300
  128.9 4.5 %copy-start.4 = (f32[16,48]{1,0:T(8,128)S(1)}, f32[16,48]{1,0:T(8,128)}, u32[]{:S(2)}) copy-start(f32[16,48]{1,0:T(8,128)} %copy-done.3) | copy-start | bytes 9220
  128.9 4.5 %copy-start.6 = (f32[16,48]{1,0:T(8,128)S(1)}, f32[16,48]{1,0:T(8,128)}, u32[]{:S(2)}) copy-start(f32[16,48]{1,0:T(8,128)} %copy-done.5) | copy-start | bytes 9220
  128.9 4.5 %copy-start.8 = (f32[16,48]{1,0:T(8,128)S(1)}, f32[16,48]{1,0:T(8,128)}, u32[]{:S(2)}) copy-start(f32[16,48]{1,0:T(8,128)} %copy-done.7) | copy-start | bytes 9220
  128.9 4.5 %copy-start.10 = (f32[16,48]{1,0:T(8,128)S(1)}, f32[16,48]{1,0:T(8,128)}, u32[]{:S(2)}) copy-start(f32[16,48]{1,0:T(8,128)} %copy-done.9) | copy-start | bytes 9220
  128.9 4.5 %copy-start.12 = (f32[256]{0:T(256)S(1)}, f32[256]{0:T(256)}, u32[]{:S(2)}) copy-start(f32[256]{0:T(256)} %copy-done.11) | copy-start | bytes 3076
  129.0 4.5 %copy-start.14 = (f32[256]{0:T(256)S(1)}, f32[256]{0:T(256)}, u32[]{:S(2)}) copy-start(f32[256]{0:T(256)} %copy-done.13) | copy-start | bytes 3076
  130.0 15.0 %all-to-all-start.4 = ((f32[25,8,256]{2,0,1:T(8,128)}), f32[25,8,256]{2,0,1:T(8,128)S(1)}, u32[]{:S(2)}, u32[]{:S(2)}) async-start(f32[25,8,256]{2,0,1:T(8,128)} %copy.288), calls=%async_computation.4 | async-start | bytes 524288 | tf_op jit(solution)/shard_map/all_to_all | solution.py:175

commit v4 on v3

--- a/solution.py
+++ b/solution.py
@@ -111,27 +111,25 @@
     entry_slot = column * capacity + ranking
     request = jnp.zeros((slot_count,), jnp.int32).at[entry_slot].set(in_column)
     wanted = lax.all_to_all(request, "tiles", split_axis=0, concat_axis=0, tiled=True)
-    raw_params = geometry_col.reshape(6, per_column, BLK)[:, wanted].reshape(6, slot_count * BLK)
-    raw_colours = appearance_col.reshape(channels, per_column, BLK)[:, wanted].reshape(
-        channels, slot_count * BLK
+    rows = params_col.shape[0]
+    payload_col = jnp.concatenate(
+        [project(geometry_col, linear, camera_shift), appearance_col], axis=0
+    ).astype(jnp.bfloat16)
+    owner_hot = (jnp.arange(per_column, dtype=jnp.int32)[:, None] == wanted[None, :]).astype(
+        jnp.bfloat16
     )
-    send_proj = project(raw_params, linear, camera_shift).astype(jnp.bfloat16)
-    sent = lax.all_to_all(
-        jnp.concatenate([send_proj, raw_colours.astype(jnp.bfloat16)], axis=0),
-        "tiles",
-        split_axis=1,
-        concat_axis=1,
-        tiled=True,
-    )
-    rows = sent.shape[0]
+    send = jnp.einsum(
+        "rkb,ks->rbs",
+        payload_col.reshape(rows, per_column, BLK),
+        owner_hot,
+        preferred_element_type=jnp.float32,
+    ).astype(jnp.bfloat16)
+    sent = lax.all_to_all(send, "tiles", split_axis=2, concat_axis=2, tiled=True)
     slot_hot = (jnp.arange(slot_count, dtype=jnp.int32)[:, None] == entry_slot[None, :]).astype(
         jnp.bfloat16
     )
     picked = jnp.einsum(
-        "rsb,se->reb",
-        sent.reshape(rows, slot_count, BLK),
-        slot_hot,
-        preferred_element_type=jnp.float32,
+        "rbs,se->reb", sent, slot_hot, preferred_element_type=jnp.float32
     ).reshape(rows, entry_count * BLK)
     projected = picked[:6]
     colours = picked[6:]
@@ -139,39 +137,21 @@
     picture, grad_proj, grad_colour = tile_grads(projected, colours, cotangent)
     entry_grads = jnp.concatenate([grad_proj, grad_colour], axis=0).astype(jnp.bfloat16)
     back = jnp.einsum(
-        "reb,se->rsb",
+        "reb,se->rbs",
         entry_grads.reshape(rows, entry_count, BLK),
         slot_hot,
         preferred_element_type=jnp.float32,
     ).astype(jnp.bfloat16)
-    returned = lax.all_to_all(
-        back.reshape(rows, -1),
-        "tiles",
-        split_axis=1,
-        concat_axis=1,
-        tiled=True,
+    returned = lax.all_to_all(back, "tiles", split_axis=2, concat_axis=2, tiled=True)
+    summed = jnp.einsum(
+        "rbs,ks->rkb", returned, owner_hot, preferred_element_type=jnp.float32
+    ).reshape(rows, per_column * BLK)
+    unused, pull_params = jax.vjp(
+        lambda params: project(params, linear, camera_shift), geometry_col
     )
-    ret_proj = returned[:6]
-    ret_colour = returned[6:]
-    unused, pull_params = jax.vjp(lambda params: project(params, linear, camera_shift), raw_params)
-    grad_raw = pull_params(ret_proj.astype(jnp.float32))[0]
-    owner_hot = (wanted[:, None] == jnp.arange(per_column, dtype=jnp.int32)[None, :]).astype(
-        jnp.float32
-    )
-
-    def collect(values, row_count):
-        summed = jnp.einsum(
-            "rsb,sk->rkb",
-            values.reshape(row_count, slot_count, BLK),
-            owner_hot,
-            precision=lax.Precision.HIGHEST,
-        )
-        return summed.reshape(row_count, per_column * BLK)
-
-    column_geometry = collect(grad_raw, 6)
-    column_colour = collect(ret_colour.astype(jnp.float32), channels)
+    column_geometry = pull_params(summed[:6])[0]
+    column_colour = summed[6:]
     column_all = jnp.concatenate([column_geometry, column_colour], axis=0)
-    rows = column_all.shape[0]
     grads = lax.all_to_all(
         column_all.reshape(rows, cams, -1), "cams", 1, 1, tiled=True
     ).sum(axis=1)

time: 148 us -> 142 us (0.959)
  local copies, waits for them, and re-layouts: 27.5 us -> 20.4 us
  waiting for transfers between devices: 46.3 us -> 48.8 us
  other arithmetic: 18 us -> 16.1 us
    mul x2, other arithmetic: 3.91 us -> 1.31 us  [project(): opacity = 0.95 * jax.nn.sigmoid(geometry[5])]
    all_to_all x1, waiting for transfers between devices: 7.42 us -> 9.6 us  [local(): lax.all_to_all(request, 'tiles', split_axis=0, concat_axis=0, tiled=True)]
    gather x3 -> x0, local copies, waits for them, and re-layouts: 1.91 us -> none  [the longest x2 1.16 us: local(): geometry_col.reshape(6, per_column, BLK)[:, wanted]]
    another operation x7 -> x5, local copies, waits for them, and re-layouts: 1.81 us -> 0.23 us
    reshape x4 -> x0, local copies, waits for them, and re-layouts: 1.49 us -> none  [the longest x2 0.92 us: local(): geometry_col.reshape(6, per_column, BLK)[:, wanted]]
    unnamed x39 -> x55, local copies, waits for them, and re-layouts: 3.63 us -> 4.31 us
  transfers between devices with their start and end apart: 5 -> 5, of which waited for: 5 -> 5; matrix products, arithmetic and copies ran while one was open for 7% -> 5% of each run, Pallas kernels for 0% -> 0%
where the time goes in v4:
time: 142 us; the launch traced here: 140 us
  waiting for transfers between devices  48.8 us (34%)
  starting transfers between devices  46.2 us (33%)
  local copies, waits for them, and re-layouts  20.4 us (14%)
  other arithmetic  16.1 us (11%)
  matrix products  5.86 us (4%)
  between operations  2.84 us (2%)
    all_to_all x1, starting transfers between devices, local(): lax.all_to_all(request, 'tiles', split_axis=0, concat_axis=0, tiled=True)  19.5 us
    all_to_all x1, waiting for transfers between devices, local(): lax.all_to_all(send, 'tiles', split_axis=2, concat_axis=2, tiled=True)  11.8 us
    all_to_all x1, waiting for transfers between devices, local(): lax.all_to_all(back, 'tiles', split_axis=2, concat_axis=2, tiled=True)  11.3 us
    all_to_all x1, waiting for transfers between devices, local(): lax.all_to_all(request, 'tiles', split_axis=0, concat_axis=0, tiled=True)  9.6 us
    all_to_all x1, waiting for transfers between devices, local(): lax.all_to_all(column_all.reshape(rows, cams, -1), 'cams', 1, 1, tiled=True)  8.66 us
    all_to_all x1, starting transfers between devices, local(): lax.all_to_all(send, 'tiles', split_axis=2, concat_axis=2, tiled=True)  8.01 us
    all_to_all x1, starting transfers between devices, local(): lax.all_to_all(back, 'tiles', split_axis=2, concat_axis=2, tiled=True)  7.87 us
    all_to_all x1, waiting for transfers between devices, local(): lax.all_to_all(jnp.broadcast_to(params[None], (cams,) + params.shape), 'c...  7.5 us
  transfers between devices with their start and end apart: 5, of which 5 were waited for; matrix products, arithmetic and copies ran while one was open for 5% of the time, Pallas kernels for 0%

profile of v4, /device:TPU:6, one launch (start us, length us, event | category | flops | bytes accessed | tf_op | source)
XLA Modules:
  0.0 140.2 jit_solution(863531274051215451)
XLA Ops:
  3.7 19.5 %all-to-all-start.1 = ((s32[96,2,1]{1,2,0:T(1,128)}), s32[96,2,1]{1,2,0:T(1,128)S(1)}, u32[]{:S(2)}, u32[]{:S(2)}) async-start(s32[96,2,1]{1,2,0:T(1,128)} %bitcast.13), calls=%async_computation.1 | async-start | bytes 98304 | tf_op jit(solution)/shard_map/all_to_all | solution.py:113
  24.1 9.6 %all-to-all-done.1 = s32[96,2,1]{1,2,0:T(1,128)S(1)} async-done(((s32[96,2,1]{1,2,0:T(1,128)}), s32[96,2,1]{1,2,0:T(1,128)S(1)}, u32[]{:S(2)}, u32[]{:S(2)}) %all-to-all-start.1) | async-done | bytes 800 | tf_op jit(solution)/shard_map/all_to_all | solution.py:113
  34.4 7.2 %all-to-all-start = ((f32[8,25,256]{2,1,0:T(8,128)}), f32[8,25,256]{2,1,0:T(8,128)S(1)}, u32[]{:S(2)}, u32[]{:S(2)}) async-start(f32[8,25,256]{2,1,0:T(8,128)} %broadcast_in_dim.16), calls=%async_computation | async-start | bytes 524288 | tf_op jit(solution)/shard_map/all_to_all | solution.py:99
  45.8 7.5 %all-to-all-done = f32[8,25,256]{2,1,0:T(8,128)S(1)} async-done(((f32[8,25,256]{2,1,0:T(8,128)}), f32[8,25,256]{2,1,0:T(8,128)S(1)}, u32[]{:S(2)}, u32[]{:S(2)}) %all-to-all-start) | async-done | bytes 204832 | tf_op jit(solution)/shard_map/all_to_all | solution.py:99
  53.4 1.3 fusion.51
  54.7 2.6 %add_convert_fusion.1 = (bf16[1,8,256]{2,1,0:T(8,128)(2,1)S(1)}, bf16[1,8,256]{2,1,0:T(8,128)(2,1)S(1)}) fusion(f32[25,8,256]{2,1,0:T(8,128)S(1)} %bitcast.96, f32[]{:T(128)} %bitcast.9, f32[]{:T(128)} %bitcast.8, f32[]{:T(128)} %bitcast.7, f32[]{:T(128)} %bitcast.6, f32[]{:T(128)} %bitcast.5, f32[]{:T(128)} %bitcast.1), kind=kLoop, calls=%fused_computation.115 | loop fusion | flops 20480 | bytes 24600 | tf_op jit(solution)/shard_map/convert.14
  60.3 1.0 reshape.1198
  61.3 8.0 %all-to-all-start.2 = ((bf16[96,2,200]{2,1,0:T(2,128)(2,1)}), bf16[96,2,200]{2,1,0:T(2,128)(2,1)S(1)}, u32[]{:S(2)}, u32[]{:S(2)}) async-start(bf16[96,2,200]{2,1,0:T(2,128)(2,1)} %reshape.1198), calls=%async_computation.2 | async-start | bytes 196608 | tf_op jit(solution)/shard_map/all_to_all | solution.py:127
  69.5 11.8 %all-to-all-done.2 = bf16[96,2,200]{2,1,0:T(2,128)(2,1)S(1)} async-done(((bf16[96,2,200]{2,1,0:T(2,128)(2,1)}), bf16[96,2,200]{2,1,0:T(2,128)(2,1)S(1)}, u32[]{:S(2)}, u32[]{:S(2)}) %all-to-all-start.2) | async-done | bytes 76832 | tf_op jit(solution)/shard_map/all_to_all | solution.py:127
  84.5 1.8 %fusion = bf16[19,16,48]{2,0,1:T(8,128)(2,1)S(1)} fusion(f32[16,48]{1,0:T(8,128)S(1)} %mul.1655, f32[16,48]{1,0:T(8,128)S(1)} %sub.119, f32[256]{0:T(256)S(1)} %get-tuple-element.77, f32[16,48]{1,0:T(8,128)S(1)} %mul.1651, f32[16,48]{1,0:T(8,128)S(1)} %sub.113, f32[256]{0:T(256)S(1)} %get-tuple-element.78, f32[16,48]{1,0:T(8,128)S(1)} %mul.1646, ...), kind=kOutput, calls=%fused_computation.17 | convolution fusion | flops 47790336 | bytes 991744 | tf_op jit(solution)/shard_map/transpose(jvp(vmap()))/dot_general | solution.py:53
  86.7 1.3 multiply_multiply_fusion.1
  88.1 0.9 fusion.20
  89.1 2.9 %fusion.14 = (f32[16,48]{1,0:T(8,128)S(1)}, f32[16,48]{1,0:T(8,128)S(1)}, f32[16,48]{1,0:T(8,128)S(1)}, f32[16,48]{1,0:T(8,128)S(1)}, f32[16,48]{1,0:T(8,128)S(1)}, /*index=5*/f32[16,48]{1,0:T(8,128)S(1)}) fusion(f32[16,48]{1,0:T(8,128)S(1)} %sub.119, f32[256]{0:T(256)S(1)} %get-tuple-element.77, f32[16,48]{1,0:T(8,128)S(1)} %mul.1655, ...), kind=kLoop, calls=%fused_computation.32 | loop fusion | flops 9432576 | bytes 2398208 | tf_op jit(solution)/shard_map/transpose(jvp(vmap()))/reduce_sum | solution.py:48
  92.8 1.0 reshape.1200
  93.9 7.9 %all-to-all-start.3 = ((bf16[96,2,200]{2,1,0:T(2,128)(2,1)}), bf16[96,2,200]{2,1,0:T(2,128)(2,1)S(1)}, u32[]{:S(2)}, u32[]{:S(2)}) async-start(bf16[96,2,200]{2,1,0:T(2,128)(2,1)} %reshape.1200), calls=%async_computation.3 | async-start | bytes 196608 | tf_op jit(solution)/shard_map/all_to_all | solution.py:145
  102.4 11.3 %all-to-all-done.3 = bf16[96,2,200]{2,1,0:T(2,128)(2,1)S(1)} async-done(((bf16[96,2,200]{2,1,0:T(2,128)(2,1)}), bf16[96,2,200]{2,1,0:T(2,128)(2,1)S(1)}, u32[]{:S(2)}, u32[]{:S(2)}) %all-to-all-start.3) | async-done | bytes 76832 | tf_op jit(solution)/shard_map/all_to_all | solution.py:145
  114.7 1.3 slice_multiply_fusion
  118.4 1.4 negate_add_fusion
  119.8 1.4 multiply_add_fusion.1
  122.8 1.0 copy.252
  123.8 3.6 %all-to-all-start.4 = ((f32[25,8,256]{2,0,1:T(8,128)}), f32[25,8,256]{2,0,1:T(8,128)S(1)}, u32[]{:S(2)}, u32[]{:S(2)}) async-start(f32[25,8,256]{2,0,1:T(8,128)} %copy.252), calls=%async_computation.4 | async-start | bytes 524288 | tf_op jit(solution)/shard_map/all_to_all | solution.py:155
  127.5 1.7 %convolution_bitcast_fusion = f32[19,16,256]{2,0,1:T(8,128)S(1)} fusion(f32[19,16,48]{0,2,1:T(8,128)S(1)} %bitcast.100, f32[16,48]{1,0:T(8,128)S(1)} %mul.1655, f32[16,48]{1,0:T(8,128)S(1)} %sub.119, f32[256]{0:T(256)S(1)} %copy-done.13, f32[16,48]{1,0:T(8,128)S(1)} %copy-done.4, f32[16,48]{1,0:T(8,128)S(1)} %copy-done.6, f32[256]{0:T(256)S(1)} %copy-done.15, ...), kind=kOutput, calls=%fused_computation.12 | convolution fusion | flops 47775744 | bytes 1176576 | tf_op jit(solution)/shard_map/jvp(vmap())/dot_general | solution.py:53
  129.3 1.0 reshape.1186
  130.3 8.7 %all-to-all-done.4 = f32[25,8,256]{2,0,1:T(8,128)S(1)} async-done(((f32[25,8,256]{2,0,1:T(8,128)}), f32[25,8,256]{2,0,1:T(8,128)S(1)}, u32[]{:S(2)}, u32[]{:S(2)}) %all-to-all-start.4) | async-done | bytes 204832 | tf_op jit(solution)/shard_map/all_to_all | solution.py:155
  (158 shorter events, 21.5 us)
Async XLA Ops:
  3.7 19.5 %copy-start.11 = (f32[19,256]{1,0:T(8,128)S(1)}, f32[19,256]{1,0:T(8,128)}, u32[]{:S(2)}) copy-start(f32[19,256]{1,0:T(8,128)} %param.13) | copy-start | bytes 58372
  3.7 19.6 %copy-start.18 = (f32[2,256]{1,0:T(2,128)S(1)}, f32[2,256]{1,0:T(2,128)}, u32[]{:S(2)}) copy-start(f32[2,256]{1,0:T(2,128)} %param.10) | copy-start | bytes 6148
  3.7 19.6 %copy-start.21 = (f32[256]{0:T(256)S(1)}, f32[256]{0:T(256)}, u32[]{:S(2)}) copy-start(f32[256]{0:T(256)} %param.12) | copy-start | bytes 3076
  3.7 30.0 %all-to-all-start.1 = ((s32[96,2,1]{1,2,0:T(1,128)}), s32[96,2,1]{1,2,0:T(1,128)S(1)}, u32[]{:S(2)}, u32[]{:S(2)}) async-start(s32[96,2,1]{1,2,0:T(1,128)} %bitcast.13), calls=%async_computation.1 | async-start | bytes 98304 | tf_op jit(solution)/shard_map/all_to_all | solution.py:113
  34.4 7.2 %copy-start.16 = (f32[1,4]{1,0:T(1,128)S(1)}, f32[1,4]{1,0:T(1,128)}, u32[]{:S(2)}) copy-start(f32[1,4]{1,0:T(1,128)} %param.14) | copy-start | bytes 52
  34.4 18.8 %all-to-all-start = ((f32[8,25,256]{2,1,0:T(8,128)}), f32[8,25,256]{2,1,0:T(8,128)S(1)}, u32[]{:S(2)}, u32[]{:S(2)}) async-start(f32[8,25,256]{2,1,0:T(8,128)} %broadcast_in_dim.16), calls=%async_computation | async-start | bytes 524288 | tf_op jit(solution)/shard_map/all_to_all | solution.py:99
  61.3 8.1 %copy-start.2 = (bf16[19,1,4096]{2,0,1:T(8,128)(2,1)S(1)}, bf16[19,1,4096]{2,0,1:T(8,128)(2,1)}, u32[]{:S(2)}) copy-start(bf16[19,1,4096]{2,0,1:T(8,128)(2,1)} %param.17) | copy-start | bytes 466948
  61.3 20.0 %all-to-all-start.2 = ((bf16[96,2,200]{2,1,0:T(2,128)(2,1)}), bf16[96,2,200]{2,1,0:T(2,128)(2,1)S(1)}, u32[]{:S(2)}, u32[]{:S(2)}) async-start(bf16[96,2,200]{2,1,0:T(2,128)(2,1)} %reshape.1198), calls=%async_computation.2 | async-start | bytes 196608 | tf_op jit(solution)/shard_map/all_to_all | solution.py:127
  69.3 19.7 %copy-start.12 = (f32[256]{0:T(256)}, f32[256]{0:T(256)S(1)}, u32[]{:S(2)}) copy-start(f32[256]{0:T(256)S(1)} %get-tuple-element.77) | copy-start | bytes 3076
  69.3 19.7 %copy-start.14 = (f32[256]{0:T(256)}, f32[256]{0:T(256)S(1)}, u32[]{:S(2)}) copy-start(f32[256]{0:T(256)S(1)} %get-tuple-element.78) | copy-start | bytes 3076
  82.7 6.3 %copy-start.3 = (f32[16,48]{1,0:T(8,128)}, f32[16,48]{1,0:T(8,128)S(1)}, u32[]{:S(2)}) copy-start(f32[16,48]{1,0:T(8,128)S(1)} %mul.1651) | copy-start | bytes 9220
  82.9 6.1 %copy-start.5 = (f32[16,48]{1,0:T(8,128)}, f32[16,48]{1,0:T(8,128)S(1)}, u32[]{:S(2)}) copy-start(f32[16,48]{1,0:T(8,128)S(1)} %sub.113) | copy-start | bytes 9220
  83.1 6.0 %copy-start.7 = (f32[16,48]{1,0:T(8,128)}, f32[16,48]{1,0:T(8,128)S(1)}, u32[]{:S(2)}) copy-start(f32[16,48]{1,0:T(8,128)S(1)} %mul.1646) | copy-start | bytes 9220
  83.2 5.8 %copy-start.9 = (f32[16,48]{1,0:T(8,128)}, f32[16,48]{1,0:T(8,128)S(1)}, u32[]{:S(2)}) copy-start(f32[16,48]{1,0:T(8,128)S(1)} %mul.1644) | copy-start | bytes 9220
  84.5 4.6 %copy-start = (f32[16,48,256]{2,0,1:T(8,128)}, f32[16,48,256]{2,0,1:T(8,128)S(1)}, u32[]{:S(2)}) copy-start(f32[16,48,256]{2,0,1:T(8,128)S(1)} %fusion.23) | copy-start | bytes 2359300
  93.9 19.9 %all-to-all-start.3 = ((bf16[96,2,200]{2,1,0:T(2,128)(2,1)}), bf16[96,2,200]{2,1,0:T(2,128)(2,1)S(1)}, u32[]{:S(2)}, u32[]{:S(2)}) async-start(bf16[96,2,200]{2,1,0:T(2,128)(2,1)} %reshape.1200), calls=%async_computation.3 | async-start | bytes 196608 | tf_op jit(solution)/shard_map/all_to_all | solution.py:145
  122.8 4.6 %copy-start.1 = (f32[16,48,256]{2,0,1:T(8,128)S(1)}, f32[16,48,256]{2,0,1:T(8,128)}, u32[]{:S(2)}) copy-start(f32[16,48,256]{2,0,1:T(8,128)} %copy-done) | copy-start | bytes 2359300
  123.8 3.6 %copy-start.4 = (f32[16,48]{1,0:T(8,128)S(1)}, f32[16,48]{1,0:T(8,128)}, u32[]{:S(2)}) copy-start(f32[16,48]{1,0:T(8,128)} %copy-done.3) | copy-start | bytes 9220
  123.8 3.6 %copy-start.6 = (f32[16,48]{1,0:T(8,128)S(1)}, f32[16,48]{1,0:T(8,128)}, u32[]{:S(2)}) copy-start(f32[16,48]{1,0:T(8,128)} %copy-done.5) | copy-start | bytes 9220
  123.8 3.6 %copy-start.8 = (f32[16,48]{1,0:T(8,128)S(1)}, f32[16,48]{1,0:T(8,128)}, u32[]{:S(2)}) copy-start(f32[16,48]{1,0:T(8,128)} %copy-done.7) | copy-start | bytes 9220
  123.8 3.6 %copy-start.10 = (f32[16,48]{1,0:T(8,128)S(1)}, f32[16,48]{1,0:T(8,128)}, u32[]{:S(2)}) copy-start(f32[16,48]{1,0:T(8,128)} %copy-done.9) | copy-start | bytes 9220
  123.8 3.6 %copy-start.13 = (f32[256]{0:T(256)S(1)}, f32[256]{0:T(256)}, u32[]{:S(2)}) copy-start(f32[256]{0:T(256)} %copy-done.12) | copy-start | bytes 3076
  123.8 3.6 %copy-start.15 = (f32[256]{0:T(256)S(1)}, f32[256]{0:T(256)}, u32[]{:S(2)}) copy-start(f32[256]{0:T(256)} %copy-done.14) | copy-start | bytes 3076
  123.8 15.2 %all-to-all-start.4 = ((f32[25,8,256]{2,0,1:T(8,128)}), f32[25,8,256]{2,0,1:T(8,128)S(1)}, u32[]{:S(2)}, u32[]{:S(2)}) async-start(f32[25,8,256]{2,0,1:T(8,128)} %copy.252), calls=%async_computation.4 | async-start | bytes 524288 | tf_op jit(solution)/shard_map/all_to_all | solution.py:155
  (3 other events, 2.0 us)

commit v5 on v4

--- a/solution.py
+++ b/solution.py
@@ -99,10 +99,11 @@
     gathered = lax.all_to_all(
         jnp.broadcast_to(params[None], (cams,) + params.shape), "cams", 0, 0, tiled=True
     )
-    params_col = gathered.transpose(1, 0, 2).reshape(params.shape[0], cams * params.shape[1])
+    params_col = gathered.transpose(1, 0, 2)
     geometry_col = params_col[:6]
     appearance_col = params_col[6:]
-    per_column = geometry_col.shape[1] // BLK
+    per_column = cams * params.shape[1] // BLK
+    local_blocks = params.shape[1] // BLK
     linear = cam_linear[0]
     camera_shift = cam_shift[0]
     entries = block_lists.reshape(-1)
@@ -110,6 +111,7 @@
     column, ranking, in_column = slot_ranks(entries, per_column, columns)
     entry_slot = column * capacity + ranking
     request = jnp.zeros((slot_count,), jnp.int32).at[entry_slot].set(in_column)
+    request, params_col = lax.optimization_barrier((request, params_col))
     wanted = lax.all_to_all(request, "tiles", split_axis=0, concat_axis=0, tiled=True)
     rows = params_col.shape[0]
     payload_col = jnp.concatenate(
@@ -119,9 +121,9 @@
         jnp.bfloat16
     )
     send = jnp.einsum(
-        "rkb,ks->rbs",
-        payload_col.reshape(rows, per_column, BLK),
-        owner_hot,
+        "rjlb,jls->rbs",
+        payload_col.reshape(rows, cams, local_blocks, BLK),
+        owner_hot.reshape(cams, local_blocks, slot_count),
         preferred_element_type=jnp.float32,
     ).astype(jnp.bfloat16)
     sent = lax.all_to_all(send, "tiles", split_axis=2, concat_axis=2, tiled=True)
@@ -144,17 +146,18 @@
     ).astype(jnp.bfloat16)
     returned = lax.all_to_all(back, "tiles", split_axis=2, concat_axis=2, tiled=True)
     summed = jnp.einsum(
-        "rbs,ks->rkb", returned, owner_hot, preferred_element_type=jnp.float32
-    ).reshape(rows, per_column * BLK)
+        "rbs,jls->rjlb",
+        returned,
+        owner_hot.reshape(cams, local_blocks, slot_count),
+        preferred_element_type=jnp.float32,
+    ).reshape(rows, cams, local_blocks * BLK)
     unused, pull_params = jax.vjp(
         lambda params: project(params, linear, camera_shift), geometry_col
     )
     column_geometry = pull_params(summed[:6])[0]
     column_colour = summed[6:]
     column_all = jnp.concatenate([column_geometry, column_colour], axis=0)
-    grads = lax.all_to_all(
-        column_all.reshape(rows, cams, -1), "cams", 1, 1, tiled=True
-    ).sum(axis=1)
+    grads = lax.all_to_all(column_all, "cams", 1, 1, tiled=True).sum(axis=1)
     grad_geometry = grads[:6]
     grad_appearance = grads[6:]
     return (picture.reshape(channels, 1, -1), grad_geometry, grad_appearance)

time: 142 us -> 136 us (0.958)
  blocking collectives: 0 us -> 19.2 us
  waiting for transfers between devices: 48.8 us -> 31.4 us
  starting transfers between devices: 46.2 us -> 39.2 us
  other arithmetic: 16.1 us -> 13.1 us
  local copies, waits for them, and re-layouts: 20.4 us -> 23.1 us
    all_to_all x0 -> x1, blocking collectives: none -> 19.2 us  [local(): lax.all_to_all(back, 'tiles', split_axis=2, concat_axis=2, tiled=True)]
    all_to_all x2 -> x1, waiting for transfers between devices: 20 us -> 8.69 us  [local(): grads = lax.all_to_all(column_all, 'cams', 1, 1, tiled=True).sum(axis=1)]
    all_to_all x2 -> x1, starting transfers between devices: 11.4 us -> 3.55 us  [local(): grads = lax.all_to_all(column_all, 'cams', 1, 1, tiled=True).sum(axis=1)]
    all_to_all x1, waiting for transfers between devices: 9.6 us -> 4.34 us  [local(): lax.all_to_all(request, 'tiles', split_axis=0, concat_axis=0, tiled=True)]
    concatenate x2 -> x14, local copies, waits for them, and re-layouts: 0.64 us -> 3.11 us  [local(): jnp.concatenate([project(geometry_col, linear, camera_shift), appearance_...]
    add_any x2 -> x0, other arithmetic: 2.09 us -> none  [the longest x1 1.39 us: project(): img_yy / determ]
    unnamed x55 -> x46, local copies, waits for them, and re-layouts: 4.31 us -> 4.13 us
  transfers between devices with their start and end apart: 5 -> 4, of which waited for: 5 -> 4; matrix products, arithmetic and copies ran while one was open for 5% -> 9% of each run, Pallas kernels for 0% -> 0%
where the time goes in v5:
time: 136 us; the launch traced here: 135 us
  starting transfers between devices  39.2 us (29%)
  waiting for transfers between devices  31.4 us (23%)
  local copies, waits for them, and re-layouts  23.1 us (17%)
  blocking collectives  19.2 us (14%)
  other arithmetic  13.1 us (10%)
  matrix products  6.04 us (4%)
  between operations  2.71 us (2%)
    all_to_all x1, starting transfers between devices, local(): lax.all_to_all(request, 'tiles', split_axis=0, concat_axis=0, tiled=True)  19.4 us
    all_to_all x1, blocking collectives, local(): lax.all_to_all(back, 'tiles', split_axis=2, concat_axis=2, tiled=True)  19.2 us
    all_to_all x1, waiting for transfers between devices, local(): lax.all_to_all(send, 'tiles', split_axis=2, concat_axis=2, tiled=True)  11.8 us
    all_to_all x1, starting transfers between devices, local(): lax.all_to_all(send, 'tiles', split_axis=2, concat_axis=2, tiled=True)  9.06 us
    all_to_all x1, waiting for transfers between devices, local(): grads = lax.all_to_all(column_all, 'cams', 1, 1, tiled=True).sum(axis=1)  8.69 us
    all_to_all x1, starting transfers between devices, local(): lax.all_to_all(jnp.broadcast_to(params[None], (cams,) + params.shape), 'c...  7.23 us
    all_to_all x1, waiting for transfers between devices, local(): lax.all_to_all(jnp.broadcast_to(params[None], (cams,) + params.shape), 'c...  6.48 us
    dot_general x3, matrix products, render_tile(): jnp.dot(colours, weight, precision=lax.Precision.HIGHEST, preferred_eleme...  4.87 us
  transfers between devices with their start and end apart: 4, of which 4 were waited for; matrix products, arithmetic and copies ran while one was open for 9% of the time, Pallas kernels for 0%

profile of v5, /device:TPU:6, one launch (start us, length us, event | category | flops | bytes accessed | tf_op | source)
XLA Modules:
  0.0 134.7 jit_solution(17308538181587142426)
XLA Ops:
  1.3 1.5 %concatenate.34 = f32[25,256]{1,0:T(8,128)S(1)} concatenate(f32[2,256]{1,0:T(2,128)S(1)} %copy-done.17, f32[2,256]{1,0:T(2,128)} %param.10, f32[1,256]{1,0:T(1,128)S(1)} %bitcast.119, f32[1,256]{1,0:T(1,128)} %bitcast.120, f32[19,256]{1,0:T(8,128)} %param.13), dimensions={0} | concatenate | bytes 51200 | tf_op jit(solution)/shard_map/concatenate | solution.py:97
  3.6 7.2 %all-to-all-start = ((f32[8,25,256]{2,1,0:T(8,128)}), f32[8,25,256]{2,1,0:T(8,128)S(1)}, u32[]{:S(2)}, u32[]{:S(2)}) async-start(f32[8,25,256]{2,1,0:T(8,128)} %broadcast_in_dim.16), calls=%async_computation | async-start | bytes 524288 | tf_op jit(solution)/shard_map/all_to_all | solution.py:99
  14.1 0.9 scatter_custom_fusion
  16.2 6.5 %all-to-all-done = f32[8,25,256]{2,1,0:T(8,128)S(1)} async-done(((f32[8,25,256]{2,1,0:T(8,128)}), f32[8,25,256]{2,1,0:T(8,128)S(1)}, u32[]{:S(2)}, u32[]{:S(2)}) %all-to-all-start) | async-done | bytes 204832 | tf_op jit(solution)/shard_map/all_to_all | solution.py:99
  23.6 19.4 %all-to-all-start.1 = ((s32[96,2,1]{1,2,0:T(1,128)}), s32[96,2,1]{1,2,0:T(1,128)S(1)}, u32[]{:S(2)}, u32[]{:S(2)}) async-start(s32[96,2,1]{1,2,0:T(1,128)} %bitcast.13), calls=%async_computation.1 | async-start | bytes 98304 | tf_op jit(solution)/shard_map/all_to_all | solution.py:115
  43.0 2.6 %divide_convert_fusion = (bf16[1,8,256]{2,1,0:T(8,128)(2,1)S(1)}, f32[1,8,256]{2,1,0:T(8,128)S(1)}, f32[1,8,256]{2,1,0:T(8,128)S(1)}, f32[1,8,256]{2,1,0:T(8,128...) fusion(f32[25,8,256]{2,1,0:T(8,128)S(1)} %bitcast.106, ...), kind=kLoop, calls=%fused_computation.107 | loop fusion | flops 98304 | bytes 98328 | tf_op jit(solution)/shard_map/convert.15
  47.9 1.2 concatenate.42
  49.1 4.3 %all-to-all-done.1 = s32[96,2,1]{1,2,0:T(1,128)S(1)} async-done(((s32[96,2,1]{1,2,0:T(1,128)}), s32[96,2,1]{1,2,0:T(1,128)S(1)}, u32[]{:S(2)}, u32[]{:S(2)}) %all-to-all-start.1) | async-done | bytes 800 | tf_op jit(solution)/shard_map/all_to_all | solution.py:115
  55.4 1.0 reshape.434
  56.5 9.1 %all-to-all-start.2 = ((bf16[96,2,200]{2,1,0:T(2,128)(2,1)}), bf16[96,2,200]{2,1,0:T(2,128)(2,1)S(1)}, u32[]{:S(2)}, u32[]{:S(2)}) async-start(bf16[96,2,200]{2,1,0:T(2,128)(2,1)} %reshape.434), calls=%async_computation.2 | async-start | bytes 196608 | tf_op jit(solution)/shard_map/all_to_all | solution.py:129
  65.7 11.8 %all-to-all-done.2 = bf16[96,2,200]{2,1,0:T(2,128)(2,1)S(1)} async-done(((bf16[96,2,200]{2,1,0:T(2,128)(2,1)}), bf16[96,2,200]{2,1,0:T(2,128)(2,1)S(1)}, u32[]{:S(2)}, u32[]{:S(2)}) %all-to-all-start.2) | async-done | bytes 76832 | tf_op jit(solution)/shard_map/all_to_all | solution.py:129
  80.7 1.8 %fusion.1 = bf16[19,16,48]{2,0,1:T(8,128)(2,1)S(1)} fusion(f32[16,48]{1,0:T(8,128)S(1)} %mul.731, f32[16,48]{1,0:T(8,128)S(1)} %sub.85, f32[256]{0:T(256)S(1)} %get-tuple-element.64, f32[16,48]{1,0:T(8,128)S(1)} %mul.727, f32[16,48]{1,0:T(8,128)S(1)} %sub.79, f32[256]{0:T(256)S(1)} %get-tuple-element.65, f32[16,48]{1,0:T(8,128)S(1)} %mul.722, ...), kind=kOutput, calls=%fused_computation.17 | convolution fusion | flops 47790336 | bytes 991744 | tf_op jit(solution)/shard_map/transpose(jvp(vmap()))/dot_general | solution.py:53
  83.0 1.3 multiply_multiply_fusion.1
  84.3 0.9 fusion.21
  85.3 2.9 %fusion.15 = (f32[16,48]{1,0:T(8,128)S(1)}, f32[16,48]{1,0:T(8,128)S(1)}, f32[16,48]{1,0:T(8,128)S(1)}, f32[16,48]{1,0:T(8,128)S(1)}, f32[16,48]{1,0:T(8,128)S(1)}, /*index=5*/f32[16,48]{1,0:T(8,128)S(1)}) fusion(f32[16,48]{1,0:T(8,128)S(1)} %sub.85, f32[256]{0:T(256)S(1)} %get-tuple-element.64, f32[16,48]{1,0:T(8,128)S(1)} %mul.731, f32[16,48]{1,0:T(8,128)S(1)} %mul.727, ...), kind=kLoop, calls=%fused_computation.33 | loop fusion | flops 9432576 | bytes 2398208 | tf_op jit(solution)/shard_map/transpose(jvp(vmap()))/reduce_sum | solution.py:48
  89.5 19.2 %all_to_all.29 = bf16[96,2,200]{2,1,0:T(2,128)(2,1)S(1)} all-to-all(bf16[96,2,200]{2,1,0:T(2,128)(2,1)S(1)} %reshape.436), channel_id=1, replica_groups=mesh['tiles'=96,'cams'=8] {'tiles'}, dimensions={0} | all-to-all | bytes 153600 | tf_op jit(solution)/shard_map/all_to_all | solution.py:147
  110.2 1.3 slice_multiply_fusion
  113.9 1.3 multiply_add_fusion
  115.2 1.3 add_multiply_fusion
  117.2 1.0 copy.201
  118.3 3.6 %all-to-all-start.4 = ((f32[25,8,256]{2,0,1:T(8,128)}), f32[25,8,256]{2,0,1:T(8,128)S(1)}, u32[]{:S(2)}, u32[]{:S(2)}) async-start(f32[25,8,256]{2,0,1:T(8,128)} %copy.201), calls=%async_computation.4 | async-start | bytes 524288 | tf_op jit(solution)/shard_map/all_to_all | solution.py:160
  121.9 1.7 %convolution_bitcast_fusion = f32[19,16,256]{2,0,1:T(8,128)S(1)} fusion(f32[19,16,48]{0,2,1:T(8,128)S(1)} %bitcast.114, f32[16,48]{1,0:T(8,128)S(1)} %mul.731, f32[16,48]{1,0:T(8,128)S(1)} %copy-done.4, f32[256]{0:T(256)S(1)} %copy-done.12, f32[16,48]{1,0:T(8,128)S(1)} %copy-done.6, f32[16,48]{1,0:T(8,128)S(1)} %copy-done.8, f32[256]{0:T(256)S(1)} %copy-done.14, ...), kind=kOutput, calls=%fused_computation.12 | convolution fusion | flops 47775744 | bytes 1176576 | tf_op jit(solution)/shard_map/jvp(vmap())/dot_general | solution.py:53
  123.7 1.0 reshape.422
  124.8 8.7 %all-to-all-done.4 = f32[25,8,256]{2,0,1:T(8,128)S(1)} async-done(((f32[25,8,256]{2,0,1:T(8,128)}), f32[25,8,256]{2,0,1:T(8,128)S(1)}, u32[]{:S(2)}, u32[]{:S(2)}) %all-to-all-start.4) | async-done | bytes 204832 | tf_op jit(solution)/shard_map/all_to_all | solution.py:160
  (139 shorter events, 20.4 us)
Async XLA Ops:
  0.6 0.7 copy-start.17
  0.6 0.7 copy-start.19
  3.6 7.2 %copy-start.16 = (s32[1,16,2,3]{1,2,3,0:T(2,128)S(1)}, s32[1,16,2,3]{1,2,3,0:T(2,128)}, u32[]{:S(2)}) copy-start(s32[1,16,2,3]{1,2,3,0:T(2,128)} %param.16) | copy-start | bytes 1156
  3.6 19.1 %all-to-all-start = ((f32[8,25,256]{2,1,0:T(8,128)}), f32[8,25,256]{2,1,0:T(8,128)S(1)}, u32[]{:S(2)}, u32[]{:S(2)}) async-start(f32[8,25,256]{2,1,0:T(8,128)} %broadcast_in_dim.16), calls=%async_computation | async-start | bytes 524288 | tf_op jit(solution)/shard_map/all_to_all | solution.py:99
  11.0 0.7 copy-start.15
  15.0 0.7 copy-start.18
  23.6 29.8 %all-to-all-start.1 = ((s32[96,2,1]{1,2,0:T(1,128)}), s32[96,2,1]{1,2,0:T(1,128)S(1)}, u32[]{:S(2)}, u32[]{:S(2)}) async-start(s32[96,2,1]{1,2,0:T(1,128)} %bitcast.13), calls=%async_computation.1 | async-start | bytes 98304 | tf_op jit(solution)/shard_map/all_to_all | solution.py:115
  56.5 9.1 %copy-start.2 = (bf16[19,1,4096]{2,0,1:T(8,128)(2,1)S(1)}, bf16[19,1,4096]{2,0,1:T(8,128)(2,1)}, u32[]{:S(2)}) copy-start(bf16[19,1,4096]{2,0,1:T(8,128)(2,1)} %param.17) | copy-start | bytes 466948
  56.5 21.0 %all-to-all-start.2 = ((bf16[96,2,200]{2,1,0:T(2,128)(2,1)}), bf16[96,2,200]{2,1,0:T(2,128)(2,1)S(1)}, u32[]{:S(2)}, u32[]{:S(2)}) async-start(bf16[96,2,200]{2,1,0:T(2,128)(2,1)} %reshape.434), calls=%async_computation.2 | async-start | bytes 196608 | tf_op jit(solution)/shard_map/all_to_all | solution.py:129
  65.6 19.7 %copy-start.11 = (f32[256]{0:T(256)}, f32[256]{0:T(256)S(1)}, u32[]{:S(2)}) copy-start(f32[256]{0:T(256)S(1)} %get-tuple-element.64) | copy-start | bytes 3076
  65.6 19.7 %copy-start.13 = (f32[256]{0:T(256)}, f32[256]{0:T(256)S(1)}, u32[]{:S(2)}) copy-start(f32[256]{0:T(256)S(1)} %get-tuple-element.65) | copy-start | bytes 3076
  78.7 6.5 %copy-start.3 = (f32[16,48]{1,0:T(8,128)}, f32[16,48]{1,0:T(8,128)S(1)}, u32[]{:S(2)}) copy-start(f32[16,48]{1,0:T(8,128)S(1)} %sub.85) | copy-start | bytes 9220
  78.9 6.4 %copy-start.5 = (f32[16,48]{1,0:T(8,128)}, f32[16,48]{1,0:T(8,128)S(1)}, u32[]{:S(2)}) copy-start(f32[16,48]{1,0:T(8,128)S(1)} %mul.727) | copy-start | bytes 9220
  79.1 6.2 %copy-start.7 = (f32[16,48]{1,0:T(8,128)}, f32[16,48]{1,0:T(8,128)S(1)}, u32[]{:S(2)}) copy-start(f32[16,48]{1,0:T(8,128)S(1)} %sub.79) | copy-start | bytes 9220
  79.2 6.0 %copy-start.9 = (f32[16,48]{1,0:T(8,128)}, f32[16,48]{1,0:T(8,128)S(1)}, u32[]{:S(2)}) copy-start(f32[16,48]{1,0:T(8,128)S(1)} %mul.722) | copy-start | bytes 9220
  80.7 4.6 %copy-start = (f32[16,48,256]{2,0,1:T(8,128)}, f32[16,48,256]{2,0,1:T(8,128)S(1)}, u32[]{:S(2)}) copy-start(f32[16,48,256]{2,0,1:T(8,128)S(1)} %fusion.24) | copy-start | bytes 2359300
  117.2 4.6 %copy-start.1 = (f32[16,48,256]{2,0,1:T(8,128)S(1)}, f32[16,48,256]{2,0,1:T(8,128)}, u32[]{:S(2)}) copy-start(f32[16,48,256]{2,0,1:T(8,128)} %copy-done) | copy-start | bytes 2359300
  118.2 3.6 %copy-start.4 = (f32[16,48]{1,0:T(8,128)S(1)}, f32[16,48]{1,0:T(8,128)}, u32[]{:S(2)}) copy-start(f32[16,48]{1,0:T(8,128)} %copy-done.3) | copy-start | bytes 9220
  118.2 3.6 %copy-start.6 = (f32[16,48]{1,0:T(8,128)S(1)}, f32[16,48]{1,0:T(8,128)}, u32[]{:S(2)}) copy-start(f32[16,48]{1,0:T(8,128)} %copy-done.5) | copy-start | bytes 9220
  118.2 3.6 %copy-start.8 = (f32[16,48]{1,0:T(8,128)S(1)}, f32[16,48]{1,0:T(8,128)}, u32[]{:S(2)}) copy-start(f32[16,48]{1,0:T(8,128)} %copy-done.7) | copy-start | bytes 9220
  118.2 3.6 %copy-start.10 = (f32[16,48]{1,0:T(8,128)S(1)}, f32[16,48]{1,0:T(8,128)}, u32[]{:S(2)}) copy-start(f32[16,48]{1,0:T(8,128)} %copy-done.9) | copy-start | bytes 9220
  118.2 3.6 %copy-start.12 = (f32[256]{0:T(256)S(1)}, f32[256]{0:T(256)}, u32[]{:S(2)}) copy-start(f32[256]{0:T(256)} %copy-done.11) | copy-start | bytes 3076
  118.3 3.6 %copy-start.14 = (f32[256]{0:T(256)S(1)}, f32[256]{0:T(256)}, u32[]{:S(2)}) copy-start(f32[256]{0:T(256)} %copy-done.13) | copy-start | bytes 3076
  118.3 15.2 %all-to-all-start.4 = ((f32[25,8,256]{2,0,1:T(8,128)}), f32[25,8,256]{2,0,1:T(8,128)S(1)}, u32[]{:S(2)}, u32[]{:S(2)}) async-start(f32[25,8,256]{2,0,1:T(8,128)} %copy.201), calls=%async_computation.4 | async-start | bytes 524288 | tf_op jit(solution)/shard_map/all_to_all | solution.py:160

commit v6 on v5

--- a/solution.py
+++ b/solution.py
@@ -36,6 +36,50 @@
     )
 
 
+def project_pullback(geometry, linear, grad):
+    lin_xx = 1.0 + linear[0]
+    lin_xy = linear[1]
+    lin_yx = linear[2]
+    lin_yy = 1.0 + linear[3]
+    diag_x = geometry[2]
+    diag_y = geometry[3]
+    lower = geometry[4]
+    cov_xx = diag_x * diag_x
+    cov_xy = diag_x * lower
+    cov_yy = lower * lower + diag_y * diag_y
+    half_xx = lin_xx * cov_xx + lin_xy * cov_xy
+    half_xy = lin_xx * cov_xy + lin_xy * cov_yy
+    half_yx = lin_yx * cov_xx + lin_yy * cov_xy
+    half_yy = lin_yx * cov_xy + lin_yy * cov_yy
+    img_xx = half_xx * lin_xx + half_xy * lin_xy + 0.3
+    img_xy = half_xx * lin_yx + half_xy * lin_yy
+    img_yy = half_yx * lin_yx + half_yy * lin_yy + 0.3
+    determ = img_xx * img_yy - img_xy * img_xy
+    inv = 1.0 / determ
+    scale = (grad[2] * img_yy - grad[3] * img_xy + grad[4] * img_xx) * inv * inv
+    g_xx = grad[4] * inv - scale * img_yy
+    g_yy = grad[2] * inv - scale * img_xx
+    g_xy = 2.0 * scale * img_xy - grad[3] * inv
+    g_half_xx = g_xx * lin_xx + g_xy * lin_yx
+    g_half_xy = g_xx * lin_xy + g_xy * lin_yy
+    g_half_yx = g_yy * lin_yx
+    g_half_yy = g_yy * lin_yy
+    g_cov_xx = g_half_xx * lin_xx + g_half_yx * lin_yx
+    g_cov_xy = g_half_xx * lin_xy + g_half_xy * lin_xx + g_half_yx * lin_yy + g_half_yy * lin_yx
+    g_cov_yy = g_half_xy * lin_xy + g_half_yy * lin_yy
+    opacity = jax.nn.sigmoid(geometry[5])
+    return jnp.stack(
+        [
+            grad[0] * lin_xx + grad[1] * lin_yx,
+            grad[0] * lin_xy + grad[1] * lin_yy,
+            2.0 * g_cov_xx * diag_x + g_cov_xy * lower,
+            2.0 * g_cov_yy * diag_y,
+            g_cov_xy * diag_x + 2.0 * g_cov_yy * lower,
+            grad[5] * 0.95 * opacity * (1.0 - opacity),
+        ]
+    )
+
+
 def render_tile(projected, colours):
     pixels = jnp.arange(SIDE * SIDE)
     across = (pixels % SIDE).astype(jnp.float32) + 0.5 - SIDE / 2
@@ -151,15 +195,12 @@
         owner_hot.reshape(cams, local_blocks, slot_count),
         preferred_element_type=jnp.float32,
     ).reshape(rows, cams, local_blocks * BLK)
-    unused, pull_params = jax.vjp(
-        lambda params: project(params, linear, camera_shift), geometry_col
-    )
-    column_geometry = pull_params(summed[:6])[0]
+    column_geometry = project_pullback(geometry_col, linear, summed[:6])
     column_colour = summed[6:]
     column_all = jnp.concatenate([column_geometry, column_colour], axis=0)
-    grads = lax.all_to_all(column_all, "cams", 1, 1, tiled=True).sum(axis=1)
-    grad_geometry = grads[:6]
-    grad_appearance = grads[6:]
+    grads = lax.all_to_all(column_all, "cams", 1, 1, tiled=True)
+    grad_geometry = grads[:6].sum(axis=1)
+    grad_appearance = grads[6:].sum(axis=1)
     return (picture.reshape(channels, 1, -1), grad_geometry, grad_appearance)
 
 

time: 136 us -> 146 us (1.074)
  local copies, waits for them, and re-layouts: 23.1 us -> 32.2 us
    add x0 -> x6, local copies, waits for them, and re-layouts: none -> 4.56 us  [the longest x1 1.41 us: project_pullback(): 2.0 * g_cov_xx * diag_x + g_cov_xy * lower]
    concatenate x1 -> x2, local copies, waits for them, and re-layouts: 1.03 us -> 5.27 us  [local(): column_all = jnp.concatenate([column_geometry, column_colour], axis=0)]
    add_any x3 -> x0, other arithmetic: 2.57 us -> none  [the longest x1 1.28 us: project(): cov_xy = diag_x * lower]
    mul x10 -> x4, local copies, waits for them, and re-layouts: 1.02 us -> 2.91 us  [the longest x3 1.55 us: project_pullback(): grad[5] * 0.95 * opacity * (1.0 - opacity)]
  transfers between devices with their start and end apart: 4 -> 4, of which waited for: 4 -> 4; matrix products, arithmetic and copies ran while one was open for 9% -> 8% of each run, Pallas kernels for 0% -> 0%
where the time goes in v6:
time: 146 us; the launch traced here: 145 us
  starting transfers between devices  39.2 us (27%)
  local copies, waits for them, and re-layouts  32.2 us (22%)
  waiting for transfers between devices  31.3 us (21%)
  blocking collectives  19.2 us (13%)
  other arithmetic  13.9 us (10%)
  matrix products  6.04 us (4%)
  between operations  2.67 us (2%)
    all_to_all x1, starting transfers between devices, local(): lax.all_to_all(request, 'tiles', split_axis=0, concat_axis=0, tiled=True)  19.4 us
    all_to_all x1, blocking collectives, local(): lax.all_to_all(back, 'tiles', split_axis=2, concat_axis=2, tiled=True)  19.2 us
    all_to_all x1, waiting for transfers between devices, local(): lax.all_to_all(send, 'tiles', split_axis=2, concat_axis=2, tiled=True)  11.8 us
    all_to_all x1, starting transfers between devices, local(): lax.all_to_all(send, 'tiles', split_axis=2, concat_axis=2, tiled=True)  9.05 us
    all_to_all x1, waiting for transfers between devices, local(): grads = lax.all_to_all(column_all, 'cams', 1, 1, tiled=True)  8.69 us
    all_to_all x1, starting transfers between devices, local(): lax.all_to_all(jnp.broadcast_to(params[None], (cams,) + params.shape), 'c...  7.23 us
    all_to_all x1, waiting for transfers between devices, local(): lax.all_to_all(jnp.broadcast_to(params[None], (cams,) + params.shape), 'c...  6.46 us
    concatenate x2, local copies, waits for them, and re-layouts, local(): column_all = jnp.concatenate([column_geometry, column_colour], axis=0)  5.27 us
  transfers between devices with their start and end apart: 4, of which 4 were waited for; matrix products, arithmetic and copies ran while one was open for 8% of the time, Pallas kernels for 0%

profile of v6, /device:TPU:6, one launch (start us, length us, event | category | flops | bytes accessed | tf_op | source)
XLA Modules:
  0.0 144.6 jit_solution(8762235410390175626)
XLA Ops:
  1.3 1.5 %concatenate.34 = f32[25,256]{1,0:T(8,128)S(1)} concatenate(f32[2,256]{1,0:T(2,128)S(1)} %copy-done.17, f32[2,256]{1,0:T(2,128)} %param.10, f32[1,256]{1,0:T(1,128)S(1)} %bitcast.115, f32[1,256]{1,0:T(1,128)} %bitcast.116, f32[19,256]{1,0:T(8,128)} %param.13), dimensions={0} | concatenate | bytes 51200 | tf_op jit(solution)/shard_map/concatenate | solution.py:141
  3.6 7.2 %all-to-all-start = ((f32[8,25,256]{2,1,0:T(8,128)}), f32[8,25,256]{2,1,0:T(8,128)S(1)}, u32[]{:S(2)}, u32[]{:S(2)}) async-start(f32[8,25,256]{2,1,0:T(8,128)} %broadcast_in_dim.16), calls=%async_computation | async-start | bytes 524288 | tf_op jit(solution)/shard_map/all_to_all | solution.py:143
  16.2 6.5 %all-to-all-done = f32[8,25,256]{2,1,0:T(8,128)S(1)} async-done(((f32[8,25,256]{2,1,0:T(8,128)}), f32[8,25,256]{2,1,0:T(8,128)S(1)}, u32[]{:S(2)}, u32[]{:S(2)}) %all-to-all-start) | async-done | bytes 204832 | tf_op jit(solution)/shard_map/all_to_all | solution.py:143
  23.6 19.4 %all-to-all-start.1 = ((s32[96,2,1]{1,2,0:T(1,128)}), s32[96,2,1]{1,2,0:T(1,128)S(1)}, u32[]{:S(2)}, u32[]{:S(2)}) async-start(s32[96,2,1]{1,2,0:T(1,128)} %bitcast.13), calls=%async_computation.1 | async-start | bytes 98304 | tf_op jit(solution)/shard_map/all_to_all | solution.py:159
  43.0 2.6 %divide_convert_fusion = (bf16[1,8,256]{2,1,0:T(8,128)(2,1)S(1)}, f32[1,8,256]{2,1,0:T(8,128)S(1)}, f32[1,8,256]{2,1,0:T(8,128)S(1)}, f32[1,8,256]{2,1,0:T(8,128...) fusion(f32[25,8,256]{2,1,0:T(8,128)S(1)} %bitcast.102, ...), kind=kLoop, calls=%fused_computation.103 | loop fusion | flops 98304 | bytes 98328 | tf_op jit(solution)/shard_map/convert.15
  49.1 4.3 %all-to-all-done.1 = s32[96,2,1]{1,2,0:T(1,128)S(1)} async-done(((s32[96,2,1]{1,2,0:T(1,128)}), s32[96,2,1]{1,2,0:T(1,128)S(1)}, u32[]{:S(2)}, u32[]{:S(2)}) %all-to-all-start.1) | async-done | bytes 800 | tf_op jit(solution)/shard_map/all_to_all | solution.py:159
  56.5 9.1 %all-to-all-start.2 = ((bf16[96,2,200]{2,1,0:T(2,128)(2,1)}), bf16[96,2,200]{2,1,0:T(2,128)(2,1)S(1)}, u32[]{:S(2)}, u32[]{:S(2)}) async-start(bf16[96,2,200]{2,1,0:T(2,128)(2,1)} %reshape.442), calls=%async_computation.2 | async-start | bytes 196608 | tf_op jit(solution)/shard_map/all_to_all | solution.py:173
  65.7 11.8 %all-to-all-done.2 = bf16[96,2,200]{2,1,0:T(2,128)(2,1)S(1)} async-done(((bf16[96,2,200]{2,1,0:T(2,128)(2,1)}), bf16[96,2,200]{2,1,0:T(2,128)(2,1)S(1)}, u32[]{:S(2)}, u32[]{:S(2)}) %all-to-all-start.2) | async-done | bytes 76832 | tf_op jit(solution)/shard_map/all_to_all | solution.py:173
  80.7 1.8 %fusion.1 = bf16[19,16,48]{2,0,1:T(8,128)(2,1)S(1)} fusion(f32[16,48]{1,0:T(8,128)S(1)} %mul.739, f32[16,48]{1,0:T(8,128)S(1)} %sub.109, f32[256]{0:T(256)S(1)} %get-tuple-element.62, f32[16,48]{1,0:T(8,128)S(1)} %mul.735, f32[16,48]{1,0:T(8,128)S(1)} %sub.103, f32[256]{0:T(256)S(1)} %get-tuple-element.63, f32[16,48]{1,0:T(8,128)S(1)} %mul.730, ...), kind=kOutput, calls=%fused_computation.17 | convolution fusion | flops 47790336 | bytes 991744 | tf_op jit(solution)/shard_map/transpose(jvp(vmap()))/dot_general | solution.py:97
  83.0 1.3 multiply_multiply_fusion.1
  85.3 2.9 %fusion.15 = (f32[16,48]{1,0:T(8,128)S(1)}, f32[16,48]{1,0:T(8,128)S(1)}, f32[16,48]{1,0:T(8,128)S(1)}, f32[16,48]{1,0:T(8,128)S(1)}, f32[16,48]{1,0:T(8,128)S(1)}, /*index=5*/f32[16,48]{1,0:T(8,128)S(1)}) fusion(f32[16,48]{1,0:T(8,128)S(1)} %sub.109, f32[256]{0:T(256)S(1)} %get-tuple-element.62, f32[16,48]{1,0:T(8,128)S(1)} %mul.739, ...), kind=kLoop, calls=%fused_computation.32 | loop fusion | flops 9432576 | bytes 2398208 | tf_op jit(solution)/shard_map/transpose(jvp(vmap()))/reduce_sum | solution.py:92
  89.5 19.2 %all_to_all.29 = bf16[96,2,200]{2,1,0:T(2,128)(2,1)S(1)} all-to-all(bf16[96,2,200]{2,1,0:T(2,128)(2,1)S(1)} %reshape.444), channel_id=1, replica_groups=mesh['tiles'=96,'cams'=8] {'tiles'}, dimensions={0} | all-to-all | bytes 153600 | tf_op jit(solution)/shard_map/all_to_all | solution.py:191
  110.2 1.3 slice_multiply_fusion
  113.5 1.3 add.373
  114.8 1.3 multiply_add_fusion.2
  116.1 1.3 slice_multiply_fusion.1
  117.4 1.4 copy.207
  118.7 1.4 copy.208
  120.1 1.4 copy.206
  121.5 1.4 copy.209
  122.8 4.2 %concatenate.46 = f32[25,8,256]{0,2,1:T(8,128)S(1)} concatenate(f32[1,8,256]{0,2,1:T(8,128)} %add.373, f32[1,8,256]{0,2,1:T(8,128)S(1)} %add.374, f32[1,8,256]{0,2,1:T(8,128)} %copy.206, f32[1,8,256]{0,2,1:T(8,128)} %copy.207, f32[1,8,256]{0,2,1:T(8,128)} %copy.208, f32[1,8,256]{0,2,1:T(8,128)} %copy.209, f32[19,8,256]{0,2,1:T(8,128)S(1)} %bitcast.93), dimensions={0} | concatenate | bytes 409600 | tf_op jit(solution)/shard_map/concatenate | solution.py:200
  128.2 3.6 %all-to-all-start.4 = ((f32[25,8,256]{2,0,1:T(8,128)}), f32[25,8,256]{2,0,1:T(8,128)S(1)}, u32[]{:S(2)}, u32[]{:S(2)}) async-start(f32[25,8,256]{2,0,1:T(8,128)} %copy.210), calls=%async_computation.4 | async-start | bytes 524288 | tf_op jit(solution)/shard_map/all_to_all | solution.py:201
  131.8 1.7 %convolution_bitcast_fusion = f32[19,16,256]{2,0,1:T(8,128)S(1)} fusion(f32[19,16,48]{0,2,1:T(8,128)S(1)} %bitcast.110, f32[16,48]{1,0:T(8,128)S(1)} %mul.739, f32[16,48]{1,0:T(8,128)S(1)} %copy-done.4, f32[256]{0:T(256)S(1)} %copy-done.12, f32[16,48]{1,0:T(8,128)S(1)} %copy-done.6, f32[16,48]{1,0:T(8,128)S(1)} %copy-done.8, f32[256]{0:T(256)S(1)} %copy-done.14, ...), kind=kOutput, calls=%fused_computation.12 | convolution fusion | flops 47775744 | bytes 1176576 | tf_op jit(solution)/shard_map/jvp(vmap())/dot_general | solution.py:97
  134.7 8.7 %all-to-all-done.4 = f32[25,8,256]{2,0,1:T(8,128)S(1)} async-done(((f32[25,8,256]{2,0,1:T(8,128)}), f32[25,8,256]{2,0,1:T(8,128)S(1)}, u32[]{:S(2)}, u32[]{:S(2)}) %all-to-all-start.4) | async-done | bytes 204832 | tf_op jit(solution)/shard_map/all_to_all | solution.py:201
  (136 shorter events, 25.4 us)
Async XLA Ops:
  0.6 0.7 copy-start.17
  0.6 0.7 copy-start.19
  3.6 7.2 %copy-start.16 = (s32[1,16,2,3]{1,2,3,0:T(2,128)S(1)}, s32[1,16,2,3]{1,2,3,0:T(2,128)}, u32[]{:S(2)}) copy-start(s32[1,16,2,3]{1,2,3,0:T(2,128)} %param.16) | copy-start | bytes 1156
  3.6 19.1 %all-to-all-start = ((f32[8,25,256]{2,1,0:T(8,128)}), f32[8,25,256]{2,1,0:T(8,128)S(1)}, u32[]{:S(2)}, u32[]{:S(2)}) async-start(f32[8,25,256]{2,1,0:T(8,128)} %broadcast_in_dim.16), calls=%async_computation | async-start | bytes 524288 | tf_op jit(solution)/shard_map/all_to_all | solution.py:143
  11.0 0.7 copy-start.15
  15.0 0.7 copy-start.18
  23.6 29.8 %all-to-all-start.1 = ((s32[96,2,1]{1,2,0:T(1,128)}), s32[96,2,1]{1,2,0:T(1,128)S(1)}, u32[]{:S(2)}, u32[]{:S(2)}) async-start(s32[96,2,1]{1,2,0:T(1,128)} %bitcast.13), calls=%async_computation.1 | async-start | bytes 98304 | tf_op jit(solution)/shard_map/all_to_all | solution.py:159
  56.5 9.1 %copy-start.2 = (bf16[19,1,4096]{2,0,1:T(8,128)(2,1)S(1)}, bf16[19,1,4096]{2,0,1:T(8,128)(2,1)}, u32[]{:S(2)}) copy-start(bf16[19,1,4096]{2,0,1:T(8,128)(2,1)} %param.17) | copy-start | bytes 466948
  56.5 21.0 %all-to-all-start.2 = ((bf16[96,2,200]{2,1,0:T(2,128)(2,1)}), bf16[96,2,200]{2,1,0:T(2,128)(2,1)S(1)}, u32[]{:S(2)}, u32[]{:S(2)}) async-start(bf16[96,2,200]{2,1,0:T(2,128)(2,1)} %reshape.442), calls=%async_computation.2 | async-start | bytes 196608 | tf_op jit(solution)/shard_map/all_to_all | solution.py:173
  65.6 19.7 %copy-start.11 = (f32[256]{0:T(256)}, f32[256]{0:T(256)S(1)}, u32[]{:S(2)}) copy-start(f32[256]{0:T(256)S(1)} %get-tuple-element.62) | copy-start | bytes 3076
  65.6 19.7 %copy-start.13 = (f32[256]{0:T(256)}, f32[256]{0:T(256)S(1)}, u32[]{:S(2)}) copy-start(f32[256]{0:T(256)S(1)} %get-tuple-element.63) | copy-start | bytes 3076
  78.7 6.5 %copy-start.3 = (f32[16,48]{1,0:T(8,128)}, f32[16,48]{1,0:T(8,128)S(1)}, u32[]{:S(2)}) copy-start(f32[16,48]{1,0:T(8,128)S(1)} %sub.109) | copy-start | bytes 9220
  78.9 6.4 %copy-start.5 = (f32[16,48]{1,0:T(8,128)}, f32[16,48]{1,0:T(8,128)S(1)}, u32[]{:S(2)}) copy-start(f32[16,48]{1,0:T(8,128)S(1)} %mul.735) | copy-start | bytes 9220
  79.1 6.2 %copy-start.7 = (f32[16,48]{1,0:T(8,128)}, f32[16,48]{1,0:T(8,128)S(1)}, u32[]{:S(2)}) copy-start(f32[16,48]{1,0:T(8,128)S(1)} %sub.103) | copy-start | bytes 9220
  79.2 6.0 %copy-start.9 = (f32[16,48]{1,0:T(8,128)}, f32[16,48]{1,0:T(8,128)S(1)}, u32[]{:S(2)}) copy-start(f32[16,48]{1,0:T(8,128)S(1)} %mul.730) | copy-start | bytes 9220
  80.7 4.6 %copy-start = (f32[16,48,256]{2,0,1:T(8,128)}, f32[16,48,256]{2,0,1:T(8,128)S(1)}, u32[]{:S(2)}) copy-start(f32[16,48,256]{2,0,1:T(8,128)S(1)} %fusion.24) | copy-start | bytes 2359300
  127.1 4.6 %copy-start.1 = (f32[16,48,256]{2,0,1:T(8,128)S(1)}, f32[16,48,256]{2,0,1:T(8,128)}, u32[]{:S(2)}) copy-start(f32[16,48,256]{2,0,1:T(8,128)} %copy-done) | copy-start | bytes 2359300
  128.1 3.6 %copy-start.4 = (f32[16,48]{1,0:T(8,128)S(1)}, f32[16,48]{1,0:T(8,128)}, u32[]{:S(2)}) copy-start(f32[16,48]{1,0:T(8,128)} %copy-done.3) | copy-start | bytes 9220
  128.1 3.6 %copy-start.6 = (f32[16,48]{1,0:T(8,128)S(1)}, f32[16,48]{1,0:T(8,128)}, u32[]{:S(2)}) copy-start(f32[16,48]{1,0:T(8,128)} %copy-done.5) | copy-start | bytes 9220
  128.1 3.6 %copy-start.8 = (f32[16,48]{1,0:T(8,128)S(1)}, f32[16,48]{1,0:T(8,128)}, u32[]{:S(2)}) copy-start(f32[16,48]{1,0:T(8,128)} %copy-done.7) | copy-start | bytes 9220
  128.1 3.6 %copy-start.10 = (f32[16,48]{1,0:T(8,128)S(1)}, f32[16,48]{1,0:T(8,128)}, u32[]{:S(2)}) copy-start(f32[16,48]{1,0:T(8,128)} %copy-done.9) | copy-start | bytes 9220
  128.1 3.6 %copy-start.12 = (f32[256]{0:T(256)S(1)}, f32[256]{0:T(256)}, u32[]{:S(2)}) copy-start(f32[256]{0:T(256)} %copy-done.11) | copy-start | bytes 3076
  128.2 3.6 %copy-start.14 = (f32[256]{0:T(256)S(1)}, f32[256]{0:T(256)}, u32[]{:S(2)}) copy-start(f32[256]{0:T(256)} %copy-done.13) | copy-start | bytes 3076
  128.2 15.2 %all-to-all-start.4 = ((f32[25,8,256]{2,0,1:T(8,128)}), f32[25,8,256]{2,0,1:T(8,128)S(1)}, u32[]{:S(2)}, u32[]{:S(2)}) async-start(f32[25,8,256]{2,0,1:T(8,128)} %copy.210), calls=%async_computation.4 | async-start | bytes 524288 | tf_op jit(solution)/shard_map/all_to_all | solution.py:201

commit v7 on v6

--- a/solution.py
+++ b/solution.py
@@ -140,14 +140,15 @@
     geometry = jnp.concatenate([offsets, factor_diag, factor_off[None, :], logit[None, :]], axis=0)
     params = jnp.concatenate([geometry, appearance], axis=0)
     cams = lax.axis_size("cams")
+    local_blocks = params.shape[1] // BLK
+    per_column = cams * local_blocks
+    by_lane = params.reshape(params.shape[0], local_blocks, BLK).transpose(0, 2, 1)
     gathered = lax.all_to_all(
-        jnp.broadcast_to(params[None], (cams,) + params.shape), "cams", 0, 0, tiled=True
-    )
-    params_col = gathered.transpose(1, 0, 2)
+        jnp.broadcast_to(by_lane[None], (cams,) + by_lane.shape), "cams", 0, 0, tiled=True
+    )
+    params_col = gathered.transpose(1, 2, 0, 3).reshape(params.shape[0], BLK, per_column)
     geometry_col = params_col[:6]
     appearance_col = params_col[6:]
-    per_column = cams * params.shape[1] // BLK
-    local_blocks = params.shape[1] // BLK
     linear = cam_linear[0]
     camera_shift = cam_shift[0]
     entries = block_lists.reshape(-1)
@@ -165,9 +166,9 @@
         jnp.bfloat16
     )
     send = jnp.einsum(
-        "rjlb,jls->rbs",
-        payload_col.reshape(rows, cams, local_blocks, BLK),
-        owner_hot.reshape(cams, local_blocks, slot_count),
+        "rbk,ks->rbs",
+        payload_col,
+        owner_hot,
         preferred_element_type=jnp.float32,
     ).astype(jnp.bfloat16)
     sent = lax.all_to_all(send, "tiles", split_axis=2, concat_axis=2, tiled=True)
@@ -189,18 +190,16 @@
         preferred_element_type=jnp.float32,
     ).astype(jnp.bfloat16)
     returned = lax.all_to_all(back, "tiles", split_axis=2, concat_axis=2, tiled=True)
-    summed = jnp.einsum(
-        "rbs,jls->rjlb",
-        returned,
-        owner_hot.reshape(cams, local_blocks, slot_count),
-        preferred_element_type=jnp.float32,
-    ).reshape(rows, cams, local_blocks * BLK)
+    summed = jnp.einsum("rbs,ks->rbk", returned, owner_hot, preferred_element_type=jnp.float32)
     column_geometry = project_pullback(geometry_col, linear, summed[:6])
     column_colour = summed[6:]
     column_all = jnp.concatenate([column_geometry, column_colour], axis=0)
-    grads = lax.all_to_all(column_all, "cams", 1, 1, tiled=True)
-    grad_geometry = grads[:6].sum(axis=1)
-    grad_appearance = grads[6:].sum(axis=1)
+    grads = lax.all_to_all(
+        column_all.reshape(rows, BLK, cams, local_blocks), "cams", 2, 2, tiled=True
+    ).sum(axis=2)
+    grads = grads.transpose(0, 2, 1).reshape(rows, local_blocks * BLK)
+    grad_geometry = grads[:6]
+    grad_appearance = grads[6:]
     return (picture.reshape(channels, 1, -1), grad_geometry, grad_appearance)
 
 

time: 146 us -> 136 us (0.932)
  local copies, waits for them, and re-layouts: 32.2 us -> 20.7 us
  other arithmetic: 13.9 us -> 16.2 us
    concatenate x2 -> x8, local copies, waits for them, and re-layouts: 5.27 us -> 0.73 us  [local(): column_all = jnp.concatenate([column_geometry, column_colour], axis=0)]
    add x6 -> x2, local copies, waits for them, and re-layouts: 4.56 us -> 0.18 us  [the longest x1 0.09 us: project(): centre_y = lin_yx * geometry[0] + lin_yy * geometry[1] + camera_shift[1]]
    unnamed x46 -> x36, local copies, waits for them, and re-layouts: 4.13 us -> 8.45 us
    mul x4 -> x0, local copies, waits for them, and re-layouts: 2.91 us -> none  [the longest x3 1.55 us: project_pullback(): grad[5] * 0.95 * opacity * (1.0 - opacity)]
    concatenate x14 -> x1, local copies, waits for them, and re-layouts: 3.11 us -> 0.28 us  [local(): jnp.concatenate([project(geometry_col, linear, camera_shift), appearance_...]
    div x0 -> x1, other arithmetic: none -> 2.53 us  [project(): opacity = 0.95 * jax.nn.sigmoid(geometry[5])]
    all_to_all x0 -> x2, other arithmetic: none -> 2.26 us  [the longest x1 1.14 us: local(): lax.all_to_all(column_all.reshape(rows, BLK, cams, local_blocks), 'cams',...]
    all_to_all x1, waiting for transfers between devices: 4.35 us -> 6.13 us  [local(): lax.all_to_all(request, 'tiles', split_axis=0, concat_axis=0, tiled=True)]
  transfers between devices with their start and end apart: 4 -> 4, of which waited for: 4 -> 4; matrix products, arithmetic and copies ran while one was open for 8% -> 6% of each run, Pallas kernels for 0% -> 0%
where the time goes in v7:
time: 136 us; the launch traced here: 135 us
  starting transfers between devices  38.4 us (28%)
  waiting for transfers between devices  31.7 us (23%)
  local copies, waits for them, and re-layouts  20.7 us (15%)
  blocking collectives  19.2 us (14%)
  other arithmetic  16.2 us (12%)
  matrix products  5.86 us (4%)
  between operations  2.62 us (2%)
    all_to_all x1, starting transfers between devices, local(): lax.all_to_all(request, 'tiles', split_axis=0, concat_axis=0, tiled=True)  19.5 us
    all_to_all x1, blocking collectives, local(): lax.all_to_all(back, 'tiles', split_axis=2, concat_axis=2, tiled=True)  19.2 us
    all_to_all x1, waiting for transfers between devices, local(): lax.all_to_all(send, 'tiles', split_axis=2, concat_axis=2, tiled=True)  11.9 us
    unnamed x36, local copies, waits for them, and re-layouts  8.45 us
    all_to_all x1, starting transfers between devices, local(): lax.all_to_all(send, 'tiles', split_axis=2, concat_axis=2, tiled=True)  8.02 us
    all_to_all x1, waiting for transfers between devices, local(): lax.all_to_all(column_all.reshape(rows, BLK, cams, local_blocks), 'cams',...  7.31 us
    all_to_all x1, starting transfers between devices, local(): lax.all_to_all(jnp.broadcast_to(by_lane[None], (cams,) + by_lane.shape),...  7.23 us
    all_to_all x1, waiting for transfers between devices, local(): lax.all_to_all(jnp.broadcast_to(by_lane[None], (cams,) + by_lane.shape),...  6.36 us
  transfers between devices with their start and end apart: 4, of which 4 were waited for; matrix products, arithmetic and copies ran while one was open for 6% of the time, Pallas kernels for 0%

profile of v7, /device:TPU:6, one launch (start us, length us, event | category | flops | bytes accessed | tf_op | source)
XLA Modules:
  0.0 134.7 jit_solution(5710050897029911438)
XLA Ops:
  3.7 19.5 %all-to-all-start.1 = ((s32[96,2,1]{1,2,0:T(1,128)}), s32[96,2,1]{1,2,0:T(1,128)S(1)}, u32[]{:S(2)}, u32[]{:S(2)}) async-start(s32[96,2,1]{1,2,0:T(1,128)} %bitcast.14), calls=%async_computation.1 | async-start | bytes 98304 | tf_op jit(solution)/shard_map/all_to_all | solution.py:160
  26.6 1.0 reshape.705
  27.6 6.1 %all-to-all-done.1 = s32[96,2,1]{1,2,0:T(1,128)S(1)} async-done(((s32[96,2,1]{1,2,0:T(1,128)}), s32[96,2,1]{1,2,0:T(1,128)S(1)}, u32[]{:S(2)}, u32[]{:S(2)}) %all-to-all-start.1) | async-done | bytes 800 | tf_op jit(solution)/shard_map/all_to_all | solution.py:160
  33.7 7.2 %all-to-all-start = ((f32[8,1,6400]{2,1,0:T(1,128)}), f32[8,1,6400]{2,1,0:T(1,128)S(1)}, u32[]{:S(2)}, u32[]{:S(2)}) async-start(f32[8,1,6400]{2,1,0:T(1,128)} %reshape.705), calls=%async_computation | async-start | bytes 409600 | tf_op jit(solution)/shard_map/all_to_all | solution.py:146
  45.0 6.4 %all-to-all-done = f32[8,1,6400]{2,1,0:T(1,128)S(1)} async-done(((f32[8,1,6400]{2,1,0:T(1,128)}), f32[8,1,6400]{2,1,0:T(1,128)S(1)}, u32[]{:S(2)}, u32[]{:S(2)}) %all-to-all-start) | async-done | bytes 204832 | tf_op jit(solution)/shard_map/all_to_all | solution.py:146
  51.9 1.1 reduce.4
  53.7 2.5 %fusion.49 = (f32[1,8,8,32]{3,1,0,2:T(8,128)S(1)}, f32[1,8,8,32]{3,1,0,2:T(8,128)S(1)}, f32[1,8,8,32]{3,1,0,2:T(8,128)S(1)}, f32[1,8,8,32]{3,1,0,2:T(8,128)S(1)}...) fusion(f32[25,8,8,32]{3,1,0,2:T(8,128)S(1)} %bitcast.88, f32[]{:T(128)} %bitcast.8, f32[]{:T(128)} %bitcast.7, ...), kind=kLoop, calls=%fused_computation.77 | loop fusion | flops 26624 | bytes 90136 | tf_op jit(solution)/shard_map/div | solution.py:33
  56.8 1.3 divide_convert_fusion
  59.0 1.0 reshape.707
  60.0 8.0 %all-to-all-start.2 = ((bf16[96,2,200]{2,1,0:T(2,128)(2,1)}), bf16[96,2,200]{2,1,0:T(2,128)(2,1)S(1)}, u32[]{:S(2)}, u32[]{:S(2)}) async-start(bf16[96,2,200]{2,1,0:T(2,128)(2,1)} %reshape.707), calls=%async_computation.2 | async-start | bytes 196608 | tf_op jit(solution)/shard_map/all_to_all | solution.py:174
  68.1 11.9 %all-to-all-done.2 = bf16[96,2,200]{2,1,0:T(2,128)(2,1)S(1)} async-done(((bf16[96,2,200]{2,1,0:T(2,128)(2,1)}), bf16[96,2,200]{2,1,0:T(2,128)(2,1)S(1)}, u32[]{:S(2)}, u32[]{:S(2)}) %all-to-all-start.2) | async-done | bytes 76832 | tf_op jit(solution)/shard_map/all_to_all | solution.py:174
  83.2 1.8 %fusion = bf16[19,16,48]{2,0,1:T(8,128)(2,1)S(1)} fusion(f32[16,48]{1,0:T(8,128)S(1)} %mul.1130, f32[16,48]{1,0:T(8,128)S(1)} %sub.130, f32[256]{0:T(256)S(1)} %get-tuple-element.63, f32[16,48]{1,0:T(8,128)S(1)} %mul.1126, f32[16,48]{1,0:T(8,128)S(1)} %sub.124, f32[256]{0:T(256)S(1)} %get-tuple-element.64, f32[16,48]{1,0:T(8,128)S(1)} %mul.1121, ...), kind=kOutput, calls=%fused_computation.16 | convolution fusion | flops 47790336 | bytes 991744 | tf_op jit(solution)/shard_map/transpose(jvp(vmap()))/dot_general | solution.py:97
  85.4 1.3 multiply_multiply_fusion.1
  87.7 2.9 %fusion.14 = (f32[16,48]{1,0:T(8,128)S(1)}, f32[16,48]{1,0:T(8,128)S(1)}, f32[16,48]{1,0:T(8,128)S(1)}, f32[16,48]{1,0:T(8,128)S(1)}, f32[16,48]{1,0:T(8,128)S(1)}, /*index=5*/f32[16,48]{1,0:T(8,128)S(1)}) fusion(f32[16,48]{1,0:T(8,128)S(1)} %sub.130, f32[256]{0:T(256)S(1)} %get-tuple-element.63, f32[16,48]{1,0:T(8,128)S(1)} %mul.1130, ...), kind=kLoop, calls=%fused_computation.30 | loop fusion | flops 9432576 | bytes 2398208 | tf_op jit(solution)/shard_map/transpose(jvp(vmap()))/reduce_sum | solution.py:92
  91.9 19.2 %all_to_all.29 = bf16[96,2,200]{2,1,0:T(2,128)(2,1)S(1)} all-to-all(bf16[96,2,200]{2,1,0:T(2,128)(2,1)S(1)} %reshape.709), channel_id=1, replica_groups=mesh['tiles'=96,'cams'=8] {'tiles'}, dimensions={0} | all-to-all | bytes 153600 | tf_op jit(solution)/shard_map/all_to_all | solution.py:192
  112.0 1.3 fusion.51
  113.3 1.3 multiply_add_fusion
  114.5 1.3 fusion.52
  116.7 1.0 reshape.711
  117.7 3.6 %all-to-all-start.4 = ((f32[8,1,6400]{2,1,0:T(1,128)}), f32[8,1,6400]{2,1,0:T(1,128)S(1)}, u32[]{:S(2)}, u32[]{:S(2)}) async-start(f32[8,1,6400]{2,1,0:T(1,128)} %reshape.711), calls=%async_computation.4 | async-start | bytes 409600 | tf_op jit(solution)/shard_map/all_to_all | solution.py:197
  121.3 1.7 %convolution_bitcast_fusion = f32[19,16,256]{2,0,1:T(8,128)S(1)} fusion(f32[19,16,48]{0,2,1:T(8,128)S(1)} %bitcast.106, f32[16,48]{1,0:T(8,128)S(1)} %mul.1130, f32[16,48]{1,0:T(8,128)S(1)} %sub.130, f32[256]{0:T(256)S(1)} %get-tuple-element.63, f32[16,48]{1,0:T(8,128)S(1)} %mul.1126, f32[16,48]{1,0:T(8,128)S(1)} %sub.124, f32[256]{0:T(256)S(1)} %get-tuple-element.64, ...), kind=kOutput, calls=%fused_computation.12 | convolution fusion | flops 47775744 | bytes 1176576 | tf_op jit(solution)/shard_map/jvp(vmap())/dot_general | solution.py:97
  123.2 1.0 reshape.693
  124.2 7.3 %all-to-all-done.4 = f32[8,1,6400]{2,1,0:T(1,128)S(1)} async-done(((f32[8,1,6400]{2,1,0:T(1,128)}), f32[8,1,6400]{2,1,0:T(1,128)S(1)}, u32[]{:S(2)}, u32[]{:S(2)}) %all-to-all-start.4) | async-done | bytes 204832 | tf_op jit(solution)/shard_map/all_to_all | solution.py:197
  131.5 1.1 reduce.5
  (131 shorter events, 20.9 us)
Async XLA Ops:
  3.7 19.5 %copy-start.4 = (f32[2,256]{1,0:T(2,128)S(1)}, f32[2,256]{1,0:T(2,128)}, u32[]{:S(2)}) copy-start(f32[2,256]{1,0:T(2,128)} %param.9) | copy-start | bytes 6148
  3.7 30.0 %all-to-all-start.1 = ((s32[96,2,1]{1,2,0:T(1,128)}), s32[96,2,1]{1,2,0:T(1,128)S(1)}, u32[]{:S(2)}, u32[]{:S(2)}) async-start(s32[96,2,1]{1,2,0:T(1,128)} %bitcast.14), calls=%async_computation.1 | async-start | bytes 98304 | tf_op jit(solution)/shard_map/all_to_all | solution.py:160
  23.2 0.7 copy-start.5
  23.9 0.7 copy-start.7
  24.6 0.7 copy-start.8
  25.3 0.7 copy-start.2
  33.7 7.2 %copy-start.3 = (f32[1,4]{1,0:T(1,128)S(1)}, f32[1,4]{1,0:T(1,128)}, u32[]{:S(2)}) copy-start(f32[1,4]{1,0:T(1,128)} %param.14) | copy-start | bytes 52
  33.7 17.6 %all-to-all-start = ((f32[8,1,6400]{2,1,0:T(1,128)}), f32[8,1,6400]{2,1,0:T(1,128)S(1)}, u32[]{:S(2)}, u32[]{:S(2)}) async-start(f32[8,1,6400]{2,1,0:T(1,128)} %reshape.705), calls=%async_computation | async-start | bytes 409600 | tf_op jit(solution)/shard_map/all_to_all | solution.py:146
  42.3 0.7 copy-start.6
  60.0 8.0 %copy-start.1 = (bf16[19,1,4096]{2,0,1:T(8,128)(2,1)S(1)}, bf16[19,1,4096]{2,0,1:T(8,128)(2,1)}, u32[]{:S(2)}) copy-start(bf16[19,1,4096]{2,0,1:T(8,128)(2,1)} %param.17) | copy-start | bytes 466948
  60.0 20.0 %all-to-all-start.2 = ((bf16[96,2,200]{2,1,0:T(2,128)(2,1)}), bf16[96,2,200]{2,1,0:T(2,128)(2,1)S(1)}, u32[]{:S(2)}, u32[]{:S(2)}) async-start(bf16[96,2,200]{2,1,0:T(2,128)(2,1)} %reshape.707), calls=%async_computation.2 | async-start | bytes 196608 | tf_op jit(solution)/shard_map/all_to_all | solution.py:174
  112.0 1.3 copy-start
  114.5 1.8 %slice-start = ((f32[25,8,256]{2,1,0:T(8,128)}), f32[19,8,256]{2,1,0:T(8,128)S(1)}, s32[]{:S(2)}) async-start(f32[25,8,256]{2,1,0:T(8,128)} %copy-done), calls=%async_computation.5 | async-start | bytes 311296 | tf_op jit(solution)/shard_map/slice | solution.py:195
  117.7 13.8 %all-to-all-start.4 = ((f32[8,1,6400]{2,1,0:T(1,128)}), f32[8,1,6400]{2,1,0:T(1,128)S(1)}, u32[]{:S(2)}, u32[]{:S(2)}) async-start(f32[8,1,6400]{2,1,0:T(1,128)} %reshape.711), calls=%async_computation.4 | async-start | bytes 409600 | tf_op jit(solution)/shard_map/all_to_all | solution.py:197

commit v8 on v7

--- a/solution.py
+++ b/solution.py
@@ -147,8 +147,6 @@
         jnp.broadcast_to(by_lane[None], (cams,) + by_lane.shape), "cams", 0, 0, tiled=True
     )
     params_col = gathered.transpose(1, 2, 0, 3).reshape(params.shape[0], BLK, per_column)
-    geometry_col = params_col[:6]
-    appearance_col = params_col[6:]
     linear = cam_linear[0]
     camera_shift = cam_shift[0]
     entries = block_lists.reshape(-1)
@@ -157,6 +155,8 @@
     entry_slot = column * capacity + ranking
     request = jnp.zeros((slot_count,), jnp.int32).at[entry_slot].set(in_column)
     request, params_col = lax.optimization_barrier((request, params_col))
+    geometry_col = params_col[:6]
+    appearance_col = params_col[6:]
     wanted = lax.all_to_all(request, "tiles", split_axis=0, concat_axis=0, tiled=True)
     rows = params_col.shape[0]
     payload_col = jnp.concatenate(

time: 136 us -> 135 us (level)
    unnamed x0 -> x6, other arithmetic: none -> 3.8 us
    div x1 -> x0, other arithmetic: 2.53 us -> none  [project(): opacity = 0.95 * jax.nn.sigmoid(geometry[5])]
  transfers between devices with their start and end apart: 4 -> 4, of which waited for: 4 -> 4; matrix products, arithmetic and copies ran while one was open for 6% -> 7% of each run, Pallas kernels for 0% -> 0%
where the time goes in v8:
time: 135 us; the launch traced here: 133 us
  starting transfers between devices  38.2 us (28%)
  waiting for transfers between devices  31.7 us (23%)
  local copies, waits for them, and re-layouts  19.9 us (15%)
  blocking collectives  19.2 us (14%)
  other arithmetic  15.6 us (12%)
  matrix products  5.88 us (4%)
  between operations  2.56 us (2%)
    all_to_all x1, starting transfers between devices, local(): lax.all_to_all(request, 'tiles', split_axis=0, concat_axis=0, tiled=True)  19.4 us
    all_to_all x1, blocking collectives, local(): lax.all_to_all(back, 'tiles', split_axis=2, concat_axis=2, tiled=True)  19.2 us
    all_to_all x1, waiting for transfers between devices, local(): lax.all_to_all(send, 'tiles', split_axis=2, concat_axis=2, tiled=True)  11.9 us
    all_to_all x1, starting transfers between devices, local(): lax.all_to_all(send, 'tiles', split_axis=2, concat_axis=2, tiled=True)  8.01 us
    unnamed x36, local copies, waits for them, and re-layouts  7.81 us
    all_to_all x1, waiting for transfers between devices, local(): lax.all_to_all(column_all.reshape(rows, BLK, cams, local_blocks), 'cams',...  7.31 us
    all_to_all x1, starting transfers between devices, local(): lax.all_to_all(jnp.broadcast_to(by_lane[None], (cams,) + by_lane.shape),...  7.23 us
    all_to_all x1, waiting for transfers between devices, local(): lax.all_to_all(request, 'tiles', split_axis=0, concat_axis=0, tiled=True)  6.59 us
  transfers between devices with their start and end apart: 4, of which 4 were waited for; matrix products, arithmetic and copies ran while one was open for 7% of the time, Pallas kernels for 0%

profile of v8, /device:TPU:6, one launch (start us, length us, event | category | flops | bytes accessed | tf_op | source)
XLA Modules:
  0.0 133.1 jit_solution(11739445216375385236)
XLA Ops:
  4.1 1.0 reshape.340
  5.2 7.2 %all-to-all-start = ((f32[8,1,6400]{2,1,0:T(1,128)}), f32[8,1,6400]{2,1,0:T(1,128)S(1)}, u32[]{:S(2)}, u32[]{:S(2)}) async-start(f32[8,1,6400]{2,1,0:T(1,128)} %reshape.340), calls=%async_computation | async-start | bytes 409600 | tf_op jit(solution)/shard_map/all_to_all | solution.py:146
  17.1 5.9 %all-to-all-done = f32[8,1,6400]{2,1,0:T(1,128)S(1)} async-done(((f32[8,1,6400]{2,1,0:T(1,128)}), f32[8,1,6400]{2,1,0:T(1,128)S(1)}, u32[]{:S(2)}, u32[]{:S(2)}) %all-to-all-start) | async-done | bytes 204832 | tf_op jit(solution)/shard_map/all_to_all | solution.py:146
  23.6 1.1 reduce.4
  26.1 19.4 %all-to-all-start.1 = ((s32[96,2,1]{1,2,0:T(1,128)}), s32[96,2,1]{1,2,0:T(1,128)S(1)}, u32[]{:S(2)}, u32[]{:S(2)}) async-start(s32[96,2,1]{1,2,0:T(1,128)} %bitcast.14), calls=%async_computation.1 | async-start | bytes 98304 | tf_op jit(solution)/shard_map/all_to_all | solution.py:160
  45.5 1.2 constant_dynamic-update-slice_fusion.5
  46.7 1.3 %constant_dynamic-update-slice_fusion.4 = bf16[25,8,256]{2,1,0:T(8,128)(2,1)S(1)} fusion(bf16[25,8,256]{2,1,0:T(8,128)(2,1)S(1)} %constant_dynamic-update-slice_fusion.5, f32[25,8,256]{2,1,0:T(8,128)S(1)} %reshape.314, f32[]{:T(128)} %bitcast.13, f32[]{:T(128)} %bitcast.12, f32[]{:T(128)} %bitcast.11), kind=kLoop, calls=%fused_computation.86 | loop fusion | flops 10240 | bytes 20492
  48.0 1.3 constant_dynamic-update-slice_fusion.3
  49.4 6.6 %all-to-all-done.1 = s32[96,2,1]{1,2,0:T(1,128)S(1)} async-done(((s32[96,2,1]{1,2,0:T(1,128)}), s32[96,2,1]{1,2,0:T(1,128)S(1)}, u32[]{:S(2)}, u32[]{:S(2)}) %all-to-all-start.1) | async-done | bytes 800 | tf_op jit(solution)/shard_map/all_to_all | solution.py:160
  58.0 1.0 reshape.342
  59.0 8.0 %all-to-all-start.2 = ((bf16[96,2,200]{2,1,0:T(2,128)(2,1)}), bf16[96,2,200]{2,1,0:T(2,128)(2,1)S(1)}, u32[]{:S(2)}, u32[]{:S(2)}) async-start(bf16[96,2,200]{2,1,0:T(2,128)(2,1)} %reshape.342), calls=%async_computation.2 | async-start | bytes 196608 | tf_op jit(solution)/shard_map/all_to_all | solution.py:174
  67.1 11.9 %all-to-all-done.2 = bf16[96,2,200]{2,1,0:T(2,128)(2,1)S(1)} async-done(((bf16[96,2,200]{2,1,0:T(2,128)(2,1)}), bf16[96,2,200]{2,1,0:T(2,128)(2,1)S(1)}, u32[]{:S(2)}, u32[]{:S(2)}) %all-to-all-start.2) | async-done | bytes 76832 | tf_op jit(solution)/shard_map/all_to_all | solution.py:174
  82.2 1.8 %fusion = bf16[19,16,48]{2,0,1:T(8,128)(2,1)S(1)} fusion(f32[16,48]{1,0:T(8,128)S(1)} %mul.694, f32[16,48]{1,0:T(8,128)S(1)} %sub.109, f32[256]{0:T(256)S(1)} %get-tuple-element.59, f32[16,48]{1,0:T(8,128)S(1)} %mul.690, f32[16,48]{1,0:T(8,128)S(1)} %sub.103, f32[256]{0:T(256)S(1)} %get-tuple-element.60, f32[16,48]{1,0:T(8,128)S(1)} %mul.685, ...), kind=kOutput, calls=%fused_computation.16 | convolution fusion | flops 47790336 | bytes 991744 | tf_op jit(solution)/shard_map/transpose(jvp(vmap()))/dot_general | solution.py:97
  84.4 1.3 multiply_multiply_fusion.1
  86.7 2.9 %fusion.14 = (f32[16,48]{1,0:T(8,128)S(1)}, f32[16,48]{1,0:T(8,128)S(1)}, f32[16,48]{1,0:T(8,128)S(1)}, f32[16,48]{1,0:T(8,128)S(1)}, f32[16,48]{1,0:T(8,128)S(1)}, /*index=5*/f32[16,48]{1,0:T(8,128)S(1)}) fusion(f32[16,48]{1,0:T(8,128)S(1)} %sub.109, f32[256]{0:T(256)S(1)} %get-tuple-element.59, f32[16,48]{1,0:T(8,128)S(1)} %mul.694, ...), kind=kLoop, calls=%fused_computation.30 | loop fusion | flops 9432576 | bytes 2398208 | tf_op jit(solution)/shard_map/transpose(jvp(vmap()))/reduce_sum | solution.py:92
  90.9 19.2 %all_to_all.29 = bf16[96,2,200]{2,1,0:T(2,128)(2,1)S(1)} all-to-all(bf16[96,2,200]{2,1,0:T(2,128)(2,1)S(1)} %reshape.344), channel_id=1, replica_groups=mesh['tiles'=96,'cams'=8] {'tiles'}, dimensions={0} | all-to-all | bytes 153600 | tf_op jit(solution)/shard_map/all_to_all | solution.py:192
  111.7 1.3 multiply_add_fusion
  112.9 1.3 slice_multiply_fusion.1
  115.1 1.0 reshape.346
  116.1 3.6 %all-to-all-start.4 = ((f32[8,1,6400]{2,1,0:T(1,128)}), f32[8,1,6400]{2,1,0:T(1,128)S(1)}, u32[]{:S(2)}, u32[]{:S(2)}) async-start(f32[8,1,6400]{2,1,0:T(1,128)} %reshape.346), calls=%async_computation.4 | async-start | bytes 409600 | tf_op jit(solution)/shard_map/all_to_all | solution.py:197
  119.7 1.7 %convolution_bitcast_fusion = f32[19,16,256]{2,0,1:T(8,128)S(1)} fusion(f32[19,16,48]{0,2,1:T(8,128)S(1)} %bitcast.90, f32[16,48]{1,0:T(8,128)S(1)} %mul.694, f32[16,48]{1,0:T(8,128)S(1)} %sub.109, f32[256]{0:T(256)S(1)} %get-tuple-element.59, f32[16,48]{1,0:T(8,128)S(1)} %mul.690, f32[16,48]{1,0:T(8,128)S(1)} %sub.103, f32[256]{0:T(256)S(1)} %get-tuple-element.60, ...), kind=kOutput, calls=%fused_computation.12 | convolution fusion | flops 47775744 | bytes 1176576 | tf_op jit(solution)/shard_map/jvp(vmap())/dot_general | solution.py:97
  121.6 1.0 reshape.328
  122.6 7.3 %all-to-all-done.4 = f32[8,1,6400]{2,1,0:T(1,128)S(1)} async-done(((f32[8,1,6400]{2,1,0:T(1,128)}), f32[8,1,6400]{2,1,0:T(1,128)S(1)}, u32[]{:S(2)}, u32[]{:S(2)}) %all-to-all-start.4) | async-done | bytes 204832 | tf_op jit(solution)/shard_map/all_to_all | solution.py:197
  129.9 1.1 reduce.5
  (116 shorter events, 20.8 us)
Async XLA Ops:
  0.6 0.8 copy-start.5
  1.5 0.7 copy-start.7
  2.2 0.7 copy-start.8
  2.8 0.7 copy-start.2
  5.2 7.2 %copy-start.4 = (s32[1,16,2,3]{1,2,3,0:T(2,128)S(1)}, s32[1,16,2,3]{1,2,3,0:T(2,128)}, u32[]{:S(2)}) copy-start(s32[1,16,2,3]{1,2,3,0:T(2,128)} %param.16) | copy-start | bytes 1156
  5.2 17.9 %all-to-all-start = ((f32[8,1,6400]{2,1,0:T(1,128)}), f32[8,1,6400]{2,1,0:T(1,128)S(1)}, u32[]{:S(2)}, u32[]{:S(2)}) async-start(f32[8,1,6400]{2,1,0:T(1,128)} %reshape.340), calls=%async_computation | async-start | bytes 409600 | tf_op jit(solution)/shard_map/all_to_all | solution.py:146
  12.9 0.7 copy-start.3
  15.6 0.9 copy-start.6
  26.1 29.8 %all-to-all-start.1 = ((s32[96,2,1]{1,2,0:T(1,128)}), s32[96,2,1]{1,2,0:T(1,128)S(1)}, u32[]{:S(2)}, u32[]{:S(2)}) async-start(s32[96,2,1]{1,2,0:T(1,128)} %bitcast.14), calls=%async_computation.1 | async-start | bytes 98304 | tf_op jit(solution)/shard_map/all_to_all | solution.py:160
  59.0 8.0 %copy-start.1 = (bf16[19,1,4096]{2,0,1:T(8,128)(2,1)S(1)}, bf16[19,1,4096]{2,0,1:T(8,128)(2,1)}, u32[]{:S(2)}) copy-start(bf16[19,1,4096]{2,0,1:T(8,128)(2,1)} %param.17) | copy-start | bytes 466948
  59.0 20.0 %all-to-all-start.2 = ((bf16[96,2,200]{2,1,0:T(2,128)(2,1)}), bf16[96,2,200]{2,1,0:T(2,128)(2,1)S(1)}, u32[]{:S(2)}, u32[]{:S(2)}) async-start(bf16[96,2,200]{2,1,0:T(2,128)(2,1)} %reshape.342), calls=%async_computation.2 | async-start | bytes 196608 | tf_op jit(solution)/shard_map/all_to_all | solution.py:174
  111.0 0.7 copy-start
  112.9 1.8 %slice-start = ((f32[25,8,256]{2,1,0:T(8,128)}), f32[19,8,256]{2,1,0:T(8,128)S(1)}, s32[]{:S(2)}) async-start(f32[25,8,256]{2,1,0:T(8,128)} %copy-done), calls=%async_computation.5 | async-start | bytes 311296 | tf_op jit(solution)/shard_map/slice | solution.py:195
  116.1 13.8 %all-to-all-start.4 = ((f32[8,1,6400]{2,1,0:T(1,128)}), f32[8,1,6400]{2,1,0:T(1,128)S(1)}, u32[]{:S(2)}, u32[]{:S(2)}) async-start(f32[8,1,6400]{2,1,0:T(1,128)} %reshape.346), calls=%async_computation.4 | async-start | bytes 409600 | tf_op jit(solution)/shard_map/all_to_all | solution.py:197

commit v9 on v8

--- a/solution.py
+++ b/solution.py
@@ -113,6 +113,49 @@
     return (picture, grad_proj.reshape(6, -1), grad_colour.reshape(channels, -1))
 
 
+def tile_grads_direct(projected, colours, cotangent):
+    channels = colours.shape[0]
+    proj = projected.reshape(6, TPD, -1)
+    colour_tiles = colours.reshape(channels, TPD, -1)
+    pixels = jnp.arange(SIDE * SIDE)
+    across = (pixels % SIDE).astype(jnp.float32) + 0.5 - SIDE / 2
+    downward = (pixels // SIDE).astype(jnp.float32) + 0.5 - SIDE / 2
+    delta_x = across[None, None, :] - proj[0][..., None]
+    delta_y = downward[None, None, :] - proj[1][..., None]
+    conic_0 = proj[2][..., None]
+    conic_1 = proj[3][..., None]
+    conic_2 = proj[4][..., None]
+    quadric = (
+        conic_0 * delta_x * delta_x
+        + 2.0 * conic_1 * delta_x * delta_y
+        + conic_2 * delta_y * delta_y
+    )
+    falloff = jnp.exp(-0.5 * quadric)
+    coverage = proj[5][..., None] * falloff
+    log_keep = jnp.log1p(-coverage)
+    keep = jnp.exp(jnp.cumsum(log_keep, axis=1) - log_keep)
+    weight = keep * coverage
+    hi = lax.Precision.HIGHEST
+    picture = jnp.einsum("cti,tip->ctp", colour_tiles, weight, precision=hi)
+    grad_colour = jnp.einsum("ctp,tip->cti", cotangent, weight, precision=hi)
+    grad_weight = jnp.einsum("cti,ctp->tip", colour_tiles, cotangent, precision=hi)
+    grad_sum = grad_weight * weight
+    grad_log = jnp.sum(grad_sum, axis=1, keepdims=True) - jnp.cumsum(grad_sum, axis=1)
+    grad_cover = grad_weight * keep - grad_log / (1.0 - coverage)
+    grad_quad = -0.5 * grad_cover * coverage
+    grad_proj = jnp.stack(
+        [
+            -jnp.sum(grad_quad * (2.0 * conic_0 * delta_x + 2.0 * conic_1 * delta_y), axis=2),
+            -jnp.sum(grad_quad * (2.0 * conic_1 * delta_x + 2.0 * conic_2 * delta_y), axis=2),
+            jnp.sum(grad_quad * delta_x * delta_x, axis=2),
+            jnp.sum(2.0 * grad_quad * delta_x * delta_y, axis=2),
+            jnp.sum(grad_quad * delta_y * delta_y, axis=2),
+            jnp.sum(grad_cover * falloff, axis=2),
+        ]
+    )
+    return (picture, grad_proj.reshape(6, -1), grad_colour.reshape(channels, -1))
+
+
 def slot_ranks(entries, blocks_per_column, columns):
     column = entries // blocks_per_column
     in_column = entries % blocks_per_column
@@ -181,7 +224,7 @@
     projected = picked[:6]
     colours = picked[6:]
     cotangent = pix_grad.reshape(channels, TPD, -1).astype(jnp.float32)
-    picture, grad_proj, grad_colour = tile_grads(projected, colours, cotangent)
+    picture, grad_proj, grad_colour = tile_grads_direct(projected, colours, cotangent)
     entry_grads = jnp.concatenate([grad_proj, grad_colour], axis=0).astype(jnp.bfloat16)
     back = jnp.einsum(
         "reb,se->rbs",

time: 135 us -> 135 us (level)
    reduce_sum x1 -> x0, other arithmetic: 2.93 us -> none  [render_tile(): projected[4][:, None] * delta_y * delta_y]
    sub x1 -> x2, other arithmetic: 0.01 us -> 2.68 us  [the longest x1 2.68 us: tile_grads_direct(): jnp.sum(grad_sum, axis=1, keepdims=True) - jnp.cumsum(grad_sum, axis=1)]
    unnamed x36 -> x42, local copies, waits for them, and re-layouts: 7.81 us -> 7.85 us
where the time goes in v9:
time: 135 us; the launch traced here: 133 us
  starting transfers between devices  38.2 us (28%)
  waiting for transfers between devices  31.7 us (23%)
  local copies, waits for them, and re-layouts  20.8 us (15%)
  blocking collectives  19.2 us (14%)
  other arithmetic  14.9 us (11%)
  matrix products  5.92 us (4%)
  between operations  2.6 us (2%)
    all_to_all x1, starting transfers between devices, local(): lax.all_to_all(request, 'tiles', split_axis=0, concat_axis=0, tiled=True)  19.4 us
    all_to_all x1, blocking collectives, local(): lax.all_to_all(back, 'tiles', split_axis=2, concat_axis=2, tiled=True)  19.2 us
    all_to_all x1, waiting for transfers between devices, local(): lax.all_to_all(send, 'tiles', split_axis=2, concat_axis=2, tiled=True)  11.9 us
    all_to_all x1, starting transfers between devices, local(): lax.all_to_all(send, 'tiles', split_axis=2, concat_axis=2, tiled=True)  8.01 us
    unnamed x42, local copies, waits for them, and re-layouts  7.85 us
    all_to_all x1, waiting for transfers between devices, local(): lax.all_to_all(column_all.reshape(rows, BLK, cams, local_blocks), 'cams',...  7.27 us
    all_to_all x1, starting transfers between devices, local(): lax.all_to_all(jnp.broadcast_to(by_lane[None], (cams,) + by_lane.shape),...  7.23 us
    all_to_all x1, waiting for transfers between devices, local(): lax.all_to_all(request, 'tiles', split_axis=0, concat_axis=0, tiled=True)  6.59 us
  transfers between devices with their start and end apart: 4, of which 4 were waited for; matrix products, arithmetic and copies ran while one was open for 7% of the time, Pallas kernels for 0%

profile of v9, /device:TPU:6, one launch (start us, length us, event | category | flops | bytes accessed | tf_op | source)
XLA Modules:
  0.0 133.3 jit_solution(4488139363661590495)
XLA Ops:
  4.1 1.0 reshape.353
  5.2 7.2 %all-to-all-start = ((f32[8,1,6400]{2,1,0:T(1,128)}), f32[8,1,6400]{2,1,0:T(1,128)S(1)}, u32[]{:S(2)}, u32[]{:S(2)}) async-start(f32[8,1,6400]{2,1,0:T(1,128)} %reshape.353), calls=%async_computation | async-start | bytes 409600 | tf_op jit(solution)/shard_map/all_to_all | solution.py:189
  17.1 5.9 %all-to-all-done = f32[8,1,6400]{2,1,0:T(1,128)S(1)} async-done(((f32[8,1,6400]{2,1,0:T(1,128)}), f32[8,1,6400]{2,1,0:T(1,128)S(1)}, u32[]{:S(2)}, u32[]{:S(2)}) %all-to-all-start) | async-done | bytes 204832 | tf_op jit(solution)/shard_map/all_to_all | solution.py:189
  23.6 1.1 reduce.4
  26.1 19.4 %all-to-all-start.1 = ((s32[96,2,1]{1,2,0:T(1,128)}), s32[96,2,1]{1,2,0:T(1,128)S(1)}, u32[]{:S(2)}, u32[]{:S(2)}) async-start(s32[96,2,1]{1,2,0:T(1,128)} %bitcast.14), calls=%async_computation.1 | async-start | bytes 98304 | tf_op jit(solution)/shard_map/all_to_all | solution.py:203
  45.5 1.2 constant_dynamic-update-slice_fusion.5
  46.7 1.3 %constant_dynamic-update-slice_fusion.4 = bf16[25,8,256]{2,1,0:T(8,128)(2,1)S(1)} fusion(bf16[25,8,256]{2,1,0:T(8,128)(2,1)S(1)} %constant_dynamic-update-slice_fusion.5, f32[25,8,256]{2,1,0:T(8,128)S(1)} %reshape.327, f32[]{:T(128)} %bitcast.13, f32[]{:T(128)} %bitcast.12, f32[]{:T(128)} %bitcast.11), kind=kLoop, calls=%fused_computation.74 | loop fusion | flops 10240 | bytes 20492
  48.0 1.3 constant_dynamic-update-slice_fusion.3
  49.4 6.6 %all-to-all-done.1 = s32[96,2,1]{1,2,0:T(1,128)S(1)} async-done(((s32[96,2,1]{1,2,0:T(1,128)}), s32[96,2,1]{1,2,0:T(1,128)S(1)}, u32[]{:S(2)}, u32[]{:S(2)}) %all-to-all-start.1) | async-done | bytes 800 | tf_op jit(solution)/shard_map/all_to_all | solution.py:203
  58.0 1.0 reshape.355
  59.0 8.0 %all-to-all-start.2 = ((bf16[96,2,200]{2,1,0:T(2,128)(2,1)}), bf16[96,2,200]{2,1,0:T(2,128)(2,1)S(1)}, u32[]{:S(2)}, u32[]{:S(2)}) async-start(bf16[96,2,200]{2,1,0:T(2,128)(2,1)} %reshape.355), calls=%async_computation.2 | async-start | bytes 196608 | tf_op jit(solution)/shard_map/all_to_all | solution.py:217
  67.1 11.9 %all-to-all-done.2 = bf16[96,2,200]{2,1,0:T(2,128)(2,1)S(1)} async-done(((bf16[96,2,200]{2,1,0:T(2,128)(2,1)}), bf16[96,2,200]{2,1,0:T(2,128)(2,1)S(1)}, u32[]{:S(2)}, u32[]{:S(2)}) %all-to-all-start.2) | async-done | bytes 76832 | tf_op jit(solution)/shard_map/all_to_all | solution.py:217
  82.2 1.8 %fusion.4 = bf16[19,16,48]{2,0,1:T(8,128)(2,1)S(1)} fusion(bf16[19,16,256]{2,1,0:T(8,128)(2,1)S(1)} %slice.192, f32[16,48]{1,0:T(8,128)S(1)} %mul.701, f32[16,48]{1,0:T(8,128)S(1)} %sub.126, f32[256]{0:T(256)S(1)} %get-tuple-element.59, f32[16,48]{1,0:T(8,128)S(1)} %mul.697, f32[16,48]{1,0:T(8,128)S(1)} %sub.120, f32[256]{0:T(256)S(1)} %get-tuple-element.60, ...), kind=kOutput, calls=%fused_computation.24 | convolution fusion | flops 47790336 | bytes 991744 | tf_op jit(solution)/shard_map/ctp,tip->cti/dot_general | solution.py:140
  84.4 1.3 %fusion.52 = (f32[16,48,256]{2,1,0:T(8,128)S(1)}, f32[16,48,256]{2,1,0:T(8,128)S(1)}) fusion(f32[16,48]{1,0:T(8,128)S(1)} %mul.701, f32[16,48]{1,0:T(8,128)S(1)} %sub.126, f32[256]{0:T(256)S(1)} %get-tuple-element.59, f32[16,48]{1,0:T(8,128)S(1)} %mul.697, f32[16,48]{1,0:T(8,128)S(1)} %sub.120, f32[256]{0:T(256)S(1)} %get-tuple-element.60, ...), kind=kOutput, calls=%fused_computation.151 | convolution fusion | flops 47972352 | bytes 2593792 | tf_op jit(solution)/shard_map/cti,ctp->tip/dot_general | solution.py:141
  86.3 2.7 %fusion.17 = (bf16[16,48]{1,0:T(8,128)(2,1)S(1)}, bf16[16,48]{1,0:T(8,128)(2,1)S(1)}, f32[16,48]{1,0:T(8,128)S(1)}, bf16[16,48]{1,0:T(8,128)(2,1)S(1)}, f32[16,48]{1,0:T(8,128)S(1)}, /*index=5*/bf16[16,48]{1,0:T(8,128)(2,1)S(1)}) fusion(f32[16,48]{1,0:T(8,128)S(1)} %sub.126, f32[256]{0:T(256)S(1)} %get-tuple-element.59, f32[16,48]{1,0:T(8,128)S(1)} %mul.701, ...), kind=kOutput, calls=%fused_computation.37 | output fusion | flops 8257071 | bytes 3184640 | tf_op jit(solution)/shard_map/sub | solution.py:143
  91.1 19.2 %all_to_all.29 = bf16[96,2,200]{2,1,0:T(2,128)(2,1)S(1)} all-to-all(bf16[96,2,200]{2,1,0:T(2,128)(2,1)S(1)} %reshape.357), channel_id=1, replica_groups=mesh['tiles'=96,'cams'=8] {'tiles'}, dimensions={0} | all-to-all | bytes 153600 | tf_op jit(solution)/shard_map/all_to_all | solution.py:235
  111.9 1.3 multiply_add_fusion
  113.1 1.3 slice_multiply_fusion.1
  115.3 1.0 reshape.359
  116.3 3.6 %all-to-all-start.4 = ((f32[8,1,6400]{2,1,0:T(1,128)}), f32[8,1,6400]{2,1,0:T(1,128)S(1)}, u32[]{:S(2)}, u32[]{:S(2)}) async-start(f32[8,1,6400]{2,1,0:T(1,128)} %reshape.359), calls=%async_computation.4 | async-start | bytes 409600 | tf_op jit(solution)/shard_map/all_to_all | solution.py:240
  119.9 1.8 %convolution_bitcast_fusion = f32[19,16,256]{2,0,1:T(8,128)S(1)} fusion(f32[19,16,48]{0,2,1:T(8,128)S(1)} %bitcast.76, f32[16,48]{1,0:T(8,128)S(1)} %mul.701, f32[16,48]{1,0:T(8,128)S(1)} %sub.126, f32[256]{0:T(256)S(1)} %get-tuple-element.59, f32[16,48]{1,0:T(8,128)S(1)} %mul.697, f32[16,48]{1,0:T(8,128)S(1)} %sub.120, f32[256]{0:T(256)S(1)} %get-tuple-element.60, ...), kind=kOutput, calls=%fused_computation.20 | convolution fusion | flops 47775744 | bytes 1176576 | tf_op jit(solution)/shard_map/cti,tip->ctp/dot_general | solution.py:139
  121.8 1.0 reshape.341
  122.9 7.3 %all-to-all-done.4 = f32[8,1,6400]{2,1,0:T(1,128)S(1)} async-done(((f32[8,1,6400]{2,1,0:T(1,128)}), f32[8,1,6400]{2,1,0:T(1,128)S(1)}, u32[]{:S(2)}, u32[]{:S(2)}) %all-to-all-start.4) | async-done | bytes 204832 | tf_op jit(solution)/shard_map/all_to_all | solution.py:240
  130.1 1.1 reduce.5
  (132 shorter events, 21.2 us)
Async XLA Ops:
  0.6 0.8 copy-start.5
  1.5 0.7 copy-start.7
  2.2 0.7 copy-start.8
  2.8 0.7 copy-start.2
  5.2 7.2 %copy-start.4 = (s32[1,16,2,3]{1,2,3,0:T(2,128)S(1)}, s32[1,16,2,3]{1,2,3,0:T(2,128)}, u32[]{:S(2)}) copy-start(s32[1,16,2,3]{1,2,3,0:T(2,128)} %param.16) | copy-start | bytes 1156
  5.2 17.9 %all-to-all-start = ((f32[8,1,6400]{2,1,0:T(1,128)}), f32[8,1,6400]{2,1,0:T(1,128)S(1)}, u32[]{:S(2)}, u32[]{:S(2)}) async-start(f32[8,1,6400]{2,1,0:T(1,128)} %reshape.353), calls=%async_computation | async-start | bytes 409600 | tf_op jit(solution)/shard_map/all_to_all | solution.py:189
  12.9 0.7 copy-start.3
  15.6 0.9 copy-start.6
  26.1 29.8 %all-to-all-start.1 = ((s32[96,2,1]{1,2,0:T(1,128)}), s32[96,2,1]{1,2,0:T(1,128)S(1)}, u32[]{:S(2)}, u32[]{:S(2)}) async-start(s32[96,2,1]{1,2,0:T(1,128)} %bitcast.14), calls=%async_computation.1 | async-start | bytes 98304 | tf_op jit(solution)/shard_map/all_to_all | solution.py:203
  59.0 8.0 %copy-start.1 = (bf16[19,1,4096]{2,0,1:T(8,128)(2,1)S(1)}, bf16[19,1,4096]{2,0,1:T(8,128)(2,1)}, u32[]{:S(2)}) copy-start(bf16[19,1,4096]{2,0,1:T(8,128)(2,1)} %param.17) | copy-start | bytes 466948
  59.0 20.0 %all-to-all-start.2 = ((bf16[96,2,200]{2,1,0:T(2,128)(2,1)}), bf16[96,2,200]{2,1,0:T(2,128)(2,1)S(1)}, u32[]{:S(2)}, u32[]{:S(2)}) async-start(bf16[96,2,200]{2,1,0:T(2,128)(2,1)} %reshape.355), calls=%async_computation.2 | async-start | bytes 196608 | tf_op jit(solution)/shard_map/all_to_all | solution.py:217
  111.2 0.7 copy-start
  113.1 1.8 %slice-start = ((f32[25,8,256]{2,1,0:T(8,128)}), f32[19,8,256]{2,1,0:T(8,128)S(1)}, s32[]{:S(2)}) async-start(f32[25,8,256]{2,1,0:T(8,128)} %copy-done), calls=%async_computation.5 | async-start | bytes 311296 | tf_op jit(solution)/shard_map/slice | solution.py:238
  116.3 13.8 %all-to-all-start.4 = ((f32[8,1,6400]{2,1,0:T(1,128)}), f32[8,1,6400]{2,1,0:T(1,128)S(1)}, u32[]{:S(2)}, u32[]{:S(2)}) async-start(f32[8,1,6400]{2,1,0:T(1,128)} %reshape.359), calls=%async_computation.4 | async-start | bytes 409600 | tf_op jit(solution)/shard_map/all_to_all | solution.py:240

commit v10 on v8

--- a/solution.py
+++ b/solution.py
@@ -196,10 +196,13 @@
     column_all = jnp.concatenate([column_geometry, column_colour], axis=0)
     grads = lax.all_to_all(
         column_all.reshape(rows, BLK, cams, local_blocks), "cams", 2, 2, tiled=True
-    ).sum(axis=2)
-    grads = grads.transpose(0, 2, 1).reshape(rows, local_blocks * BLK)
-    grad_geometry = grads[:6]
-    grad_appearance = grads[6:]
+    )
+
+    def finish(part):
+        return part.sum(axis=2).transpose(0, 2, 1).reshape(part.shape[0], local_blocks * BLK)
+
+    grad_geometry = finish(grads[:6])
+    grad_appearance = finish(grads[6:])
     return (picture.reshape(channels, 1, -1), grad_geometry, grad_appearance)
 
 

time: 135 us -> 135 us (level)
  no operation moved by 1% of the time
where the time goes in v10:
time: 135 us; the launch traced here: 133 us
  starting transfers between devices  38.2 us (28%)
  waiting for transfers between devices  31.7 us (23%)
  local copies, waits for them, and re-layouts  19.9 us (15%)
  blocking collectives  19.2 us (14%)
  other arithmetic  15.6 us (12%)
  matrix products  5.88 us (4%)
  between operations  2.55 us (2%)
    all_to_all x1, starting transfers between devices, local(): lax.all_to_all(request, 'tiles', split_axis=0, concat_axis=0, tiled=True)  19.4 us
    all_to_all x1, blocking collectives, local(): lax.all_to_all(back, 'tiles', split_axis=2, concat_axis=2, tiled=True)  19.2 us
    all_to_all x1, waiting for transfers between devices, local(): lax.all_to_all(send, 'tiles', split_axis=2, concat_axis=2, tiled=True)  11.9 us
    all_to_all x1, starting transfers between devices, local(): lax.all_to_all(send, 'tiles', split_axis=2, concat_axis=2, tiled=True)  8.01 us
    unnamed x36, local copies, waits for them, and re-layouts  7.81 us
    all_to_all x1, waiting for transfers between devices, local(): lax.all_to_all(column_all.reshape(rows, BLK, cams, local_blocks), 'cams',...  7.31 us
    all_to_all x1, starting transfers between devices, local(): lax.all_to_all(jnp.broadcast_to(by_lane[None], (cams,) + by_lane.shape),...  7.23 us
    all_to_all x1, waiting for transfers between devices, local(): lax.all_to_all(request, 'tiles', split_axis=0, concat_axis=0, tiled=True)  6.59 us
  transfers between devices with their start and end apart: 4, of which 4 were waited for; matrix products, arithmetic and copies ran while one was open for 7% of the time, Pallas kernels for 0%

profile of v10, /device:TPU:6, one launch (start us, length us, event | category | flops | bytes accessed | tf_op | source)
XLA Modules:
  0.0 133.0 jit_solution(118582039243183096)
XLA Ops:
  4.1 1.0 reshape.345
  5.2 7.2 %all-to-all-start = ((f32[8,1,6400]{2,1,0:T(1,128)}), f32[8,1,6400]{2,1,0:T(1,128)S(1)}, u32[]{:S(2)}, u32[]{:S(2)}) async-start(f32[8,1,6400]{2,1,0:T(1,128)} %reshape.345), calls=%async_computation | async-start | bytes 409600 | tf_op jit(solution)/shard_map/all_to_all | solution.py:146
  17.1 5.9 %all-to-all-done = f32[8,1,6400]{2,1,0:T(1,128)S(1)} async-done(((f32[8,1,6400]{2,1,0:T(1,128)}), f32[8,1,6400]{2,1,0:T(1,128)S(1)}, u32[]{:S(2)}, u32[]{:S(2)}) %all-to-all-start) | async-done | bytes 204832 | tf_op jit(solution)/shard_map/all_to_all | solution.py:146
  23.6 1.1 reduce.4
  26.1 19.4 %all-to-all-start.1 = ((s32[96,2,1]{1,2,0:T(1,128)}), s32[96,2,1]{1,2,0:T(1,128)S(1)}, u32[]{:S(2)}, u32[]{:S(2)}) async-start(s32[96,2,1]{1,2,0:T(1,128)} %bitcast.14), calls=%async_computation.1 | async-start | bytes 98304 | tf_op jit(solution)/shard_map/all_to_all | solution.py:160
  45.5 1.2 constant_dynamic-update-slice_fusion.5
  46.7 1.3 %constant_dynamic-update-slice_fusion.4 = bf16[25,8,256]{2,1,0:T(8,128)(2,1)S(1)} fusion(bf16[25,8,256]{2,1,0:T(8,128)(2,1)S(1)} %constant_dynamic-update-slice_fusion.5, f32[25,8,256]{2,1,0:T(8,128)S(1)} %reshape.317, f32[]{:T(128)} %bitcast.13, f32[]{:T(128)} %bitcast.12, f32[]{:T(128)} %bitcast.11), kind=kLoop, calls=%fused_computation.88 | loop fusion | flops 10240 | bytes 20492
  48.0 1.3 constant_dynamic-update-slice_fusion.3
  49.4 6.6 %all-to-all-done.1 = s32[96,2,1]{1,2,0:T(1,128)S(1)} async-done(((s32[96,2,1]{1,2,0:T(1,128)}), s32[96,2,1]{1,2,0:T(1,128)S(1)}, u32[]{:S(2)}, u32[]{:S(2)}) %all-to-all-start.1) | async-done | bytes 800 | tf_op jit(solution)/shard_map/all_to_all | solution.py:160
  58.0 1.0 reshape.347
  59.0 8.0 %all-to-all-start.2 = ((bf16[96,2,200]{2,1,0:T(2,128)(2,1)}), bf16[96,2,200]{2,1,0:T(2,128)(2,1)S(1)}, u32[]{:S(2)}, u32[]{:S(2)}) async-start(bf16[96,2,200]{2,1,0:T(2,128)(2,1)} %reshape.347), calls=%async_computation.2 | async-start | bytes 196608 | tf_op jit(solution)/shard_map/all_to_all | solution.py:174
  67.1 11.9 %all-to-all-done.2 = bf16[96,2,200]{2,1,0:T(2,128)(2,1)S(1)} async-done(((bf16[96,2,200]{2,1,0:T(2,128)(2,1)}), bf16[96,2,200]{2,1,0:T(2,128)(2,1)S(1)}, u32[]{:S(2)}, u32[]{:S(2)}) %all-to-all-start.2) | async-done | bytes 76832 | tf_op jit(solution)/shard_map/all_to_all | solution.py:174
  82.2 1.8 %fusion = bf16[19,16,48]{2,0,1:T(8,128)(2,1)S(1)} fusion(f32[16,48]{1,0:T(8,128)S(1)} %mul.694, f32[16,48]{1,0:T(8,128)S(1)} %sub.109, f32[256]{0:T(256)S(1)} %get-tuple-element.59, f32[16,48]{1,0:T(8,128)S(1)} %mul.690, f32[16,48]{1,0:T(8,128)S(1)} %sub.103, f32[256]{0:T(256)S(1)} %get-tuple-element.60, f32[16,48]{1,0:T(8,128)S(1)} %mul.685, ...), kind=kOutput, calls=%fused_computation.16 | convolution fusion | flops 47790336 | bytes 991744 | tf_op jit(solution)/shard_map/transpose(jvp(vmap()))/dot_general | solution.py:97
  84.4 1.3 multiply_multiply_fusion.1
  86.7 2.9 %fusion.14 = (f32[16,48]{1,0:T(8,128)S(1)}, f32[16,48]{1,0:T(8,128)S(1)}, f32[16,48]{1,0:T(8,128)S(1)}, f32[16,48]{1,0:T(8,128)S(1)}, f32[16,48]{1,0:T(8,128)S(1)}, /*index=5*/f32[16,48]{1,0:T(8,128)S(1)}) fusion(f32[16,48]{1,0:T(8,128)S(1)} %sub.109, f32[256]{0:T(256)S(1)} %get-tuple-element.59, f32[16,48]{1,0:T(8,128)S(1)} %mul.694, ...), kind=kLoop, calls=%fused_computation.30 | loop fusion | flops 9432576 | bytes 2398208 | tf_op jit(solution)/shard_map/transpose(jvp(vmap()))/reduce_sum | solution.py:92
  90.9 19.2 %all_to_all.29 = bf16[96,2,200]{2,1,0:T(2,128)(2,1)S(1)} all-to-all(bf16[96,2,200]{2,1,0:T(2,128)(2,1)S(1)} %reshape.349), channel_id=1, replica_groups=mesh['tiles'=96,'cams'=8] {'tiles'}, dimensions={0} | all-to-all | bytes 153600 | tf_op jit(solution)/shard_map/all_to_all | solution.py:192
  111.7 1.3 multiply_add_fusion
  112.9 1.3 slice_multiply_fusion.1
  115.1 1.0 reshape.351
  116.1 3.6 %all-to-all-start.4 = ((f32[8,1,6400]{2,1,0:T(1,128)}), f32[8,1,6400]{2,1,0:T(1,128)S(1)}, u32[]{:S(2)}, u32[]{:S(2)}) async-start(f32[8,1,6400]{2,1,0:T(1,128)} %reshape.351), calls=%async_computation.4 | async-start | bytes 409600 | tf_op jit(solution)/shard_map/all_to_all | solution.py:197
  119.7 1.7 %convolution_bitcast_fusion = f32[19,16,256]{2,0,1:T(8,128)S(1)} fusion(f32[19,16,48]{0,2,1:T(8,128)S(1)} %bitcast.90, f32[16,48]{1,0:T(8,128)S(1)} %mul.694, f32[16,48]{1,0:T(8,128)S(1)} %sub.109, f32[256]{0:T(256)S(1)} %get-tuple-element.59, f32[16,48]{1,0:T(8,128)S(1)} %mul.690, f32[16,48]{1,0:T(8,128)S(1)} %sub.103, f32[256]{0:T(256)S(1)} %get-tuple-element.60, ...), kind=kOutput, calls=%fused_computation.12 | convolution fusion | flops 47775744 | bytes 1176576 | tf_op jit(solution)/shard_map/jvp(vmap())/dot_general | solution.py:97
  121.6 1.0 reshape.333
  122.6 7.3 %all-to-all-done.4 = f32[8,1,6400]{2,1,0:T(1,128)S(1)} async-done(((f32[8,1,6400]{2,1,0:T(1,128)}), f32[8,1,6400]{2,1,0:T(1,128)S(1)}, u32[]{:S(2)}, u32[]{:S(2)}) %all-to-all-start.4) | async-done | bytes 204832 | tf_op jit(solution)/shard_map/all_to_all | solution.py:197
  129.9 1.1 reduce.5
  (115 shorter events, 20.8 us)
Async XLA Ops:
  0.6 0.8 copy-start.5
  1.5 0.7 copy-start.7
  2.2 0.7 copy-start.8
  2.8 0.7 copy-start.2
  5.2 7.2 %copy-start.4 = (s32[1,16,2,3]{1,2,3,0:T(2,128)S(1)}, s32[1,16,2,3]{1,2,3,0:T(2,128)}, u32[]{:S(2)}) copy-start(s32[1,16,2,3]{1,2,3,0:T(2,128)} %param.16) | copy-start | bytes 1156
  5.2 17.9 %all-to-all-start = ((f32[8,1,6400]{2,1,0:T(1,128)}), f32[8,1,6400]{2,1,0:T(1,128)S(1)}, u32[]{:S(2)}, u32[]{:S(2)}) async-start(f32[8,1,6400]{2,1,0:T(1,128)} %reshape.345), calls=%async_computation | async-start | bytes 409600 | tf_op jit(solution)/shard_map/all_to_all | solution.py:146
  12.9 0.7 copy-start.3
  15.6 0.9 copy-start.6
  26.1 29.8 %all-to-all-start.1 = ((s32[96,2,1]{1,2,0:T(1,128)}), s32[96,2,1]{1,2,0:T(1,128)S(1)}, u32[]{:S(2)}, u32[]{:S(2)}) async-start(s32[96,2,1]{1,2,0:T(1,128)} %bitcast.14), calls=%async_computation.1 | async-start | bytes 98304 | tf_op jit(solution)/shard_map/all_to_all | solution.py:160
  59.0 8.0 %copy-start.1 = (bf16[19,1,4096]{2,0,1:T(8,128)(2,1)S(1)}, bf16[19,1,4096]{2,0,1:T(8,128)(2,1)}, u32[]{:S(2)}) copy-start(bf16[19,1,4096]{2,0,1:T(8,128)(2,1)} %param.17) | copy-start | bytes 466948
  59.0 20.0 %all-to-all-start.2 = ((bf16[96,2,200]{2,1,0:T(2,128)(2,1)}), bf16[96,2,200]{2,1,0:T(2,128)(2,1)S(1)}, u32[]{:S(2)}, u32[]{:S(2)}) async-start(bf16[96,2,200]{2,1,0:T(2,128)(2,1)} %reshape.347), calls=%async_computation.2 | async-start | bytes 196608 | tf_op jit(solution)/shard_map/all_to_all | solution.py:174
  111.0 0.7 copy-start
  112.9 1.8 %slice-start = ((f32[25,8,256]{2,1,0:T(8,128)}), f32[19,8,256]{2,1,0:T(8,128)S(1)}, s32[]{:S(2)}) async-start(f32[25,8,256]{2,1,0:T(8,128)} %copy-done), calls=%async_computation.5 | async-start | bytes 311296 | tf_op jit(solution)/shard_map/slice | solution.py:195
  116.1 13.8 %all-to-all-start.4 = ((f32[8,1,6400]{2,1,0:T(1,128)}), f32[8,1,6400]{2,1,0:T(1,128)S(1)}, u32[]{:S(2)}, u32[]{:S(2)}) async-start(f32[8,1,6400]{2,1,0:T(1,128)} %reshape.351), calls=%async_computation.4 | async-start | bytes 409600 | tf_op jit(solution)/shard_map/all_to_all | solution.py:197

commit v11 on v8

--- a/solution.py
+++ b/solution.py
@@ -189,9 +189,31 @@
         slot_hot,
         preferred_element_type=jnp.float32,
     ).astype(jnp.bfloat16)
+    unit = jnp.eye(6, dtype=jnp.float32)[:, :, None, None]
+    ones = jnp.ones_like(geometry_col[0])
+    coeffs = jnp.stack(
+        [project_pullback(geometry_col, linear, unit[k] * ones)[2:5] for k in (2, 3, 4)]
+    )
+    slope = project_pullback(geometry_col, linear, unit[5] * ones)[5]
+    back, coeffs, slope = lax.optimization_barrier((back, coeffs, slope))
     returned = lax.all_to_all(back, "tiles", split_axis=2, concat_axis=2, tiled=True)
     summed = jnp.einsum("rbs,ks->rbk", returned, owner_hot, preferred_element_type=jnp.float32)
-    column_geometry = project_pullback(geometry_col, linear, summed[:6])
+    lin_xx = 1.0 + linear[0]
+    lin_yy = 1.0 + linear[3]
+    conic_rows = coeffs[0] * summed[2] + coeffs[1] * summed[3] + coeffs[2] * summed[4]
+    column_geometry = jnp.concatenate(
+        [
+            jnp.stack(
+                [
+                    summed[0] * lin_xx + summed[1] * linear[2],
+                    summed[0] * linear[1] + summed[1] * lin_yy,
+                ]
+            ),
+            conic_rows,
+            (summed[5] * slope)[None],
+        ],
+        axis=0,
+    )
     column_colour = summed[6:]
     column_all = jnp.concatenate([column_geometry, column_colour], axis=0)
     grads = lax.all_to_all(

time: 135 us -> 143 us (1.059)
  blocking collectives: 19.2 us -> 0 us
  starting transfers between devices: 38.2 us -> 51.3 us
  other arithmetic: 15.6 us -> 23.2 us
  waiting for transfers between devices: 31.7 us -> 35.9 us
  local copies, waits for them, and re-layouts: 19.9 us -> 21.4 us
    all_to_all x1 -> x0, blocking collectives: 19.2 us -> none  [local(): lax.all_to_all(back, 'tiles', split_axis=2, concat_axis=2, tiled=True)]
    all_to_all x0 -> x1, waiting for transfers between devices: none -> 11.7 us  [local(): lax.all_to_all(back, 'tiles', split_axis=2, concat_axis=2, tiled=True)]
    all_to_all x0 -> x1, starting transfers between devices: none -> 7.87 us  [local(): lax.all_to_all(back, 'tiles', split_axis=2, concat_axis=2, tiled=True)]
    add x1 -> x3, other arithmetic: 1.27 us -> 8.17 us  [the longest x2 8.14 us: project_pullback(): 2.0 * g_cov_xx * diag_x + g_cov_xy * lower]
    all_to_all x1, waiting for transfers between devices: 6.59 us -> 0.01 us  [local(): lax.all_to_all(request, 'tiles', split_axis=0, concat_axis=0, tiled=True)]
    all_to_all x1, starting transfers between devices: 8.01 us -> 13.3 us  [local(): lax.all_to_all(send, 'tiles', split_axis=2, concat_axis=2, tiled=True)]
    unnamed x36 -> x34, local copies, waits for them, and re-layouts: 7.81 us -> 7.87 us
  transfers between devices with their start and end apart: 4 -> 5, of which waited for: 4 -> 4; matrix products, arithmetic and copies ran while one was open for 7% -> 14% of each run, Pallas kernels for 0% -> 0%
where the time goes in v11:
time: 143 us; the launch traced here: 141 us
  starting transfers between devices  51.3 us (36%)
  waiting for transfers between devices  35.9 us (25%)
  other arithmetic  23.2 us (16%)
  local copies, waits for them, and re-layouts  21.4 us (15%)
  matrix products  5.87 us (4%)
  between operations  3.27 us (2%)
    all_to_all x1, starting transfers between devices, local(): lax.all_to_all(request, 'tiles', split_axis=0, concat_axis=0, tiled=True)  19.4 us
    all_to_all x1, starting transfers between devices, local(): lax.all_to_all(send, 'tiles', split_axis=2, concat_axis=2, tiled=True)  13.3 us
    all_to_all x1, waiting for transfers between devices, local(): lax.all_to_all(send, 'tiles', split_axis=2, concat_axis=2, tiled=True)  11.9 us
    all_to_all x1, waiting for transfers between devices, local(): lax.all_to_all(back, 'tiles', split_axis=2, concat_axis=2, tiled=True)  11.7 us
    add x2, other arithmetic, project_pullback(): 2.0 * g_cov_xx * diag_x + g_cov_xy * lower  8.14 us
    all_to_all x1, starting transfers between devices, local(): lax.all_to_all(back, 'tiles', split_axis=2, concat_axis=2, tiled=True)  7.87 us
    unnamed x34, local copies, waits for them, and re-layouts  7.87 us
    all_to_all x1, waiting for transfers between devices, local(): lax.all_to_all(column_all.reshape(rows, BLK, cams, local_blocks), 'cams',...  7.28 us
  transfers between devices with their start and end apart: 5, of which 4 were waited for; matrix products, arithmetic and copies ran while one was open for 14% of the time, Pallas kernels for 0%

profile of v11, /device:TPU:6, one launch (start us, length us, event | category | flops | bytes accessed | tf_op | source)
XLA Modules:
  0.0 140.9 jit_solution(7516088985416795377)
XLA Ops:
  5.2 7.2 %all-to-all-start = ((f32[8,1,6400]{2,1,0:T(1,128)}), f32[8,1,6400]{2,1,0:T(1,128)S(1)}, u32[]{:S(2)}, u32[]{:S(2)}) async-start(f32[8,1,6400]{2,1,0:T(1,128)} %reshape.403), calls=%async_computation | async-start | bytes 409600 | tf_op jit(solution)/shard_map/all_to_all | solution.py:146
  18.1 5.0 %all-to-all-done = f32[8,1,6400]{2,1,0:T(1,128)S(1)} async-done(((f32[8,1,6400]{2,1,0:T(1,128)}), f32[8,1,6400]{2,1,0:T(1,128)S(1)}, u32[]{:S(2)}, u32[]{:S(2)}) %all-to-all-start) | async-done | bytes 204832 | tf_op jit(solution)/shard_map/all_to_all | solution.py:146
  23.6 1.1 reduce.4
  26.1 19.4 %all-to-all-start.1 = ((s32[96,2,1]{1,2,0:T(1,128)}), s32[96,2,1]{1,2,0:T(1,128)S(1)}, u32[]{:S(2)}, u32[]{:S(2)}) async-start(s32[96,2,1]{1,2,0:T(1,128)} %bitcast.14), calls=%async_computation.1 | async-start | bytes 98304 | tf_op jit(solution)/shard_map/all_to_all | solution.py:160
  45.5 1.2 constant_dynamic-update-slice_fusion.5
  46.7 1.3 constant_dynamic-update-slice_fusion.4
  48.1 3.2 %multiply_add_fusion.14 = (f32[1,8,256]{2,1,0:T(8,128)S(1)}, f32[1,8,256]{2,1,0:T(8,128)S(1)}, f32[1,8,256]{2,1,0:T(8,128)S(1)}, f32[1,8,256]{2,1,0:T(8,128)S(1)...) fusion(f32[25,8,256]{2,1,0:T(8,128)S(1)} %reshape.372, f32[]{:T(128)} %bitcast.11, ...), kind=kLoop, calls=%fused_computation.119 | loop fusion | flops 145408 | bytes 81948 | tf_op jit(solution)/shard_map/add | solution.py:75
  51.3 5.0 %multiply_add_fusion.9 = (f32[1,8,256]{2,1,0:T(8,128)S(1)}, f32[1,8,256]{2,1,0:T(8,128)S(1)}, f32[1,8,256]{2,1,0:T(8,128)S(1)}, f32[1,8,256]{2,1,0:T(8,128)S(1)}...) fusion(f32[25,8,256]{2,1,0:T(8,128)S(1)} %reshape.372, ...), kind=kLoop, calls=%fused_computation.110 | loop fusion | flops 180224 | bytes 122924 | tf_op jit(solution)/shard_map/add | solution.py:75
  56.3 1.3 slice_multiply_fusion.2
  57.6 1.3 slice_multiply_fusion
  60.8 1.0 reshape.405
  61.9 13.3 %all-to-all-start.2 = ((bf16[96,2,200]{2,1,0:T(2,128)(2,1)}), bf16[96,2,200]{2,1,0:T(2,128)(2,1)S(1)}, u32[]{:S(2)}, u32[]{:S(2)}) async-start(bf16[96,2,200]{2,1,0:T(2,128)(2,1)} %reshape.405), calls=%async_computation.2 | async-start | bytes 196608 | tf_op jit(solution)/shard_map/all_to_all | solution.py:174
  75.2 11.9 %all-to-all-done.2 = bf16[96,2,200]{2,1,0:T(2,128)(2,1)S(1)} async-done(((bf16[96,2,200]{2,1,0:T(2,128)(2,1)}), bf16[96,2,200]{2,1,0:T(2,128)(2,1)S(1)}, u32[]{:S(2)}, u32[]{:S(2)}) %all-to-all-start.2) | async-done | bytes 76832 | tf_op jit(solution)/shard_map/all_to_all | solution.py:174
  90.3 1.8 %fusion = bf16[19,16,48]{2,0,1:T(8,128)(2,1)S(1)} fusion(f32[16,48]{1,0:T(8,128)S(1)} %mul.1325, f32[16,48]{1,0:T(8,128)S(1)} %sub.164, f32[256]{0:T(256)S(1)} %get-tuple-element.96, f32[16,48]{1,0:T(8,128)S(1)} %mul.1321, f32[16,48]{1,0:T(8,128)S(1)} %sub.158, f32[256]{0:T(256)S(1)} %get-tuple-element.97, f32[16,48]{1,0:T(8,128)S(1)} %mul.1316, ...), kind=kOutput, calls=%fused_computation.16 | convolution fusion | flops 47790336 | bytes 991744 | tf_op jit(solution)/shard_map/transpose(jvp(vmap()))/dot_general | solution.py:97
  92.5 1.3 multiply_multiply_fusion.1
  94.8 2.9 %fusion.14 = (f32[16,48]{1,0:T(8,128)S(1)}, f32[16,48]{1,0:T(8,128)S(1)}, f32[16,48]{1,0:T(8,128)S(1)}, f32[16,48]{1,0:T(8,128)S(1)}, f32[16,48]{1,0:T(8,128)S(1)}, /*index=5*/f32[16,48]{1,0:T(8,128)S(1)}) fusion(f32[16,48]{1,0:T(8,128)S(1)} %sub.164, f32[256]{0:T(256)S(1)} %get-tuple-element.96, f32[16,48]{1,0:T(8,128)S(1)} %mul.1325, ...), kind=kLoop, calls=%fused_computation.30 | loop fusion | flops 9432576 | bytes 2398208 | tf_op jit(solution)/shard_map/transpose(jvp(vmap()))/reduce_sum | solution.py:92
  98.6 1.0 reshape.407
  99.6 7.9 %all-to-all-start.3 = ((bf16[96,2,200]{2,1,0:T(2,128)(2,1)}), bf16[96,2,200]{2,1,0:T(2,128)(2,1)S(1)}, u32[]{:S(2)}, u32[]{:S(2)}) async-start(bf16[96,2,200]{2,1,0:T(2,128)(2,1)} %reshape.407), calls=%async_computation.3 | async-start | bytes 196608 | tf_op jit(solution)/shard_map/all_to_all | solution.py:199
  107.8 11.7 %all-to-all-done.3 = bf16[96,2,200]{2,1,0:T(2,128)(2,1)S(1)} async-done(((bf16[96,2,200]{2,1,0:T(2,128)(2,1)}), bf16[96,2,200]{2,1,0:T(2,128)(2,1)S(1)}, u32[]{:S(2)}, u32[]{:S(2)}) %all-to-all-start.3) | async-done | bytes 76832 | tf_op jit(solution)/shard_map/all_to_all | solution.py:199
  120.4 1.3 fusion.64
  124.0 3.6 %all-to-all-start.4 = ((f32[8,1,6400]{2,1,0:T(1,128)}), f32[8,1,6400]{2,1,0:T(1,128)S(1)}, u32[]{:S(2)}, u32[]{:S(2)}) async-start(f32[8,1,6400]{2,1,0:T(1,128)} %reshape.409), calls=%async_computation.4 | async-start | bytes 409600 | tf_op jit(solution)/shard_map/all_to_all | solution.py:219
  127.6 1.7 %convolution_bitcast_fusion = f32[19,16,256]{2,0,1:T(8,128)S(1)} fusion(f32[19,16,48]{0,2,1:T(8,128)S(1)} %bitcast.118, f32[16,48]{1,0:T(8,128)S(1)} %mul.1325, f32[16,48]{1,0:T(8,128)S(1)} %sub.164, f32[256]{0:T(256)S(1)} %get-tuple-element.96, f32[16,48]{1,0:T(8,128)S(1)} %mul.1321, f32[16,48]{1,0:T(8,128)S(1)} %sub.158, f32[256]{0:T(256)S(1)} %get-tuple-element.97, ...), kind=kOutput, calls=%fused_computation.12 | convolution fusion | flops 47775744 | bytes 1176576 | tf_op jit(solution)/shard_map/jvp(vmap())/dot_general | solution.py:97
  130.5 7.3 %all-to-all-done.4 = f32[8,1,6400]{2,1,0:T(1,128)S(1)} async-done(((f32[8,1,6400]{2,1,0:T(1,128)}), f32[8,1,6400]{2,1,0:T(1,128)S(1)}, u32[]{:S(2)}, u32[]{:S(2)}) %all-to-all-start.4) | async-done | bytes 204832 | tf_op jit(solution)/shard_map/all_to_all | solution.py:219
  137.8 1.1 reduce.5
  (128 shorter events, 23.8 us)
Async XLA Ops:
  0.6 0.8 copy-start.5
  1.5 0.7 copy-start.7
  2.2 0.7 copy-start.8
  2.8 0.7 copy-start.2
  5.2 7.3 %copy-start.4 = (s32[1,16,2,3]{1,2,3,0:T(2,128)S(1)}, s32[1,16,2,3]{1,2,3,0:T(2,128)}, u32[]{:S(2)}) copy-start(s32[1,16,2,3]{1,2,3,0:T(2,128)} %param.16) | copy-start | bytes 1156
  5.2 7.6 %copy-start.3 = (f32[1,4]{1,0:T(1,128)S(1)}, f32[1,4]{1,0:T(1,128)}, u32[]{:S(2)}) copy-start(f32[1,4]{1,0:T(1,128)} %param.14) | copy-start | bytes 52
  5.2 17.9 %all-to-all-start = ((f32[8,1,6400]{2,1,0:T(1,128)}), f32[8,1,6400]{2,1,0:T(1,128)S(1)}, u32[]{:S(2)}, u32[]{:S(2)}) async-start(f32[8,1,6400]{2,1,0:T(1,128)} %reshape.403), calls=%async_computation | async-start | bytes 409600 | tf_op jit(solution)/shard_map/all_to_all | solution.py:146
  12.4 3.5 %copy-start.1 = (bf16[19,1,4096]{2,0,1:T(8,128)(2,1)S(1)}, bf16[19,1,4096]{2,0,1:T(8,128)(2,1)}, u32[]{:S(2)}) copy-start(bf16[19,1,4096]{2,0,1:T(8,128)(2,1)} %param.17) | copy-start | bytes 466948
  16.6 0.9 copy-start.6
  26.1 32.7 %all-to-all-start.1 = ((s32[96,2,1]{1,2,0:T(1,128)}), s32[96,2,1]{1,2,0:T(1,128)S(1)}, u32[]{:S(2)}, u32[]{:S(2)}) async-start(s32[96,2,1]{1,2,0:T(1,128)} %bitcast.14), calls=%async_computation.1 | async-start | bytes 98304 | tf_op jit(solution)/shard_map/all_to_all | solution.py:160
  61.9 25.2 %all-to-all-start.2 = ((bf16[96,2,200]{2,1,0:T(2,128)(2,1)}), bf16[96,2,200]{2,1,0:T(2,128)(2,1)S(1)}, u32[]{:S(2)}, u32[]{:S(2)}) async-start(bf16[96,2,200]{2,1,0:T(2,128)(2,1)} %reshape.405), calls=%async_computation.2 | async-start | bytes 196608 | tf_op jit(solution)/shard_map/all_to_all | solution.py:174
  99.6 19.9 %all-to-all-start.3 = ((bf16[96,2,200]{2,1,0:T(2,128)(2,1)}), bf16[96,2,200]{2,1,0:T(2,128)(2,1)S(1)}, u32[]{:S(2)}, u32[]{:S(2)}) async-start(bf16[96,2,200]{2,1,0:T(2,128)(2,1)} %reshape.407), calls=%async_computation.3 | async-start | bytes 196608 | tf_op jit(solution)/shard_map/all_to_all | solution.py:199
  120.4 1.3 copy-start
  121.7 0.9 slice-start
  124.0 13.8 %all-to-all-start.4 = ((f32[8,1,6400]{2,1,0:T(1,128)}), f32[8,1,6400]{2,1,0:T(1,128)S(1)}, u32[]{:S(2)}, u32[]{:S(2)}) async-start(f32[8,1,6400]{2,1,0:T(1,128)} %reshape.409), calls=%async_computation.4 | async-start | bytes 409600 | tf_op jit(solution)/shard_map/all_to_all | solution.py:219

commit v12 on v9

--- a/solution.py
+++ b/solution.py
@@ -143,14 +143,40 @@
     grad_log = jnp.sum(grad_sum, axis=1, keepdims=True) - jnp.cumsum(grad_sum, axis=1)
     grad_cover = grad_weight * keep - grad_log / (1.0 - coverage)
     grad_quad = -0.5 * grad_cover * coverage
+    basis = jnp.stack(
+        [
+            jnp.ones_like(across),
+            across,
+            downward,
+            across * across,
+            across * downward,
+            downward * downward,
+        ],
+        axis=1,
+    )
+    moments = jnp.einsum(
+        "tip,pk->tik",
+        jnp.concatenate([grad_quad, grad_cover * falloff], axis=1),
+        basis,
+        precision=hi,
+    )
+    count = grad_quad.shape[1]
+    m_1, m_x, m_y, m_xx, m_xy, m_yy = [moments[:, :count, k] for k in range(6)]
+    centre_x = proj[0]
+    centre_y = proj[1]
+    s_x = m_x - centre_x * m_1
+    s_y = m_y - centre_y * m_1
+    s_xx = m_xx - 2.0 * centre_x * m_x + centre_x * centre_x * m_1
+    s_xy = m_xy - centre_x * m_y - centre_y * m_x + centre_x * centre_y * m_1
+    s_yy = m_yy - 2.0 * centre_y * m_y + centre_y * centre_y * m_1
     grad_proj = jnp.stack(
         [
-            -jnp.sum(grad_quad * (2.0 * conic_0 * delta_x + 2.0 * conic_1 * delta_y), axis=2),
-            -jnp.sum(grad_quad * (2.0 * conic_1 * delta_x + 2.0 * conic_2 * delta_y), axis=2),
-            jnp.sum(grad_quad * delta_x * delta_x, axis=2),
-            jnp.sum(2.0 * grad_quad * delta_x * delta_y, axis=2),
-            jnp.sum(grad_quad * delta_y * delta_y, axis=2),
-            jnp.sum(grad_cover * falloff, axis=2),
+            -2.0 * (proj[2] * s_x + proj[3] * s_y),
+            -2.0 * (proj[3] * s_x + proj[4] * s_y),
+            s_xx,
+            2.0 * s_xy,
+            s_yy,
+            moments[:, count:, 0],
         ]
     )
     return (picture, grad_proj.reshape(6, -1), grad_colour.reshape(channels, -1))

time: 135 us -> 137 us (1.015)
  matrix products: 5.92 us -> 7.52 us
    concatenate x5, local copies, waits for them, and re-layouts: 1.56 us -> 3.6 us  [local(): params = jnp.concatenate([geometry, appearance], axis=0)]
    dot_general x0 -> x1, matrix products: none -> 1.6 us  [tile_grads_direct(): jnp.einsum('tip,pk->tik', jnp.concatenate([grad_quad, grad_cover * fallof...]
    unnamed x42 -> x27, local copies, waits for them, and re-layouts: 7.85 us -> 6.44 us
    unnamed x6 -> x11, other arithmetic: 3.8 us -> 3.88 us
where the time goes in v12:
time: 137 us; the launch traced here: 135 us
  starting transfers between devices  38 us (28%)
  waiting for transfers between devices  32.1 us (23%)
  local copies, waits for them, and re-layouts  21.7 us (16%)
  blocking collectives  19.2 us (14%)
  other arithmetic  14 us (10%)
  matrix products  7.52 us (5%)
  between operations  2.61 us (2%)
    all_to_all x1, starting transfers between devices, local(): lax.all_to_all(request, 'tiles', split_axis=0, concat_axis=0, tiled=True)  19.4 us
    all_to_all x1, blocking collectives, local(): lax.all_to_all(back, 'tiles', split_axis=2, concat_axis=2, tiled=True)  19.2 us
    all_to_all x1, waiting for transfers between devices, local(): lax.all_to_all(send, 'tiles', split_axis=2, concat_axis=2, tiled=True)  11.8 us
    all_to_all x1, starting transfers between devices, local(): lax.all_to_all(send, 'tiles', split_axis=2, concat_axis=2, tiled=True)  7.88 us
    all_to_all x1, waiting for transfers between devices, local(): lax.all_to_all(column_all.reshape(rows, BLK, cams, local_blocks), 'cams',...  7.27 us
    all_to_all x1, starting transfers between devices, local(): lax.all_to_all(jnp.broadcast_to(by_lane[None], (cams,) + by_lane.shape),...  7.1 us
    all_to_all x1, waiting for transfers between devices, local(): lax.all_to_all(request, 'tiles', split_axis=0, concat_axis=0, tiled=True)  6.59 us
    unnamed x27, local copies, waits for them, and re-layouts  6.44 us
  transfers between devices with their start and end apart: 4, of which 4 were waited for; matrix products, arithmetic and copies ran while one was open for 7% of the time, Pallas kernels for 0%

profile of v12, /device:TPU:6, one launch (start us, length us, event | category | flops | bytes accessed | tf_op | source)
XLA Modules:
  0.0 135.0 jit_solution(8590236662373826696)
XLA Ops:
  5.4 1.0 reshape.583
  6.4 7.1 %all-to-all-start = ((f32[8,1,6400]{2,1,0:T(1,128)}), f32[8,1,6400]{2,1,0:T(1,128)S(1)}, u32[]{:S(2)}, u32[]{:S(2)}) async-start(f32[8,1,6400]{2,1,0:T(1,128)} %reshape.583), calls=%async_computation | async-start | bytes 409600 | tf_op jit(solution)/shard_map/all_to_all | solution.py:215
  17.8 6.4 %all-to-all-done = f32[8,1,6400]{2,1,0:T(1,128)S(1)} async-done(((f32[8,1,6400]{2,1,0:T(1,128)}), f32[8,1,6400]{2,1,0:T(1,128)S(1)}, u32[]{:S(2)}, u32[]{:S(2)}) %all-to-all-start) | async-done | bytes 204832 | tf_op jit(solution)/shard_map/all_to_all | solution.py:215
  24.7 1.1 reduce.30
  27.2 19.4 %all-to-all-start.1 = ((s32[96,2,1]{1,2,0:T(1,128)}), s32[96,2,1]{1,2,0:T(1,128)S(1)}, u32[]{:S(2)}, u32[]{:S(2)}) async-start(s32[96,2,1]{1,2,0:T(1,128)} %bitcast.14), calls=%async_computation.1 | async-start | bytes 98304 | tf_op jit(solution)/shard_map/all_to_all | solution.py:229
  46.6 1.2 constant_dynamic-update-slice_fusion.5
  47.8 1.3 constant_dynamic-update-slice_fusion.4
  49.1 1.3 constant_dynamic-update-slice_fusion.3
  50.5 6.6 %all-to-all-done.1 = s32[96,2,1]{1,2,0:T(1,128)S(1)} async-done(((s32[96,2,1]{1,2,0:T(1,128)}), s32[96,2,1]{1,2,0:T(1,128)S(1)}, u32[]{:S(2)}, u32[]{:S(2)}) %all-to-all-start.1) | async-done | bytes 800 | tf_op jit(solution)/shard_map/all_to_all | solution.py:229
  59.1 1.0 reshape.585
  60.2 7.9 %all-to-all-start.2 = ((bf16[96,2,200]{2,1,0:T(2,128)(2,1)}), bf16[96,2,200]{2,1,0:T(2,128)(2,1)S(1)}, u32[]{:S(2)}, u32[]{:S(2)}) async-start(bf16[96,2,200]{2,1,0:T(2,128)(2,1)} %reshape.585), calls=%async_computation.2 | async-start | bytes 196608 | tf_op jit(solution)/shard_map/all_to_all | solution.py:243
  68.2 11.8 %all-to-all-done.2 = bf16[96,2,200]{2,1,0:T(2,128)(2,1)S(1)} async-done(((bf16[96,2,200]{2,1,0:T(2,128)(2,1)}), bf16[96,2,200]{2,1,0:T(2,128)(2,1)S(1)}, u32[]{:S(2)}, u32[]{:S(2)}) %all-to-all-start.2) | async-done | bytes 76832 | tf_op jit(solution)/shard_map/all_to_all | solution.py:243
  83.2 1.8 %fusion.8 = bf16[19,16,48]{2,0,1:T(8,128)(2,1)S(1)} fusion(bf16[19,16,256]{2,1,0:T(8,128)(2,1)S(1)} %slice.234, f32[16,48]{1,0:T(8,128)S(1)} %mul.837, f32[16,48]{1,0:T(8,128)S(1)} %sub.202, f32[256]{0:T(256)S(1)} %get-tuple-element.61, f32[16,48]{1,0:T(8,128)S(1)} %mul.833, f32[16,48]{1,0:T(8,128)S(1)} %sub.196, f32[256]{0:T(256)S(1)} %get-tuple-element.62, ...), kind=kOutput, calls=%fused_computation.19 | convolution fusion | flops 47790336 | bytes 991744 | tf_op jit(solution)/shard_map/ctp,tip->cti/dot_general | solution.py:140
  85.0 1.3 fusion.58
  86.9 1.7 %multiply_multiply_fusion = (f32[16,48,256]{2,1,0:T(8,128)S(1)}, f32[16,48,256]{2,1,0:T(8,128)S(1)}) fusion(f32[16,48]{1,0:T(8,128)S(1)} %mul.837, f32[16,48]{1,0:T(8,128)S(1)} %sub.202, f32[256]{0:T(256)S(1)} %get-tuple-element.61, f32[16,48]{1,0:T(8,128)S(1)} %mul.833, f32[16,48]{1,0:T(8,128)S(1)} %sub.196, f32[256]{0:T(256)S(1)} %get-tuple-element.62, ...), kind=kOutput, calls=%fused_computation.30 | output fusion | flops 4329519 | bytes 4739072 | tf_op jit(solution)/shard_map/sub | solution.py:143
  88.6 1.6 %fusion.1 = f32[16,96,6]{1,2,0:T(8,128)S(1)} fusion(f32[16,48,256]{2,1,0:T(8,128)S(1)} %get-tuple-element.38, f32[16,48,256]{2,1,0:T(8,128)S(1)} %get-tuple-element.37, f32[256,6]{0,1:T(8,128)S(1)} %stack.4), kind=kOutput, calls=%fused_computation.2 | convolution fusion | flops 28704768 | bytes 1615872 | tf_op jit(solution)/shard_map/tip,pk->tik/dot_general | solution.py:157
  93.0 19.2 %all_to_all.29 = bf16[96,2,200]{2,1,0:T(2,128)(2,1)S(1)} all-to-all(bf16[96,2,200]{2,1,0:T(2,128)(2,1)S(1)} %reshape.587), channel_id=1, replica_groups=mesh['tiles'=96,'cams'=8] {'tiles'}, dimensions={0} | all-to-all | bytes 153600 | tf_op jit(solution)/shard_map/all_to_all | solution.py:261
  113.7 1.3 multiply_add_fusion
  115.0 1.3 slice_multiply_fusion.1
  117.1 1.0 reshape.589
  118.1 3.6 %all-to-all-start.4 = ((f32[8,1,6400]{2,1,0:T(1,128)}), f32[8,1,6400]{2,1,0:T(1,128)S(1)}, u32[]{:S(2)}, u32[]{:S(2)}) async-start(f32[8,1,6400]{2,1,0:T(1,128)} %reshape.589), calls=%async_computation.4 | async-start | bytes 409600 | tf_op jit(solution)/shard_map/all_to_all | solution.py:266
  121.7 1.8 %convolution_bitcast_fusion = f32[19,16,256]{2,0,1:T(8,128)S(1)} fusion(f32[19,16,48]{0,2,1:T(8,128)S(1)} %bitcast.84, f32[16,48]{1,0:T(8,128)S(1)} %mul.837, f32[16,48]{1,0:T(8,128)S(1)} %sub.202, f32[256]{0:T(256)S(1)} %get-tuple-element.61, f32[16,48]{1,0:T(8,128)S(1)} %mul.833, f32[16,48]{1,0:T(8,128)S(1)} %sub.196, f32[256]{0:T(256)S(1)} %get-tuple-element.62, ...), kind=kOutput, calls=%fused_computation.15 | convolution fusion | flops 47775744 | bytes 1176576 | tf_op jit(solution)/shard_map/cti,tip->ctp/dot_general | solution.py:139
  124.6 7.3 %all-to-all-done.4 = f32[8,1,6400]{2,1,0:T(1,128)S(1)} async-done(((f32[8,1,6400]{2,1,0:T(1,128)}), f32[8,1,6400]{2,1,0:T(1,128)S(1)}, u32[]{:S(2)}, u32[]{:S(2)}) %all-to-all-start.4) | async-done | bytes 204832 | tf_op jit(solution)/shard_map/all_to_all | solution.py:266
  131.9 1.1 reduce.31
  (128 shorter events, 23.3 us)
Async XLA Ops:
  5.3 8.2 %copy-start.2 = (s32[1,16,2,3]{1,2,3,0:T(2,128)S(1)}, s32[1,16,2,3]{1,2,3,0:T(2,128)}, u32[]{:S(2)}) copy-start(s32[1,16,2,3]{1,2,3,0:T(2,128)} %param.16) | copy-start | bytes 1156
  5.3 8.5 %copy-start.1 = (f32[1,4]{1,0:T(1,128)S(1)}, f32[1,4]{1,0:T(1,128)}, u32[]{:S(2)}) copy-start(f32[1,4]{1,0:T(1,128)} %param.14) | copy-start | bytes 52
  5.3 11.8 %copy-start.3 = (f32[1,2]{1,0:T(1,128)S(1)}, f32[1,2]{1,0:T(1,128)}, u32[]{:S(2)}) copy-start(f32[1,2]{1,0:T(1,128)} %param.15) | copy-start | bytes 28
  6.4 17.7 %all-to-all-start = ((f32[8,1,6400]{2,1,0:T(1,128)}), f32[8,1,6400]{2,1,0:T(1,128)S(1)}, u32[]{:S(2)}, u32[]{:S(2)}) async-start(f32[8,1,6400]{2,1,0:T(1,128)} %reshape.583), calls=%async_computation | async-start | bytes 409600 | tf_op jit(solution)/shard_map/all_to_all | solution.py:215
  27.2 29.8 %all-to-all-start.1 = ((s32[96,2,1]{1,2,0:T(1,128)}), s32[96,2,1]{1,2,0:T(1,128)S(1)}, u32[]{:S(2)}, u32[]{:S(2)}) async-start(s32[96,2,1]{1,2,0:T(1,128)} %bitcast.14), calls=%async_computation.1 | async-start | bytes 98304 | tf_op jit(solution)/shard_map/all_to_all | solution.py:229
  57.6 10.5 %copy-start = (bf16[19,1,4096]{2,0,1:T(8,128)(2,1)S(1)}, bf16[19,1,4096]{2,0,1:T(8,128)(2,1)}, u32[]{:S(2)}) copy-start(bf16[19,1,4096]{2,0,1:T(8,128)(2,1)} %param.17) | copy-start | bytes 466948
  60.2 19.9 %all-to-all-start.2 = ((bf16[96,2,200]{2,1,0:T(2,128)(2,1)}), bf16[96,2,200]{2,1,0:T(2,128)(2,1)S(1)}, u32[]{:S(2)}, u32[]{:S(2)}) async-start(bf16[96,2,200]{2,1,0:T(2,128)(2,1)} %reshape.585), calls=%async_computation.2 | async-start | bytes 196608 | tf_op jit(solution)/shard_map/all_to_all | solution.py:243
  118.1 13.8 %all-to-all-start.4 = ((f32[8,1,6400]{2,1,0:T(1,128)}), f32[8,1,6400]{2,1,0:T(1,128)S(1)}, u32[]{:S(2)}, u32[]{:S(2)}) async-start(f32[8,1,6400]{2,1,0:T(1,128)} %reshape.589), calls=%async_computation.4 | async-start | bytes 409600 | tf_op jit(solution)/shard_map/all_to_all | solution.py:266

commit v13 on v8

--- a/solution.py
+++ b/solution.py
@@ -143,9 +143,10 @@
     local_blocks = params.shape[1] // BLK
     per_column = cams * local_blocks
     by_lane = params.reshape(params.shape[0], local_blocks, BLK).transpose(0, 2, 1)
+    flat = by_lane.reshape(1, -1)
     gathered = lax.all_to_all(
-        jnp.broadcast_to(by_lane[None], (cams,) + by_lane.shape), "cams", 0, 0, tiled=True
-    )
+        jnp.broadcast_to(flat, (cams, flat.shape[1])), "cams", 0, 0, tiled=True
+    ).reshape((cams,) + by_lane.shape)
     params_col = gathered.transpose(1, 2, 0, 3).reshape(params.shape[0], BLK, per_column)
     linear = cam_linear[0]
     camera_shift = cam_shift[0]

time: 135 us -> 138 us (1.022)
  waiting for transfers between devices: 31.7 us -> 35.5 us
    all_to_all x1, waiting for transfers between devices: 6.59 us -> 10.4 us  [local(): lax.all_to_all(request, 'tiles', split_axis=0, concat_axis=0, tiled=True)]
    unnamed x36 -> x34, local copies, waits for them, and re-layouts: 7.81 us -> 6.5 us
  transfers between devices with their start and end apart: 4 -> 4, of which waited for: 4 -> 4; matrix products, arithmetic and copies ran while one was open for 7% -> 4% of each run, Pallas kernels for 0% -> 0%
where the time goes in v13:
time: 138 us; the launch traced here: 136 us
  starting transfers between devices  38.2 us (28%)
  waiting for transfers between devices  35.5 us (26%)
  local copies, waits for them, and re-layouts  19.7 us (14%)
  blocking collectives  19.2 us (14%)
  other arithmetic  14.9 us (11%)
  matrix products  5.87 us (4%)
  between operations  2.55 us (2%)
    all_to_all x1, starting transfers between devices, local(): lax.all_to_all(request, 'tiles', split_axis=0, concat_axis=0, tiled=True)  19.4 us
    all_to_all x1, blocking collectives, local(): lax.all_to_all(back, 'tiles', split_axis=2, concat_axis=2, tiled=True)  19.2 us
    all_to_all x1, waiting for transfers between devices, local(): lax.all_to_all(send, 'tiles', split_axis=2, concat_axis=2, tiled=True)  11.9 us
    all_to_all x1, waiting for transfers between devices, local(): lax.all_to_all(request, 'tiles', split_axis=0, concat_axis=0, tiled=True)  10.4 us
    all_to_all x1, starting transfers between devices, local(): lax.all_to_all(send, 'tiles', split_axis=2, concat_axis=2, tiled=True)  8.01 us
    all_to_all x1, waiting for transfers between devices, local(): lax.all_to_all(column_all.reshape(rows, BLK, cams, local_blocks), 'cams',...  7.31 us
    all_to_all x1, starting transfers between devices, local(): lax.all_to_all(jnp.broadcast_to(flat, (cams, flat.shape[1])), 'cams', 0,...  7.23 us
    unnamed x34, local copies, waits for them, and re-layouts  6.5 us
  transfers between devices with their start and end apart: 4, of which 4 were waited for; matrix products, arithmetic and copies ran while one was open for 4% of the time, Pallas kernels for 0%

profile of v13, /device:TPU:6, one launch (start us, length us, event | category | flops | bytes accessed | tf_op | source)
XLA Modules:
  0.0 136.0 jit_solution(809259341521532474)
XLA Ops:
  4.9 7.2 %all-to-all-start = ((f32[8,1,6400]{2,1,0:T(1,128)}), f32[8,1,6400]{2,1,0:T(1,128)S(1)}, u32[]{:S(2)}, u32[]{:S(2)}) async-start(f32[8,1,6400]{2,1,0:T(1,128)} %broadcast_in_dim.14), calls=%async_computation | async-start | bytes 409600 | tf_op jit(solution)/shard_map/all_to_all | solution.py:147
  15.4 0.9 scatter_custom_fusion
  16.9 5.9 %all-to-all-done = f32[8,1,6400]{2,1,0:T(1,128)S(1)} async-done(((f32[8,1,6400]{2,1,0:T(1,128)}), f32[8,1,6400]{2,1,0:T(1,128)S(1)}, u32[]{:S(2)}, u32[]{:S(2)}) %all-to-all-start) | async-done | bytes 204832 | tf_op jit(solution)/shard_map/all_to_all | solution.py:147
  24.0 1.2 constant_dynamic-update-slice_fusion.5
  25.2 1.3 constant_dynamic-update-slice_fusion.4
  26.5 1.3 constant_dynamic-update-slice_fusion.3
  28.6 19.4 %all-to-all-start.1 = ((s32[96,2,1]{1,2,0:T(1,128)}), s32[96,2,1]{1,2,0:T(1,128)S(1)}, u32[]{:S(2)}, u32[]{:S(2)}) async-start(s32[96,2,1]{1,2,0:T(1,128)} %bitcast.14), calls=%async_computation.1 | async-start | bytes 98304 | tf_op jit(solution)/shard_map/all_to_all | solution.py:161
  48.0 10.4 %all-to-all-done.1 = s32[96,2,1]{1,2,0:T(1,128)S(1)} async-done(((s32[96,2,1]{1,2,0:T(1,128)}), s32[96,2,1]{1,2,0:T(1,128)S(1)}, u32[]{:S(2)}, u32[]{:S(2)}) %all-to-all-start.1) | async-done | bytes 800 | tf_op jit(solution)/shard_map/all_to_all | solution.py:161
  60.5 1.0 reshape.354
  61.5 8.0 %all-to-all-start.2 = ((bf16[96,2,200]{2,1,0:T(2,128)(2,1)}), bf16[96,2,200]{2,1,0:T(2,128)(2,1)S(1)}, u32[]{:S(2)}, u32[]{:S(2)}) async-start(bf16[96,2,200]{2,1,0:T(2,128)(2,1)} %reshape.354), calls=%async_computation.2 | async-start | bytes 196608 | tf_op jit(solution)/shard_map/all_to_all | solution.py:175
  69.6 11.9 %all-to-all-done.2 = bf16[96,2,200]{2,1,0:T(2,128)(2,1)S(1)} async-done(((bf16[96,2,200]{2,1,0:T(2,128)(2,1)}), bf16[96,2,200]{2,1,0:T(2,128)(2,1)S(1)}, u32[]{:S(2)}, u32[]{:S(2)}) %all-to-all-start.2) | async-done | bytes 76832 | tf_op jit(solution)/shard_map/all_to_all | solution.py:175
  84.7 1.8 %fusion = bf16[19,16,48]{2,0,1:T(8,128)(2,1)S(1)} fusion(f32[16,48]{1,0:T(8,128)S(1)} %mul.694, f32[16,48]{1,0:T(8,128)S(1)} %sub.109, f32[256]{0:T(256)S(1)} %get-tuple-element.59, f32[16,48]{1,0:T(8,128)S(1)} %mul.690, f32[16,48]{1,0:T(8,128)S(1)} %sub.103, f32[256]{0:T(256)S(1)} %get-tuple-element.60, f32[16,48]{1,0:T(8,128)S(1)} %mul.685, ...), kind=kOutput, calls=%fused_computation.16 | convolution fusion | flops 47790336 | bytes 991744 | tf_op jit(solution)/shard_map/transpose(jvp(vmap()))/dot_general | solution.py:97
  86.9 1.3 multiply_multiply_fusion.1
  88.2 0.9 fusion.20
  89.2 2.9 %fusion.14 = (f32[16,48]{1,0:T(8,128)S(1)}, f32[16,48]{1,0:T(8,128)S(1)}, f32[16,48]{1,0:T(8,128)S(1)}, f32[16,48]{1,0:T(8,128)S(1)}, f32[16,48]{1,0:T(8,128)S(1)}, /*index=5*/f32[16,48]{1,0:T(8,128)S(1)}) fusion(f32[16,48]{1,0:T(8,128)S(1)} %sub.109, f32[256]{0:T(256)S(1)} %get-tuple-element.59, f32[16,48]{1,0:T(8,128)S(1)} %mul.694, ...), kind=kLoop, calls=%fused_computation.30 | loop fusion | flops 9432576 | bytes 2398208 | tf_op jit(solution)/shard_map/transpose(jvp(vmap()))/reduce_sum | solution.py:92
  93.3 19.2 %all_to_all.30 = bf16[96,2,200]{2,1,0:T(2,128)(2,1)S(1)} all-to-all(bf16[96,2,200]{2,1,0:T(2,128)(2,1)S(1)} %reshape.356), channel_id=1, replica_groups=mesh['tiles'=96,'cams'=8] {'tiles'}, dimensions={0} | all-to-all | bytes 153600 | tf_op jit(solution)/shard_map/all_to_all | solution.py:193
  114.1 1.3 multiply_add_fusion
  115.6 1.3 slice_multiply_fusion.1
  117.5 1.0 reshape.358
  118.6 3.6 %all-to-all-start.4 = ((f32[8,1,6400]{2,1,0:T(1,128)}), f32[8,1,6400]{2,1,0:T(1,128)S(1)}, u32[]{:S(2)}, u32[]{:S(2)}) async-start(f32[8,1,6400]{2,1,0:T(1,128)} %reshape.358), calls=%async_computation.4 | async-start | bytes 409600 | tf_op jit(solution)/shard_map/all_to_all | solution.py:198
  122.2 1.7 %convolution_bitcast_fusion = f32[19,16,256]{2,0,1:T(8,128)S(1)} fusion(f32[19,16,48]{0,2,1:T(8,128)S(1)} %bitcast.89, f32[16,48]{1,0:T(8,128)S(1)} %mul.694, f32[16,48]{1,0:T(8,128)S(1)} %sub.109, f32[256]{0:T(256)S(1)} %get-tuple-element.59, f32[16,48]{1,0:T(8,128)S(1)} %mul.690, f32[16,48]{1,0:T(8,128)S(1)} %sub.103, f32[256]{0:T(256)S(1)} %get-tuple-element.60, ...), kind=kOutput, calls=%fused_computation.12 | convolution fusion | flops 47775744 | bytes 1176576 | tf_op jit(solution)/shard_map/jvp(vmap())/dot_general | solution.py:97
  124.0 1.0 reshape.341
  125.1 7.3 %all-to-all-done.4 = f32[8,1,6400]{2,1,0:T(1,128)S(1)} async-done(((f32[8,1,6400]{2,1,0:T(1,128)}), f32[8,1,6400]{2,1,0:T(1,128)S(1)}, u32[]{:S(2)}, u32[]{:S(2)}) %all-to-all-start.4) | async-done | bytes 204832 | tf_op jit(solution)/shard_map/all_to_all | solution.py:198
  132.9 1.1 reduce.5
  (116 shorter events, 20.3 us)
Async XLA Ops:
  0.6 0.8 copy-start.5
  1.5 0.7 copy-start.7
  2.2 0.7 copy-start.8
  2.8 0.7 copy-start.2
  4.9 7.2 %copy-start.4 = (s32[1,16,2,3]{1,2,3,0:T(2,128)S(1)}, s32[1,16,2,3]{1,2,3,0:T(2,128)}, u32[]{:S(2)}) copy-start(s32[1,16,2,3]{1,2,3,0:T(2,128)} %param.16) | copy-start | bytes 1156
  4.9 17.9 %all-to-all-start = ((f32[8,1,6400]{2,1,0:T(1,128)}), f32[8,1,6400]{2,1,0:T(1,128)S(1)}, u32[]{:S(2)}, u32[]{:S(2)}) async-start(f32[8,1,6400]{2,1,0:T(1,128)} %broadcast_in_dim.14), calls=%async_computation | async-start | bytes 409600 | tf_op jit(solution)/shard_map/all_to_all | solution.py:147
  12.6 0.7 copy-start.3
  15.4 0.9 copy-start.6
  28.6 29.8 %all-to-all-start.1 = ((s32[96,2,1]{1,2,0:T(1,128)}), s32[96,2,1]{1,2,0:T(1,128)S(1)}, u32[]{:S(2)}, u32[]{:S(2)}) async-start(s32[96,2,1]{1,2,0:T(1,128)} %bitcast.14), calls=%async_computation.1 | async-start | bytes 98304 | tf_op jit(solution)/shard_map/all_to_all | solution.py:161
  61.5 8.0 %copy-start.1 = (bf16[19,1,4096]{2,0,1:T(8,128)(2,1)S(1)}, bf16[19,1,4096]{2,0,1:T(8,128)(2,1)}, u32[]{:S(2)}) copy-start(bf16[19,1,4096]{2,0,1:T(8,128)(2,1)} %param.17) | copy-start | bytes 466948
  61.5 20.0 %all-to-all-start.2 = ((bf16[96,2,200]{2,1,0:T(2,128)(2,1)}), bf16[96,2,200]{2,1,0:T(2,128)(2,1)S(1)}, u32[]{:S(2)}, u32[]{:S(2)}) async-start(bf16[96,2,200]{2,1,0:T(2,128)(2,1)} %reshape.354), calls=%async_computation.2 | async-start | bytes 196608 | tf_op jit(solution)/shard_map/all_to_all | solution.py:175
  113.5 0.7 copy-start
  115.5 1.6 %slice-start = ((f32[25,8,256]{2,1,0:T(8,128)}), f32[19,8,256]{2,1,0:T(8,128)S(1)}, s32[]{:S(2)}) async-start(f32[25,8,256]{2,1,0:T(8,128)} %copy-done), calls=%async_computation.5 | async-start | bytes 311296 | tf_op jit(solution)/shard_map/slice | solution.py:196
  118.6 13.8 %all-to-all-start.4 = ((f32[8,1,6400]{2,1,0:T(1,128)}), f32[8,1,6400]{2,1,0:T(1,128)S(1)}, u32[]{:S(2)}, u32[]{:S(2)}) async-start(f32[8,1,6400]{2,1,0:T(1,128)} %reshape.358), calls=%async_computation.4 | async-start | bytes 409600 | tf_op jit(solution)/shard_map/all_to_all | solution.py:198
